TPU v7x, 256 devices: a whole 4x4x8 slice. The times are simulated.
256 devices in a mesh: rows: 8 (over y, core), cols: 8 (over z), layers: 4 (over x).
Axes of the slice: x: 4, y: 4, z: 8, core: 2. Of those that a mesh axis runs over, the one named last changes fastest.
Arguments:
- y_blocks: bfloat16 [192, 32, 128, 128], P('rows', ('cols', 'layers')), may hold values from -1 to 1
- y_cols: int32 [192, 32], P('rows', ('cols', 'layers')), may hold values from 0 to 191, as said below
- prod_blocks: bfloat16 [192, 32, 128, 128], P('rows', ('cols', 'layers')), may hold values from -1 to 1
- prod_cols: int32 [192, 32], P('rows', ('cols', 'layers')), may hold values from 0 to 191, as said below
- out_cols: int32 [192, 32, 2], P('rows', ('cols', 'layers')), may hold values from 0 to 191, as said below
Outputs:
- y_next: bfloat16 [192, 32, 2, 128, 128], P('rows', ('cols', 'layers'))
Inputs may be any that keep to these rules, and one draw needn't show every extreme that they name: y_cols[i, t] lies in [t * 6, (t + 1) * 6): each block row of Y holds exactly one block in each range of 6 block columns. prod_cols[k, t] lies in [t * 6, (t + 1) * 6): each block row of M holds exactly one block in each range of 6 block columns. out_cols[i, t, :] are 2 distinct block columns in [t * 6, (t + 1) * 6), one of them equal to y_cols[i, t].
All inputs are finite; a program needn't handle non-finite values.
Results may differ from a plain program's by a relative error of at most 0.001.
Values may be sent and summed in bfloat16 or wider, within the bound.
No kernel may reach another device: no remote copies, remote signals or barrier semaphores. Data moves between devices by JAX's collectives and lax.ppermute only.
A program may use at most 128 MiB of HBM per device.

v0:
```python
import jax
import jax.numpy as jnp
from jax import lax
from jax.sharding import PartitionSpec as P

TILE_COLS = 6


def partial_products(
    running, shard_piece, lookup, lookup_cols, target_cols, layer_count, tile_cols
):
    left_all, left_cols = shard_piece
    block_rows, piece_len = left_cols.shape
    tile_count = target_cols.shape[1]
    outputs = block_rows * tile_count
    group_size = 1
    while group_size * 2 <= max(1, 64 // outputs) and piece_len % (group_size * 2) == 0:
        group_size = group_size * 2

    def advance(position, summed):
        offset = position * group_size
        left_blocks = lax.dynamic_slice_in_dim(left_all, offset, group_size, 1)
        inner_cols = lax.dynamic_slice_in_dim(left_cols, offset, group_size, 1)
        lookup_rows = inner_cols // (layer_count * tile_cols) * tile_cols + inner_cols % tile_cols
        right_blocks = lookup[lookup_rows]
        right_cols = lookup_cols[lookup_rows]
        present = (right_cols[:, :, :, None] == target_cols[:, None, :, :]).astype(jnp.float32)
        products = jnp.einsum(
            "igab,igtbc->igtac", left_blocks, right_blocks, preferred_element_type=jnp.float32
        )
        weighted = jnp.sum(products[:, :, :, None] * present[..., None, None], axis=1)
        return summed + weighted

    return lax.fori_loop(0, piece_len // group_size, advance, running)


def shards(y_blocks, y_cols, prod_blocks, prod_cols, out_cols):
    block_rows = y_blocks.shape[0]
    block_size = y_blocks.shape[2]
    out_width = out_cols.shape[2]
    tile_cols = TILE_COLS
    lookup, lookup_cols = (
        lax.all_gather(prod_blocks, "rows", axis=0, tiled=True),
        lax.all_gather(prod_cols, "rows", axis=0, tiled=True),
    )
    initial = jnp.zeros((block_rows, 1, out_width, block_size, block_size), jnp.float32)
    summed = partial_products(
        initial,
        (
            lax.all_gather(y_blocks, ("cols", "layers"), axis=1, tiled=True),
            lax.all_gather(y_cols, ("cols", "layers"), axis=1, tiled=True),
        ),
        lookup,
        lookup_cols,
        out_cols,
        1,
        tile_cols,
    )
    matches = out_cols == y_cols[:, :, None]
    own_blocks = jnp.where(matches[..., None, None], y_blocks[:, :, None].astype(jnp.float32), 0.0)
    updated = 1.5 * own_blocks - 0.5 * summed
    return updated.astype(jnp.bfloat16)


def solution(mesh):
    placed = (
        P("rows", ("cols", "layers"), None, None),
        P("rows", ("cols", "layers")),
        P("rows", ("cols", "layers"), None, None),
        P("rows", ("cols", "layers")),
        P("rows", ("cols", "layers"), None),
    )
    return jax.shard_map(
        shards,
        mesh=mesh,
        in_specs=placed,
        out_specs=P("rows", ("cols", "layers"), None, None, None),
        check_vma=False,
    )
```

profile of v0, /device:TPU:1, one launch (start us, length us, event | category | flops | bytes accessed | tf_op | source)
XLA Modules:
  0.0 567.5 jit_solution(7262077693090824826)
XLA Ops:
  10.6 36.9 %all-gather = s32[32,1,24]{2,1,0:T(1,128)S(1)} all-gather(s32[1,1,24]{2,1,0:T(1,128)} %bitcast.54), channel_id=1, replica_groups=mesh['rows'=8,'cols'=8,'layers'=4] {'cols','layers'}, dimensions={0}, use_global_device_ids=true | all-gather | bytes 3168 | tf_op jit(solution)/shard_map/all_gather | solution.py:51
  48.3 13.6 %all-reduce = s32[192]{0:T(256)S(1)} all-reduce(s32[192]{0:T(256)S(1)} %bitcast_dynamic-update-slice_fusion), channel_id=1, replica_groups=mesh['rows'=8,'cols'=8,'layers'=4] {'rows'}, use_global_device_ids=true, to_apply=%add | all-reduce | flops 192 | bytes 1536
  64.4 177.4 %all-gather.6.cloned.1.call-done = bf16[24,32,128,128]{3,2,1,0:T(8,128)(2,1)} async-done(((bf16[24,1,128,128]{3,2,1,0:T(8,128)(2,1)}), bf16[24,32,128,128]{3,2,1,0:T(8,128)(2,1)}) %all-gather.6.cloned.1.call-update) | async-done | bytes 25165840 | tf_op jit(solution)/shard_map/all_gather | solution.py:50
  241.8 314.7 %while.16 = (s32[]{:T(128)}, f32[24,1,2,128,128]{4,3,2,0,1:T(8,128)}, s32[24,32]{0,1:T(8,128)S(1)}, bf16[192,1,128,128]{3,2,1,0:T(8,128)(2,1)}, bf16[24,32,128,1...) while((s32[]{:T(128)}, ...), condition=%wide.region_2.3_spmd.clone, body=%wide.region_0.2_spmd.clone.sunk | while | flops 205260784 | bytes 31465964 | solution.py:34
  242.1 3.6 gather_fusion.1
  245.7 4.4 convolution_bitcast_fusion.2
  253.6 2.7 multiply_reduce_fusion.2
  256.3 4.3 bitcast_add_fusion.2
  260.8 3.6 gather_fusion.1
  264.5 4.4 convolution_bitcast_fusion.2
  275.0 5.3 bitcast_add_fusion.2
  280.6 3.6 gather_fusion.1
  284.2 4.4 convolution_bitcast_fusion.2
  294.8 5.3 bitcast_add_fusion.2
  300.3 3.6 gather_fusion.1
  303.9 4.4 convolution_bitcast_fusion.2
  311.8 2.7 multiply_reduce_fusion.2
  314.5 5.3 bitcast_add_fusion.2
  320.0 3.6 gather_fusion.1
  323.7 4.4 convolution_bitcast_fusion.2
  331.5 2.7 multiply_reduce_fusion.2
  334.2 5.3 bitcast_add_fusion.2
  339.7 3.6 gather_fusion.1
  343.4 4.4 convolution_bitcast_fusion.2
  351.3 2.7 multiply_reduce_fusion.2
  353.9 5.3 bitcast_add_fusion.2
  359.5 3.6 gather_fusion.1
  363.1 4.4 convolution_bitcast_fusion.2
  371.0 2.7 multiply_reduce_fusion.2
  373.7 5.3 bitcast_add_fusion.2
  379.2 3.6 gather_fusion.1
  382.8 4.4 convolution_bitcast_fusion.2
  393.4 5.3 bitcast_add_fusion.2
  398.9 3.6 gather_fusion.1
  402.6 4.4 convolution_bitcast_fusion.2
  410.4 2.7 multiply_reduce_fusion.2
  413.1 5.3 bitcast_add_fusion.2
  418.6 3.6 gather_fusion.1
  422.3 4.4 convolution_bitcast_fusion.2
  430.2 2.7 multiply_reduce_fusion.2
  432.9 5.3 bitcast_add_fusion.2
  438.4 3.6 gather_fusion.1
  442.0 4.4 convolution_bitcast_fusion.2
  449.9 2.7 multiply_reduce_fusion.2
  452.6 5.3 bitcast_add_fusion.2
  458.1 3.6 gather_fusion.1
  461.7 4.4 convolution_bitcast_fusion.2
  472.3 5.3 bitcast_add_fusion.2
  477.8 3.6 gather_fusion.1
  481.5 4.4 convolution_bitcast_fusion.2
  489.3 2.7 multiply_reduce_fusion.2
  492.0 5.3 bitcast_add_fusion.2
  497.6 3.6 gather_fusion.1
  501.2 4.4 convolution_bitcast_fusion.2
  509.1 2.7 multiply_reduce_fusion.2
  511.8 5.3 bitcast_add_fusion.2
  517.3 3.6 gather_fusion.1
  520.9 4.4 convolution_bitcast_fusion.2
  528.8 2.7 multiply_reduce_fusion.2
  531.5 5.3 bitcast_add_fusion.2
  537.0 3.6 gather_fusion.1
  540.6 4.4 convolution_bitcast_fusion.2
  551.2 5.3 bitcast_add_fusion.2
  556.5 4.1 fusion.6
  (179 shorter events, 78.6 us)
Async XLA Ops:
  6.5 235.3 %copy-start = (s32[24,1,2]{0,2,1:T(2,128)S(1)}, s32[24,1,2]{0,2,1:T(2,128)}, u32[]{:S(2)}) copy-start(s32[24,1,2]{0,2,1:T(2,128)} %param.11) | copy-start | bytes 580
  6.5 57.9 %all-gather.4.cloned.1.call-start = ((), (), s32[]{:S(2)}) async-start(), calls=%async_computation | async-start | bytes 7077888 | tf_op jit(solution)/shard_map/all_gather | solution.py:43
  7.3 234.6 %all-gather.6.cloned.1.call-start = ((), (), s32[]{:S(2)}) async-start(), calls=%async_computation.1 | async-start | bytes 25952256 | tf_op jit(solution)/shard_map/all_gather | solution.py:50
Sparse Core Ops, SparseCore 0:
  9.2 47.6 all-gather.3
  59.4 182.3 all-gather.5
where the time goes:
time: 569 us; the launch traced here: 567 us
  waiting for transfers between devices  179 us (31%)
  other arithmetic  136 us (24%)
  local copies, waits for them, and re-layouts  117 us (21%)
  matrix products  70.6 us (12%)
  blocking collectives  50.6 us (9%)
  between operations  14 us (2%)
    all_gather x1, waiting for transfers between devices, shards(): lax.all_gather(y_blocks, ('cols', 'layers'), axis=1, tiled=True)  177 us
    add x16, other arithmetic, advance(): return summed + weighted  83.7 us
    dot_general x16, matrix products, advance(): jnp.einsum('igab,igtbc->igtac', left_blocks, right_blocks, preferred_elem...  70.6 us
    gather x16, local copies, waits for them, and re-layouts, advance(): right_blocks = lookup[lookup_rows]  58.1 us
    reduce_sum x16, other arithmetic, advance(): jnp.sum(products[:, :, :, None] * present[..., None, None], axis=1)  43 us
    mul x16, local copies, waits for them, and re-layouts, advance(): products[:, :, :, None] * present[..., None, None]  38 us
    all_gather x1, blocking collectives, shards(): lax.all_gather(y_cols, ('cols', 'layers'), axis=1, tiled=True)  36.9 us
    unnamed x1, blocking collectives  13.6 us
  transfers between devices with their start and end apart: 2, of which 1 were waited for; matrix products, arithmetic and copies ran while one was open for 1% of the time, Pallas kernels for 0%

commit v1 on v0

v1 whole, which is shorter than its diff:
```python
import jax
import jax.numpy as jnp
from jax import lax
from jax.experimental import pallas as pl
from jax.experimental.pallas import tpu as pltpu
from jax.sharding import PartitionSpec as P


def _row_kernel(krow_ref, m0_ref, m1_ref, own_ref, y_ref, self_ref, lookup_ref, out_ref):
    i = pl.program_id(0)
    tiles = y_ref.shape[0]
    block = y_ref.shape[-1]

    def body(tp, carry):
        a0, a1 = carry
        at = i * tiles + tp
        k = krow_ref[at]
        p = jnp.dot(y_ref[tp, 0], lookup_ref[k], preferred_element_type=jnp.float32)
        a0 = a0 + jnp.where(m0_ref[at] != 0, p, 0.0)
        a1 = a1 + jnp.where(m1_ref[at] != 0, p, 0.0)
        return a0, a1

    zero = jnp.zeros((block, block), jnp.float32)
    a0, a1 = lax.fori_loop(0, tiles, body, (zero, zero))
    own = self_ref[0].astype(jnp.float32)
    own0 = jnp.where(own_ref[2 * i] != 0, own, 0.0)
    own1 = jnp.where(own_ref[2 * i + 1] != 0, own, 0.0)
    out_ref[0, 0] = (1.5 * own0 - 0.5 * a0).astype(out_ref.dtype)
    out_ref[0, 1] = (1.5 * own1 - 0.5 * a1).astype(out_ref.dtype)


def shards(y_blocks, y_cols, prod_blocks, prod_cols, out_cols):
    block_rows = y_blocks.shape[0]
    block_size = y_blocks.shape[2]
    out_width = out_cols.shape[2]

    lookup = lax.all_gather(prod_blocks[:, 0], "rows", axis=0, tiled=True)
    lookup_cols = lax.all_gather(prod_cols[:, 0], "rows", axis=0, tiled=True)
    left = lax.all_gather(y_blocks[:, 0], ("cols", "layers"), axis=0, tiled=False)
    left_cols = lax.all_gather(y_cols[:, 0], ("cols", "layers"), axis=0, tiled=False).T
    tiles = left.shape[0]

    krow = left_cols
    right_cols = lookup_cols[krow]
    m0 = (right_cols == out_cols[:, 0, 0][:, None]).astype(jnp.int32).reshape(-1)
    m1 = (right_cols == out_cols[:, 0, 1][:, None]).astype(jnp.int32).reshape(-1)
    own = (out_cols[:, 0, :] == y_cols[:, 0][:, None]).astype(jnp.int32).reshape(-1)

    nb = lookup.shape[0]
    out = pl.pallas_call(
        _row_kernel,
        out_shape=jax.ShapeDtypeStruct((block_rows, out_width, block_size, block_size), jnp.bfloat16),
        grid_spec=pltpu.PrefetchScalarGridSpec(
            num_scalar_prefetch=4,
            grid=(block_rows,),
            in_specs=[
                pl.BlockSpec((tiles, 1, block_size, block_size), lambda i, *_: (0, i, 0, 0)),
                pl.BlockSpec((1, block_size, block_size), lambda i, *_: (i, 0, 0)),
                pl.BlockSpec((nb, block_size, block_size), lambda i, *_: (0, 0, 0)),
            ],
            out_specs=pl.BlockSpec((1, out_width, block_size, block_size), lambda i, *_: (i, 0, 0, 0)),
        ),
        compiler_params=pltpu.CompilerParams(
            dimension_semantics=("arbitrary",),
            vmem_limit_bytes=40 * 1024 * 1024,
        ),
    )(krow.reshape(-1).astype(jnp.int32), m0, m1, own, left, y_blocks[:, 0], lookup)
    return out[:, None]


def solution(mesh):
    placed = (
        P("rows", ("cols", "layers"), None, None),
        P("rows", ("cols", "layers")),
        P("rows", ("cols", "layers"), None, None),
        P("rows", ("cols", "layers")),
        P("rows", ("cols", "layers"), None),
    )
    return jax.shard_map(
        shards,
        mesh=mesh,
        in_specs=placed,
        out_specs=P("rows", ("cols", "layers"), None, None, None),
        check_vma=False,
    )
```

time: 569 us -> 371 us (0.65)
  other arithmetic: 136 us -> 0.09 us
  Pallas kernels: 0 us -> 119 us
  local copies, waits for them, and re-layouts: 117 us -> 14.1 us
  matrix products: 70.6 us -> 0 us
  blocking collectives: 50.6 us -> 33 us
  waiting for transfers between devices: 179 us -> 190 us
    pallas_call x0 -> x1, Pallas kernels: none -> 119 us  [shards(): pl.pallas_call(_row_kernel, out_shape=jax.ShapeDtypeStruct((block_rows, o...]
    add x16 -> x0, other arithmetic: 83.7 us -> none  [advance(): return summed + weighted]
    dot_general x16 -> x0, matrix products: 70.6 us -> none  [advance(): jnp.einsum('igab,igtbc->igtac', left_blocks, right_blocks, preferred_elem...]
    gather x32 -> x2, local copies, waits for them, and re-layouts: 70.8 us -> 5.05 us  [shards(): right_cols = lookup_cols[krow]]
    reduce_sum x16 -> x0, other arithmetic: 43 us -> none  [advance(): jnp.sum(products[:, :, :, None] * present[..., None, None], axis=1)]
    mul x16 -> x0, local copies, waits for them, and re-layouts: 38 us -> none  [advance(): products[:, :, :, None] * present[..., None, None]]
    all_gather x1, blocking collectives: 36.9 us -> 13.1 us  [shards(): lookup_cols = lax.all_gather(prod_cols[:, 0], 'rows', axis=0, tiled=True)]
    all_gather x2, waiting for transfers between devices: 177 us -> 188 us  [the longest x1 185 us: shards(): lax.all_gather(y_blocks[:, 0], ('cols', 'layers'), axis=0, tiled=False)]
  transfers between devices with their start and end apart: 2 -> 2, of which waited for: 1 -> 2; matrix products, arithmetic and copies ran while one was open for 1% -> 3% of each run, Pallas kernels for 0% -> 0%
where the time goes in v1:
time: 371 us
  waiting for transfers between devices  190 us (51%)
  Pallas kernels  119 us (32%)
  blocking collectives  33 us (9%)
  between operations  14.7 us (4%)
  local copies, waits for them, and re-layouts  14.1 us (4%)
    all_gather x1, waiting for transfers between devices, shards(): lax.all_gather(y_blocks[:, 0], ('cols', 'layers'), axis=0, tiled=False)  185 us
    pallas_call x1, Pallas kernels, shards(): pl.pallas_call(_row_kernel, out_shape=jax.ShapeDtypeStruct((block_rows, o...  119 us
    unnamed x1, blocking collectives  19.8 us
    all_gather x1, blocking collectives, shards(): lookup_cols = lax.all_gather(prod_cols[:, 0], 'rows', axis=0, tiled=True)  13.1 us
    unnamed x13, local copies, waits for them, and re-layouts  7.66 us
  transfers between devices with their start and end apart: 2, of which 2 were waited for; matrix products, arithmetic and copies ran while one was open for 3% of the time, Pallas kernels for 0%

profile of v1, /device:TPU:1, one launch (start us, length us, event | category | flops | bytes accessed | tf_op | source)
XLA Modules:
  0.0 371.1 jit_solution(4124950261751456497)
XLA Ops:
  6.5 0.0 all-gather.9.cloned.1.call-start
  6.5 0.7 all-gather.9.cloned.1.call-update
  7.3 0.0 all-gather.7.cloned.1.call-start
  7.3 0.7 all-gather.7.cloned.1.call-update
  8.0 1.3 dynamic-slice.1
  9.3 1.3 dynamic-slice
  11.9 0.8 bitcast_dynamic-update-slice_fusion.1
  12.7 19.8 %all-reduce = s32[768]{0:T(1024)S(1)} all-reduce(s32[768]{0:T(1024)S(1)} %bitcast_dynamic-update-slice_fusion.1), channel_id=2, replica_groups=mesh['rows'=8,'cols'=8,'layers'=4] {'cols','layers'}, use_global_device_ids=true, to_apply=%add | all-reduce | flops 768 | bytes 6144
  32.5 0.1 reshape.31
  32.6 0.1 copy.14
  32.6 0.1 reshape.20.krow_ref
  32.7 0.7 eq.44
  33.5 0.1 eq.45
  33.5 0.8 copy.16
  34.3 0.1 squeeze.13
  34.4 0.1 copy.15
  34.5 0.1 reshape.25
  34.6 0.7 bitcast_dynamic-update-slice_fusion
  35.3 13.1 %all-reduce.1 = s32[192]{0:T(256)S(1)} all-reduce(s32[192]{0:T(256)S(1)} %bitcast_dynamic-update-slice_fusion), channel_id=3, replica_groups=mesh['rows'=8,'cols'=8,'layers'=4] {'rows'}, use_global_device_ids=true, to_apply=%add.1 | all-reduce | flops 192 | bytes 1536 | tf_op jit(solution)/shard_map/all_gather | solution.py:38
  48.5 0.0 copy-start.2
  48.5 0.0 copy-start.1
  48.5 5.0 %gather_fusion = s32[768]{0:T(1024)S(1)} fusion(s32[192]{0:T(256)S(1)} %all-reduce.1, s32[1024]{0:T(1024)S(1)} %pad_clamp_fusion), kind=kCustom, calls=%fused_computation | custom fusion | bytes 9216 | tf_op jit(solution)/shard_map/gather | solution.py:44
  53.5 0.1 reshape.24
  53.5 0.0 copy-done.2
  53.6 0.1 compare_convert_fusion
  53.6 0.1 reshape.22.m1_ref
  53.7 0.1 reshape.21.m0_ref
  53.8 3.1 all-gather.9.cloned.1.call-done
  56.9 185.1 %all-gather.7.cloned.1.call-done = bf16[768,1,128,128]{3,2,1,0:T(8,128)(2,1)} async-done(((bf16[24,1,128,128]{3,2,1,0:T(8,128)(2,1)}), bf16[768,1,128,128]{3,2,1,0:T(8,128)(2,1)}) %all-gather.7.cloned.1.call-update) | async-done | bytes 25165840 | tf_op jit(solution)/shard_map/all_gather | solution.py:39
  242.0 0.0 copy-done.1
  242.0 0.0 copy-start
  242.0 2.8 copy-done
  244.8 119.5 %shard_map.55 = bf16[24,2,128,128]{3,2,1,0:T(8,128)(2,1)} custom-call(s32[768]{0:T(1024)S(1)} %reshape.20.krow_ref, s32[768]{0:T(1024)S(1)} %reshape.21.m0_ref, s32[768]{0:T(1024)S(1)} %reshape.22.m1_ref, s32[48]{0:T(128)S(1)} %compare_convert_fusion.2.own_ref, bf16[32,24,128,128]{3,2,1,0:T(8,128)(2,1)} %bitcast.22, bf16[24,128,128]{2,1,0:T(8,128)(2,1)S(1)} %bitcast.21, ...), custom_call_target="tpu_custom_call" | custom-call | tf_op jit(solution)/shard_map/pallas_call | solution.py:50
  (6 shorter events, 0.0 us)
Async XLA Ops:
  6.5 50.4 %all-gather.9.cloned.1.call-start = ((), (), s32[]{:S(2)}) async-start(), calls=%async_computation.1 | async-start | bytes 7077888 | tf_op jit(solution)/shard_map/all_gather | solution.py:37
  7.3 234.7 %all-gather.7.cloned.1.call-start = ((), (), s32[]{:S(2)}) async-start(), calls=%async_computation | async-start | bytes 25952256 | tf_op jit(solution)/shard_map/all_gather | solution.py:39
  48.5 5.1 %copy-start.2 = (s32[24,1,2]{0,2,1:T(2,128)S(1)}, s32[24,1,2]{0,2,1:T(2,128)}, u32[]{:S(2)}) copy-start(s32[24,1,2]{0,2,1:T(2,128)} %param.9) | copy-start | bytes 580
  48.5 193.5 %copy-start.1 = (bf16[24,1,128,128]{3,2,1,0:T(8,128)(2,1)S(1)}, bf16[24,1,128,128]{3,2,1,0:T(8,128)(2,1)}, u32[]{:S(2)}) copy-start(bf16[24,1,128,128]{3,2,1,0:T(8,128)(2,1)} %param.5) | copy-start | bytes 2359300
  242.0 2.8 copy-start
Sparse Core Ops, SparseCore 0:
  9.2 47.6 all-gather.8
  59.5 182.4 all-gather.6

commit v2 on v1

--- a/solution.py
+++ b/solution.py
@@ -6,27 +6,32 @@
 from jax.sharding import PartitionSpec as P
 
 
-def _row_kernel(krow_ref, m0_ref, m1_ref, own_ref, y_ref, self_ref, lookup_ref, out_ref):
+def _row_kernel(krow_ref, m0_ref, m1_ref, own_ref, y_ref, self_ref, lookup_ref, out_ref, lhs_ref, stk_ref):
     i = pl.program_id(0)
     tiles = y_ref.shape[0]
-    block = y_ref.shape[-1]
+    bs = y_ref.shape[-1]
+    zeros = jnp.zeros((bs, bs), lhs_ref.dtype)
+    for tp in range(tiles):
+        at = i * tiles + tp
+        cols = slice(tp * bs, (tp + 1) * bs)
+        stk_ref[cols, :] = lookup_ref[krow_ref[at]]
+        for w, m_ref in ((0, m0_ref), (1, m1_ref)):
+            rows = slice(w * bs, (w + 1) * bs)
+            hit = m_ref[at] != 0
 
-    def body(tp, carry):
-        a0, a1 = carry
-        at = i * tiles + tp
-        k = krow_ref[at]
-        p = jnp.dot(y_ref[tp, 0], lookup_ref[k], preferred_element_type=jnp.float32)
-        a0 = a0 + jnp.where(m0_ref[at] != 0, p, 0.0)
-        a1 = a1 + jnp.where(m1_ref[at] != 0, p, 0.0)
-        return a0, a1
+            @pl.when(hit)
+            def _():
+                lhs_ref[rows, cols] = y_ref[tp, 0]
 
-    zero = jnp.zeros((block, block), jnp.float32)
-    a0, a1 = lax.fori_loop(0, tiles, body, (zero, zero))
+            @pl.when(jnp.logical_not(hit))
+            def _():
+                lhs_ref[rows, cols] = zeros
+
+    res = jnp.dot(lhs_ref[...], stk_ref[...], preferred_element_type=jnp.float32)
     own = self_ref[0].astype(jnp.float32)
-    own0 = jnp.where(own_ref[2 * i] != 0, own, 0.0)
-    own1 = jnp.where(own_ref[2 * i + 1] != 0, own, 0.0)
-    out_ref[0, 0] = (1.5 * own0 - 0.5 * a0).astype(out_ref.dtype)
-    out_ref[0, 1] = (1.5 * own1 - 0.5 * a1).astype(out_ref.dtype)
+    for w in range(2):
+        own_w = jnp.where(own_ref[2 * i + w] != 0, own, 0.0)
+        out_ref[0, w] = (1.5 * own_w - 0.5 * res[w * bs:(w + 1) * bs]).astype(out_ref.dtype)
 
 
 def shards(y_blocks, y_cols, prod_blocks, prod_cols, out_cols):
@@ -59,6 +64,10 @@
                 pl.BlockSpec((nb, block_size, block_size), lambda i, *_: (0, 0, 0)),
             ],
             out_specs=pl.BlockSpec((1, out_width, block_size, block_size), lambda i, *_: (i, 0, 0, 0)),
+            scratch_shapes=[
+                pltpu.VMEM((out_width * block_size, tiles * block_size), jnp.bfloat16),
+                pltpu.VMEM((tiles * block_size, block_size), jnp.bfloat16),
+            ],
         ),
         compiler_params=pltpu.CompilerParams(
             dimension_semantics=("arbitrary",),

time: 371 us -> 293 us (0.79)
  Pallas kernels: 119 us -> 41.4 us
    pallas_call x1, Pallas kernels: 119 us -> 41.4 us  [shards(): pl.pallas_call(_row_kernel, out_shape=jax.ShapeDtypeStruct((block_rows, o...]
  transfers between devices with their start and end apart: 2 -> 2, of which waited for: 2 -> 2; matrix products, arithmetic and copies ran while one was open for 3% -> 4% of each run, Pallas kernels for 0% -> 0%
where the time goes in v2:
time: 293 us
  waiting for transfers between devices  190 us (65%)
  Pallas kernels  41.4 us (14%)
  blocking collectives  33 us (11%)
  between operations  14.7 us (5%)
  local copies, waits for them, and re-layouts  14.1 us (5%)
    all_gather x1, waiting for transfers between devices, shards(): lax.all_gather(y_blocks[:, 0], ('cols', 'layers'), axis=0, tiled=False)  185 us
    pallas_call x1, Pallas kernels, shards(): pl.pallas_call(_row_kernel, out_shape=jax.ShapeDtypeStruct((block_rows, o...  41.4 us
    unnamed x1, blocking collectives  19.8 us
    all_gather x1, blocking collectives, shards(): lookup_cols = lax.all_gather(prod_cols[:, 0], 'rows', axis=0, tiled=True)  13.1 us
    unnamed x13, local copies, waits for them, and re-layouts  7.66 us
  transfers between devices with their start and end apart: 2, of which 2 were waited for; matrix products, arithmetic and copies ran while one was open for 4% of the time, Pallas kernels for 0%

profile of v2, /device:TPU:1, one launch (start us, length us, event | category | flops | bytes accessed | tf_op | source)
XLA Modules:
  0.0 293.0 jit_solution(7069063468067161705)
XLA Ops:
  6.5 0.0 all-gather.9.cloned.1.call-start
  6.5 0.7 all-gather.9.cloned.1.call-update
  7.3 0.0 all-gather.7.cloned.1.call-start
  7.3 0.7 all-gather.7.cloned.1.call-update
  8.0 1.3 dynamic-slice.1
  9.3 1.3 dynamic-slice
  11.9 0.8 bitcast_dynamic-update-slice_fusion.1
  12.7 19.8 %all-reduce = s32[768]{0:T(1024)S(1)} all-reduce(s32[768]{0:T(1024)S(1)} %bitcast_dynamic-update-slice_fusion.1), channel_id=2, replica_groups=mesh['rows'=8,'cols'=8,'layers'=4] {'cols','layers'}, use_global_device_ids=true, to_apply=%add | all-reduce | flops 768 | bytes 6144
  32.5 0.1 reshape.31
  32.6 0.1 copy.14
  32.6 0.1 reshape.20.krow_ref
  32.7 0.7 eq.44
  33.5 0.1 eq.45
  33.5 0.8 copy.16
  34.3 0.1 squeeze.13
  34.4 0.1 copy.15
  34.5 0.1 reshape.25
  34.6 0.7 bitcast_dynamic-update-slice_fusion
  35.3 13.1 %all-reduce.1 = s32[192]{0:T(256)S(1)} all-reduce(s32[192]{0:T(256)S(1)} %bitcast_dynamic-update-slice_fusion), channel_id=3, replica_groups=mesh['rows'=8,'cols'=8,'layers'=4] {'rows'}, use_global_device_ids=true, to_apply=%add.1 | all-reduce | flops 192 | bytes 1536 | tf_op jit(solution)/shard_map/all_gather | solution.py:43
  48.5 0.0 copy-start.2
  48.5 0.0 copy-start.1
  48.5 5.0 %gather_fusion = s32[768]{0:T(1024)S(1)} fusion(s32[192]{0:T(256)S(1)} %all-reduce.1, s32[1024]{0:T(1024)S(1)} %pad_clamp_fusion), kind=kCustom, calls=%fused_computation | custom fusion | bytes 9216 | tf_op jit(solution)/shard_map/gather | solution.py:49
  53.5 0.1 reshape.24
  53.5 0.0 copy-done.2
  53.6 0.1 compare_convert_fusion
  53.6 0.1 reshape.22.m1_ref
  53.7 0.1 reshape.21.m0_ref
  53.8 3.1 %all-gather.9.cloned.1.call-done = bf16[192,1,128,128]{3,2,1,0:T(8,128)(2,1)} async-done(((bf16[24,1,128,128]{3,2,1,0:T(8,128)(2,1)}), bf16[192,1,128,128]{3,2,1,0:T(8,128)(2,1)}) %all-gather.9.cloned.1.call-update) | async-done | bytes 6291472 | tf_op jit(solution)/shard_map/all_gather | solution.py:42
  56.9 185.1 %all-gather.7.cloned.1.call-done = bf16[768,1,128,128]{3,2,1,0:T(8,128)(2,1)} async-done(((bf16[24,1,128,128]{3,2,1,0:T(8,128)(2,1)}), bf16[768,1,128,128]{3,2,1,0:T(8,128)(2,1)}) %all-gather.7.cloned.1.call-update) | async-done | bytes 25165840 | tf_op jit(solution)/shard_map/all_gather | solution.py:44
  242.0 0.0 copy-done.1
  242.0 0.0 copy-start
  242.0 2.8 copy-done
  244.8 41.4 %shard_map.55 = bf16[24,2,128,128]{3,2,1,0:T(8,128)(2,1)} custom-call(s32[768]{0:T(1024)S(1)} %reshape.20.krow_ref, s32[768]{0:T(1024)S(1)} %reshape.21.m0_ref, s32[768]{0:T(1024)S(1)} %reshape.22.m1_ref, s32[48]{0:T(128)S(1)} %compare_convert_fusion.2.own_ref, bf16[32,24,128,128]{3,2,1,0:T(8,128)(2,1)} %bitcast.22, bf16[24,128,128]{2,1,0:T(8,128)(2,1)S(1)} %bitcast.21, ...), custom_call_target="tpu_custom_call" | custom-call | tf_op jit(solution)/shard_map/pallas_call | solution.py:55
  (6 shorter events, 0.0 us)
Async XLA Ops:
  6.5 50.4 %all-gather.9.cloned.1.call-start = ((), (), s32[]{:S(2)}) async-start(), calls=%async_computation.1 | async-start | bytes 7077888 | tf_op jit(solution)/shard_map/all_gather | solution.py:42
  7.3 234.7 %all-gather.7.cloned.1.call-start = ((), (), s32[]{:S(2)}) async-start(), calls=%async_computation | async-start | bytes 25952256 | tf_op jit(solution)/shard_map/all_gather | solution.py:44
  48.5 5.1 %copy-start.2 = (s32[24,1,2]{0,2,1:T(2,128)S(1)}, s32[24,1,2]{0,2,1:T(2,128)}, u32[]{:S(2)}) copy-start(s32[24,1,2]{0,2,1:T(2,128)} %param.9) | copy-start | bytes 580
  48.5 193.5 %copy-start.1 = (bf16[24,1,128,128]{3,2,1,0:T(8,128)(2,1)S(1)}, bf16[24,1,128,128]{3,2,1,0:T(8,128)(2,1)}, u32[]{:S(2)}) copy-start(bf16[24,1,128,128]{3,2,1,0:T(8,128)(2,1)} %param.5) | copy-start | bytes 2359300
  242.0 2.8 copy-start
Sparse Core Ops, SparseCore 0:
  9.2 47.6 all-gather.8
  59.5 182.4 all-gather.6

commit v3 on v2

--- a/solution.py
+++ b/solution.py
@@ -39,14 +39,20 @@
     block_size = y_blocks.shape[2]
     out_width = out_cols.shape[2]
 
-    lookup = lax.all_gather(prod_blocks[:, 0], "rows", axis=0, tiled=True)
+    groups = lax.axis_size("rows")
+    me = lax.axis_index("rows")
+    pieces = [prod_blocks[:, 0]]
+    for s in range(1, groups):
+        pieces.append(lax.ppermute(prod_blocks[:, 0], "rows", [(r, (r + s) % groups) for r in range(groups)]))
+    lookup = jnp.concatenate(pieces, axis=0)
     lookup_cols = lax.all_gather(prod_cols[:, 0], "rows", axis=0, tiled=True)
     left = lax.all_gather(y_blocks[:, 0], ("cols", "layers"), axis=0, tiled=False)
     left_cols = lax.all_gather(y_cols[:, 0], ("cols", "layers"), axis=0, tiled=False).T
     tiles = left.shape[0]
 
-    krow = left_cols
-    right_cols = lookup_cols[krow]
+    right_cols = lookup_cols[left_cols]
+    owner = left_cols // block_rows
+    krow = ((me - owner) % groups) * block_rows + left_cols % block_rows
     m0 = (right_cols == out_cols[:, 0, 0][:, None]).astype(jnp.int32).reshape(-1)
     m1 = (right_cols == out_cols[:, 0, 1][:, None]).astype(jnp.int32).reshape(-1)
     own = (out_cols[:, 0, :] == y_cols[:, 0][:, None]).astype(jnp.int32).reshape(-1)

time: 293 us -> 248 us (0.85)
  waiting for transfers between devices: 190 us -> 94.8 us
  blocking collectives: 33 us -> 56.3 us
  starting transfers between devices: 0.04 us -> 14.3 us
  local copies, waits for them, and re-layouts: 14.1 us -> 25.9 us
    all_gather x1, waiting for transfers between devices: 185 us -> 78.9 us  [shards(): lax.all_gather(y_blocks[:, 0], ('cols', 'layers'), axis=0, tiled=False)]
    all_gather x1, blocking collectives: 13.1 us -> 37.6 us  [shards(): lookup_cols = lax.all_gather(prod_cols[:, 0], 'rows', axis=0, tiled=True)]
    ppermute x0 -> x7, waiting for transfers between devices: none -> 15.2 us  [shards(): lax.ppermute(prod_blocks[:, 0], 'rows', [(r, (r + s) % groups) for r in r...]
    ppermute x0 -> x7, starting transfers between devices: none -> 14.3 us  [shards(): lax.ppermute(prod_blocks[:, 0], 'rows', [(r, (r + s) % groups) for r in r...]
    unnamed x13 -> x24, local copies, waits for them, and re-layouts: 7.66 us -> 18.4 us
    all_gather x1 -> x0, waiting for transfers between devices: 3.12 us -> none  [shards(): lookup = lax.all_gather(prod_blocks[:, 0], 'rows', axis=0, tiled=True)]
  transfers between devices with their start and end apart: 2 -> 8, of which waited for: 2 -> 3; matrix products, arithmetic and copies ran while one was open for 4% -> 9% of each run, Pallas kernels for 0% -> 0%
where the time goes in v3:
time: 248 us
  waiting for transfers between devices  94.8 us (38%)
  blocking collectives  56.3 us (23%)
  Pallas kernels  41.4 us (17%)
  local copies, waits for them, and re-layouts  25.9 us (10%)
  between operations  14.8 us (6%)
  starting transfers between devices  14.3 us (6%)
    all_gather x1, waiting for transfers between devices, shards(): lax.all_gather(y_blocks[:, 0], ('cols', 'layers'), axis=0, tiled=False)  78.9 us
    pallas_call x1, Pallas kernels, shards(): pl.pallas_call(_row_kernel, out_shape=jax.ShapeDtypeStruct((block_rows, o...  41.4 us
    all_gather x1, blocking collectives, shards(): lookup_cols = lax.all_gather(prod_cols[:, 0], 'rows', axis=0, tiled=True)  37.6 us
    unnamed x1, blocking collectives  18.6 us
    unnamed x24, local copies, waits for them, and re-layouts  18.4 us
    ppermute x7, waiting for transfers between devices, shards(): lax.ppermute(prod_blocks[:, 0], 'rows', [(r, (r + s) % groups) for r in r...  15.2 us
    ppermute x7, starting transfers between devices, shards(): lax.ppermute(prod_blocks[:, 0], 'rows', [(r, (r + s) % groups) for r in r...  14.3 us
    gather x2, local copies, waits for them, and re-layouts, shards(): right_cols = lookup_cols[left_cols]  5.05 us
  transfers between devices with their start and end apart: 8, of which 3 were waited for; matrix products, arithmetic and copies ran while one was open for 9% of the time, Pallas kernels for 0%

profile of v3, /device:TPU:1, one launch (start us, length us, event | category | flops | bytes accessed | tf_op | source)
XLA Modules:
  0.0 247.6 jit_solution(3738817436402131359)
XLA Ops:
  6.5 0.0 all-gather.5.cloned.1.call-start
  6.5 0.7 all-gather.5.cloned.1.call-update
  7.3 2.7 %collective-permute-start = (bf16[24,128,128]{2,1,0:T(8,128)(2,1)}, bf16[24,128,128]{2,1,0:T(8,128)(2,1)}, u32[]{:S(2)}, u32[]{:S(2)}) collective-permute-start(bf16[24,128,128]{2,1,0:T(8,128)(2,1)} %bitcast.38), channel_id=1, source_target_pairs={{0,32},{32,64},{64,96},{96,128},{128,160},{160,192},{192,224},{224... | collective-permute-start | bytes 2359304 | tf_op jit(solution)/shard_map/ppermute | solution.py:46
  9.9 1.3 collective-permute-start.1
  11.2 1.7 collective-permute-start.2
  12.9 1.3 collective-permute-start.3
  14.2 2.6 %collective-permute-start.4 = (bf16[24,128,128]{2,1,0:T(8,128)(2,1)}, bf16[24,128,128]{2,1,0:T(8,128)(2,1)S(1)}, u32[]{:S(2)}, u32[]{:S(2)}) collective-permute-start(bf16[24,128,128]{2,1,0:T(8,128)(2,1)} %bitcast.42), channel_id=1, source_target_pairs={{0,160},{32,192},{64,224},{96,0},{128,32},{160,64},{192,96},{224,1... | collective-permute-start | bytes 2359304 | tf_op jit(solution)/shard_map/ppermute | solution.py:46
  16.8 1.3 dynamic-slice
  18.8 0.8 bitcast_dynamic-update-slice_fusion.1
  19.5 18.6 %all-reduce = s32[768]{0:T(1024)S(1)} all-reduce(s32[768]{0:T(1024)S(1)} %bitcast_dynamic-update-slice_fusion.1), channel_id=2, replica_groups=mesh['rows'=8,'cols'=8,'layers'=4] {'cols','layers'}, use_global_device_ids=true, to_apply=%add | all-reduce | flops 768 | bytes 6144
  38.2 0.1 reshape.31
  38.3 1.3 dynamic-slice.1
  40.2 2.2 constant_dynamic-update-slice_fusion.7
  42.4 0.7 bitcast_dynamic-update-slice_fusion
  43.1 37.6 %all-reduce.1 = s32[192]{0:T(256)S(1)} all-reduce(s32[192]{0:T(256)S(1)} %bitcast_dynamic-update-slice_fusion), channel_id=3, replica_groups=mesh['rows'=8,'cols'=8,'layers'=4] {'rows'}, use_global_device_ids=true, to_apply=%add.1 | all-reduce | flops 192 | bytes 1536 | tf_op jit(solution)/shard_map/all_gather | solution.py:48
  80.8 0.1 copy.15
  80.8 0.1 reshape.25
  80.9 0.8 slice_bitcast_fusion
  81.7 0.0 copy-start.3
  81.7 0.0 copy-start.4
  81.7 0.0 copy-start.2
  81.7 5.0 %gather_fusion = s32[768]{0:T(1024)S(1)} fusion(s32[192]{0:T(256)S(1)} %all-reduce.1, s32[1024]{0:T(1024)S(1)} %pad_clamp_fusion), kind=kCustom, calls=%fused_computation | custom fusion | bytes 9216 | tf_op jit(solution)/shard_map/gather | solution.py:53
  86.7 0.0 copy-start.1
  86.7 0.1 reshape.24
  86.8 0.1 compare_convert_fusion
  86.8 0.0 copy-done.3
  86.8 0.1 copy.16
  86.9 0.1 reshape.21.m0_ref
  87.0 0.1 reshape.22.m1_ref
  87.1 0.1 copy.14
  87.1 0.1 reshape.20.krow_ref
  87.2 0.0 copy-done.4
  87.2 0.1 eq.47
  87.3 0.1 eq.48
  87.4 0.1 squeeze.9
  87.5 0.0 collective-permute-done
  87.5 0.0 copy-done.2
  87.5 2.5 %collective-permute-start.5 = (bf16[24,128,128]{2,1,0:T(8,128)(2,1)S(1)}, bf16[24,128,128]{2,1,0:T(8,128)(2,1)S(1)}, u32[]{:S(2)}, u32[]{:S(2)}) collective-permute-start(bf16[24,128,128]{2,1,0:T(8,128)(2,1)S(1)} %bitcast.43), channel_id=1, source_target_pairs={{0,192},{32,224},{64,0},{96,32},{128,64},{160,96},{192,128},{224,1... | collective-permute-start | bytes 2359304 | tf_op jit(solution)/shard_map/ppermute | solution.py:46
  90.0 0.0 collective-permute-done.1
  90.0 2.2 collective-permute-start.6
  92.3 2.1 constant_dynamic-update-slice_fusion.6
  94.4 2.1 constant_dynamic-update-slice_fusion.5
  96.5 0.0 collective-permute-done.2
  96.5 2.1 constant_dynamic-update-slice_fusion.4
  98.6 0.0 collective-permute-done.3
  98.6 1.0 constant_dynamic-update-slice_fusion.3
  99.6 0.0 collective-permute-done.4
  99.6 1.0 constant_dynamic-update-slice_fusion.2
  100.6 6.1 %collective-permute-done.5 = bf16[24,128,128]{2,1,0:T(8,128)(2,1)S(1)} collective-permute-done((bf16[24,128,128]{2,1,0:T(8,128)(2,1)S(1)}, bf16[24,128,128]{2,1,0:T(8,128)(2,1)S(1)}, u32[]{:S(2)}, u32[]{:S(2)}) %collective-permute-start.5) | collective-permute-done | bytes 786464 | tf_op jit(solution)/shard_map/ppermute | solution.py:46
  106.7 1.0 constant_dynamic-update-slice_fusion.1
  107.6 9.1 %collective-permute-done.6 = bf16[24,128,128]{2,1,0:T(8,128)(2,1)S(1)} collective-permute-done((bf16[24,128,128]{2,1,0:T(8,128)(2,1)S(1)}, bf16[24,128,128]{2,1,0:T(8,128)(2,1)S(1)}, u32[]{:S(2)}, u32[]{:S(2)}) %collective-permute-start.6) | collective-permute-done | bytes 786464 | tf_op jit(solution)/shard_map/ppermute | solution.py:46
  116.8 0.9 constant_dynamic-update-slice_fusion.lookup_ref
  117.7 78.9 %all-gather.5.cloned.1.call-done = bf16[768,1,128,128]{3,2,1,0:T(8,128)(2,1)} async-done(((bf16[24,1,128,128]{3,2,1,0:T(8,128)(2,1)}), bf16[768,1,128,128]{3,2,1,0:T(8,128)(2,1)}) %all-gather.5.cloned.1.call-update) | async-done | bytes 25165840 | tf_op jit(solution)/shard_map/all_gather | solution.py:49
  196.6 0.0 copy-done.1
  196.6 0.0 copy-start
  196.6 2.8 %copy-done = bf16[192,128,128]{2,1,0:T(8,128)(2,1)S(1)} copy-done((bf16[192,128,128]{2,1,0:T(8,128)(2,1)S(1)}, bf16[192,128,128]{2,1,0:T(8,128)(2,1)}, u32[]{:S(2)}) %copy-start) | copy-done | bytes 6291480
  199.4 41.4 %shard_map.55 = bf16[24,2,128,128]{3,2,1,0:T(8,128)(2,1)} custom-call(s32[768]{0:T(1024)S(1)} %reshape.20.krow_ref, s32[768]{0:T(1024)S(1)} %reshape.21.m0_ref, s32[768]{0:T(1024)S(1)} %reshape.22.m1_ref, s32[48]{0:T(128)S(1)} %compare_convert_fusion.2.own_ref, bf16[32,24,128,128]{3,2,1,0:T(8,128)(2,1)} %bitcast.37, bf16[24,128,128]{2,1,0:T(8,128)(2,1)S(1)} %bitcast.36, ...), custom_call_target="tpu_custom_call" | custom-call | tf_op jit(solution)/shard_map/pallas_call | solution.py:61
  (5 shorter events, 0.0 us)
Async XLA Ops:
  6.5 190.1 %all-gather.5.cloned.1.call-start = ((), (), s32[]{:S(2)}) async-start(), calls=%async_computation | async-start | bytes 25952256 | tf_op jit(solution)/shard_map/all_gather | solution.py:49
  7.3 80.3 %collective-permute-start = (bf16[24,128,128]{2,1,0:T(8,128)(2,1)}, bf16[24,128,128]{2,1,0:T(8,128)(2,1)}, u32[]{:S(2)}, u32[]{:S(2)}) collective-permute-start(bf16[24,128,128]{2,1,0:T(8,128)(2,1)} %bitcast.38), channel_id=1, source_target_pairs={{0,32},{32,64},{64,96},{96,128},{128,160},{160,192},{192,224},{224... | collective-permute-start | bytes 2359304 | tf_op jit(solution)/shard_map/ppermute | solution.py:46
  9.9 80.1 %collective-permute-start.1 = (bf16[24,128,128]{2,1,0:T(8,128)(2,1)}, bf16[24,128,128]{2,1,0:T(8,128)(2,1)}, u32[]{:S(2)}, u32[]{:S(2)}) collective-permute-start(bf16[24,128,128]{2,1,0:T(8,128)(2,1)} %bitcast.39), channel_id=1, source_target_pairs={{0,64},{32,96},{64,128},{96,160},{128,192},{160,224},{192,0},{224,... | collective-permute-start | bytes 2359304 | tf_op jit(solution)/shard_map/ppermute | solution.py:46
  11.2 85.3 %collective-permute-start.2 = (bf16[24,128,128]{2,1,0:T(8,128)(2,1)}, bf16[24,128,128]{2,1,0:T(8,128)(2,1)}, u32[]{:S(2)}, u32[]{:S(2)}) collective-permute-start(bf16[24,128,128]{2,1,0:T(8,128)(2,1)} %bitcast.40), channel_id=1, source_target_pairs={{0,96},{32,128},{64,160},{96,192},{128,224},{160,0},{192,32},{224,... | collective-permute-start | bytes 2359304 | tf_op jit(solution)/shard_map/ppermute | solution.py:46
  12.9 85.7 %collective-permute-start.3 = (bf16[24,128,128]{2,1,0:T(8,128)(2,1)}, bf16[24,128,128]{2,1,0:T(8,128)(2,1)S(1)}, u32[]{:S(2)}, u32[]{:S(2)}) collective-permute-start(bf16[24,128,128]{2,1,0:T(8,128)(2,1)} %bitcast.41), channel_id=1, source_target_pairs={{0,128},{32,160},{64,192},{96,224},{128,0},{160,32},{192,64},{224,... | collective-permute-start | bytes 2359304 | tf_op jit(solution)/shard_map/ppermute | solution.py:46
  14.2 85.4 %collective-permute-start.4 = (bf16[24,128,128]{2,1,0:T(8,128)(2,1)}, bf16[24,128,128]{2,1,0:T(8,128)(2,1)S(1)}, u32[]{:S(2)}, u32[]{:S(2)}) collective-permute-start(bf16[24,128,128]{2,1,0:T(8,128)(2,1)} %bitcast.42), channel_id=1, source_target_pairs={{0,160},{32,192},{64,224},{96,0},{128,32},{160,64},{192,96},{224,1... | collective-permute-start | bytes 2359304 | tf_op jit(solution)/shard_map/ppermute | solution.py:46
  81.7 5.2 %copy-start.3 = (s32[24,1,2]{0,2,1:T(2,128)S(1)}, s32[24,1,2]{0,2,1:T(2,128)}, u32[]{:S(2)}) copy-start(s32[24,1,2]{0,2,1:T(2,128)} %param.9) | copy-start | bytes 580
  81.7 5.6 %copy-start.4 = (s32[24,1]{0,1:T(1,128)S(1)}, s32[24,1]{0,1:T(1,128)}, u32[]{:S(2)}) copy-start(s32[24,1]{0,1:T(1,128)} %param.6) | copy-start | bytes 292
  81.7 5.8 %copy-start.2 = (bf16[24,1,128,128]{3,2,1,0:T(8,128)(2,1)S(1)}, bf16[24,1,128,128]{3,2,1,0:T(8,128)(2,1)}, u32[]{:S(2)}) copy-start(bf16[24,1,128,128]{3,2,1,0:T(8,128)(2,1)} %param.7) | copy-start | bytes 2359300
  86.7 109.9 %copy-start.1 = (bf16[24,1,128,128]{3,2,1,0:T(8,128)(2,1)S(1)}, bf16[24,1,128,128]{3,2,1,0:T(8,128)(2,1)}, u32[]{:S(2)}) copy-start(bf16[24,1,128,128]{3,2,1,0:T(8,128)(2,1)} %param.5) | copy-start | bytes 2359300
  87.5 19.1 %collective-permute-start.5 = (bf16[24,128,128]{2,1,0:T(8,128)(2,1)S(1)}, bf16[24,128,128]{2,1,0:T(8,128)(2,1)S(1)}, u32[]{:S(2)}, u32[]{:S(2)}) collective-permute-start(bf16[24,128,128]{2,1,0:T(8,128)(2,1)S(1)} %bitcast.43), channel_id=1, source_target_pairs={{0,192},{32,224},{64,0},{96,32},{128,64},{160,96},{192,128},{224,1... | collective-permute-start | bytes 2359304 | tf_op jit(solution)/shard_map/ppermute | solution.py:46
  90.0 26.7 %collective-permute-start.6 = (bf16[24,128,128]{2,1,0:T(8,128)(2,1)S(1)}, bf16[24,128,128]{2,1,0:T(8,128)(2,1)S(1)}, u32[]{:S(2)}, u32[]{:S(2)}) collective-permute-start(bf16[24,128,128]{2,1,0:T(8,128)(2,1)S(1)} %bitcast.44), channel_id=1, source_target_pairs={{0,224},{32,0},{64,32},{96,64},{128,96},{160,128},{192,160},{224,1... | collective-permute-start | bytes 2359304 | tf_op jit(solution)/shard_map/ppermute | solution.py:46
  196.6 2.8 %copy-start = (bf16[192,128,128]{2,1,0:T(8,128)(2,1)S(1)}, bf16[192,128,128]{2,1,0:T(8,128)(2,1)}, u32[]{:S(2)}) copy-start(bf16[192,128,128]{2,1,0:T(8,128)(2,1)} %constant_dynamic-update-slice_fusion.lookup_ref) | copy-start | bytes 18874372
Sparse Core Ops, SparseCore 0:
  9.9 186.6 all-gather.4

commit v4 on v2

v4 whole, which is shorter than its diff:
```python
import jax
import jax.numpy as jnp
from jax import lax
from jax.experimental import pallas as pl
from jax.experimental.pallas import tpu as pltpu
from jax.sharding import PartitionSpec as P


CHUNKS = 4


def _row_kernel(i0_ref, i1_ref, own_ref, y_ref, self_ref, lookup_ref, out_ref, lhs_ref, stk_ref):
    i = pl.program_id(0)
    tiles = y_ref.shape[0]
    bs = y_ref.shape[-1]
    for tp in range(tiles):
        at = i * tiles + tp
        cols = slice(tp * bs, (tp + 1) * bs)
        lhs_ref[:, cols] = y_ref[tp, 0]
        stk_ref[cols, 0:bs] = lookup_ref[i0_ref[at]]
        stk_ref[cols, bs:2 * bs] = lookup_ref[i1_ref[at]]
    res = jnp.dot(lhs_ref[...], stk_ref[...], preferred_element_type=jnp.float32)
    own = self_ref[0].astype(jnp.float32)
    for w in range(2):
        own_w = jnp.where(own_ref[2 * i + w] != 0, own, 0.0)
        out_ref[0, w] = (1.5 * own_w - 0.5 * res[:, w * bs:(w + 1) * bs]).astype(out_ref.dtype)


def _rows_product(i0, i1, own, left, own_blocks, lookup, out_width):
    tiles, block_rows, block_size, _ = left.shape
    nb = lookup.shape[0]
    return pl.pallas_call(
        _row_kernel,
        out_shape=jax.ShapeDtypeStruct((block_rows, out_width, block_size, block_size), jnp.bfloat16),
        grid_spec=pltpu.PrefetchScalarGridSpec(
            num_scalar_prefetch=3,
            grid=(block_rows,),
            in_specs=[
                pl.BlockSpec((tiles, 1, block_size, block_size), lambda i, *_: (0, i, 0, 0)),
                pl.BlockSpec((1, block_size, block_size), lambda i, *_: (i, 0, 0)),
                pl.BlockSpec((nb, block_size, block_size), lambda i, *_: (0, 0, 0)),
            ],
            out_specs=pl.BlockSpec((1, out_width, block_size, block_size), lambda i, *_: (i, 0, 0, 0)),
            scratch_shapes=[
                pltpu.VMEM((block_size, tiles * block_size), jnp.bfloat16),
                pltpu.VMEM((tiles * block_size, out_width * block_size), jnp.bfloat16),
            ],
        ),
        compiler_params=pltpu.CompilerParams(
            dimension_semantics=("arbitrary",),
            vmem_limit_bytes=40 * 1024 * 1024,
        ),
    )(i0, i1, own, left, own_blocks, lookup)


def shards(y_blocks, y_cols, prod_blocks, prod_cols, out_cols):
    block_rows = y_blocks.shape[0]
    block_size = y_blocks.shape[2]
    out_width = out_cols.shape[2]

    groups = lax.axis_size("rows")
    me = lax.axis_index("rows")
    pieces = [prod_blocks[:, 0]]
    for s in range(1, groups):
        pieces.append(lax.ppermute(prod_blocks[:, 0], "rows", [(r, (r + s) % groups) for r in range(groups)]))
    pieces.append(jnp.zeros((1, block_size, block_size), prod_blocks.dtype))
    lookup = jnp.concatenate(pieces, axis=0)
    nb = groups * block_rows
    lookup_cols = lax.all_gather(prod_cols[:, 0], "rows", axis=0, tiled=True)
    left_cols = lax.all_gather(y_cols[:, 0], ("cols", "layers"), axis=0, tiled=False).T

    right_cols = lookup_cols[left_cols]
    owner = left_cols // block_rows
    krow = ((me - owner) % groups) * block_rows + left_cols % block_rows
    i0 = jnp.where(right_cols == out_cols[:, 0, 0][:, None], krow, nb).astype(jnp.int32)
    i1 = jnp.where(right_cols == out_cols[:, 0, 1][:, None], krow, nb).astype(jnp.int32)
    own = (out_cols[:, 0, :] == y_cols[:, 0][:, None]).astype(jnp.int32)

    step = block_rows // CHUNKS
    outs = []
    for c in range(CHUNKS):
        rows = slice(c * step, (c + 1) * step)
        left = lax.all_gather(y_blocks[rows, 0], ("cols", "layers"), axis=0, tiled=False)
        outs.append(_rows_product(
            i0[rows].reshape(-1), i1[rows].reshape(-1), own[rows].reshape(-1),
            left, y_blocks[rows, 0], lookup, out_width))
    return jnp.concatenate(outs, axis=0)[:, None]


def solution(mesh):
    placed = (
        P("rows", ("cols", "layers"), None, None),
        P("rows", ("cols", "layers")),
        P("rows", ("cols", "layers"), None, None),
        P("rows", ("cols", "layers")),
        P("rows", ("cols", "layers"), None),
    )
    return jax.shard_map(
        shards,
        mesh=mesh,
        in_specs=placed,
        out_specs=P("rows", ("cols", "layers"), None, None, None),
        check_vma=False,
    )
```

time: 293 us -> 385 us (1.31)
  local copies, waits for them, and re-layouts: 14.1 us -> 52.4 us
  waiting for transfers between devices: 190 us -> 216 us
  blocking collectives: 33 us -> 58.1 us
  starting transfers between devices: 0.04 us -> 14.4 us
  Pallas kernels: 41.4 us -> 27.1 us
    unnamed x13 -> x36, local copies, waits for them, and re-layouts: 7.66 us -> 41.2 us
    all_gather x1, blocking collectives: 13.1 us -> 39.6 us  [shards(): lookup_cols = lax.all_gather(prod_cols[:, 0], 'rows', axis=0, tiled=True)]
    all_gather x2 -> x4, waiting for transfers between devices: 188 us -> 204 us  [shards(): lax.all_gather(y_blocks[rows, 0], ('cols', 'layers'), axis=0, tiled=False)]
    pallas_call x1 -> x4, Pallas kernels: 41.4 us -> 27.1 us  [_rows_product(): pl.pallas_call(_row_kernel, out_shape=jax.ShapeDtypeStruct((block_rows, o...]
    ppermute x0 -> x7, starting transfers between devices: none -> 14.3 us  [shards(): lax.ppermute(prod_blocks[:, 0], 'rows', [(r, (r + s) % groups) for r in r...]
    ppermute x0 -> x7, waiting for transfers between devices: none -> 10.9 us  [shards(): lax.ppermute(prod_blocks[:, 0], 'rows', [(r, (r + s) % groups) for r in r...]
  transfers between devices with their start and end apart: 2 -> 11, of which waited for: 2 -> 5; matrix products, arithmetic and copies ran while one was open for 4% -> 7% of each run, Pallas kernels for 0% -> 5%
where the time goes in v4:
time: 385 us; the launch traced here: 384 us
  waiting for transfers between devices  216 us (56%)
  blocking collectives  58.1 us (15%)
  local copies, waits for them, and re-layouts  52.4 us (14%)
  Pallas kernels  27.1 us (7%)
  between operations  14.7 us (4%)
  starting transfers between devices  14.4 us (4%)
    all_gather x4, waiting for transfers between devices, shards(): lax.all_gather(y_blocks[rows, 0], ('cols', 'layers'), axis=0, tiled=False)  204 us
    unnamed x36, local copies, waits for them, and re-layouts  41.2 us
    all_gather x1, blocking collectives, shards(): lookup_cols = lax.all_gather(prod_cols[:, 0], 'rows', axis=0, tiled=True)  39.6 us
    pallas_call x4, Pallas kernels, _rows_product(): pl.pallas_call(_row_kernel, out_shape=jax.ShapeDtypeStruct((block_rows, o...  27.1 us
    unnamed x1, blocking collectives  18.4 us
    ppermute x7, starting transfers between devices, shards(): lax.ppermute(prod_blocks[:, 0], 'rows', [(r, (r + s) % groups) for r in r...  14.3 us
    ppermute x7, waiting for transfers between devices, shards(): lax.ppermute(prod_blocks[:, 0], 'rows', [(r, (r + s) % groups) for r in r...  10.9 us
  transfers between devices with their start and end apart: 11, of which 5 were waited for; matrix products, arithmetic and copies ran while one was open for 7% of the time, Pallas kernels for 5%

profile of v4, /device:TPU:1, one launch (start us, length us, event | category | flops | bytes accessed | tf_op | source)
XLA Modules:
  0.0 384.4 jit_solution(5628948737842483865)
XLA Ops:
  6.5 2.4 slice_bitcast_fusion.6
  9.0 0.7 all-gather.13.cloned.1.call-update
  9.7 0.7 all-gather.15.cloned.1.call-update
  10.5 0.5 all-gather.17.cloned.1.call-update
  11.0 2.7 collective-permute-start
  13.7 1.3 collective-permute-start.1
  15.0 1.7 collective-permute-start.2
  16.7 1.3 collective-permute-start.3
  18.0 2.6 collective-permute-start.4
  20.6 1.3 dynamic-slice.1
  22.6 0.8 bitcast_dynamic-update-slice_fusion.1
  23.4 18.4 %all-reduce.1 = s32[768]{0:T(1024)S(1)} all-reduce(s32[768]{0:T(1024)S(1)} %bitcast_dynamic-update-slice_fusion.1), channel_id=3, replica_groups=mesh['rows'=8,'cols'=8,'layers'=4] {'cols','layers'}, use_global_device_ids=true, to_apply=%add.1 | all-reduce | flops 768 | bytes 6144
  41.8 0.1 reshape.59
  42.1 1.3 dynamic-slice
  44.1 0.8 bitcast_dynamic-update-slice_fusion
  44.9 39.6 %all-reduce = s32[192]{0:T(256)S(1)} all-reduce(s32[192]{0:T(256)S(1)} %bitcast_dynamic-update-slice_fusion), channel_id=2, replica_groups=mesh['rows'=8,'cols'=8,'layers'=4] {'rows'}, use_global_device_ids=true, to_apply=%add | all-reduce | flops 192 | bytes 1536 | tf_op jit(solution)/shard_map/all_gather | solution.py:69
  84.5 0.8 slice_bitcast_fusion.8
  85.3 2.1 constant_dynamic-update-slice_fusion.8
  87.4 5.0 %gather_fusion = s32[768]{0:T(1024)S(1)} fusion(s32[192]{0:T(256)S(1)} %all-reduce, s32[1024]{0:T(1024)S(1)} %pad_clamp_fusion), kind=kCustom, calls=%fused_computation | custom fusion | bytes 9216 | tf_op jit(solution)/shard_map/gather | solution.py:72
  92.6 0.1 fusion.6
  92.8 0.1 reshape.38.i0_ref
  93.0 0.1 reshape.39.i1_ref
  93.0 2.5 collective-permute-start.5
  95.6 0.1 copy.40
  95.7 0.1 reshape.40.own_ref
  95.8 0.1 reshape.41.i0_ref
  96.0 0.1 reshape.42.i1_ref
  96.1 0.1 copy.45
  96.2 0.1 reshape.43.own_ref
  96.3 0.1 reshape.44.i0_ref
  96.5 0.1 reshape.45.i1_ref
  96.6 0.1 copy.50
  96.7 0.1 reshape.46.own_ref
  96.8 0.1 reshape.47.i0_ref
  97.0 0.1 reshape.48.i1_ref
  97.1 0.1 copy.55
  97.2 0.1 reshape.49.own_ref
  97.2 2.2 collective-permute-start.6
  99.5 2.1 constant_dynamic-update-slice_fusion.7
  101.6 2.1 constant_dynamic-update-slice_fusion.6
  103.7 2.1 constant_dynamic-update-slice_fusion.5
  105.8 2.1 constant_dynamic-update-slice_fusion.4
  107.9 0.9 constant_dynamic-update-slice_fusion.3
  108.9 3.3 collective-permute-done.5
  112.2 2.1 constant_dynamic-update-slice_fusion.2
  114.3 7.6 %collective-permute-done.6 = bf16[24,128,128]{2,1,0:T(8,128)(2,1)S(1)} collective-permute-done((bf16[24,128,128]{2,1,0:T(8,128)(2,1)S(1)}, bf16[24,128,128]{2,1,0:T(8,128)(2,1)S(1)}, u32[]{:S(2)}, u32[]{:S(2)}) %collective-permute-start.6) | collective-permute-done | bytes 786464 | tf_op jit(solution)/shard_map/ppermute | solution.py:65
  121.9 1.0 constant_dynamic-update-slice_fusion.1
  122.8 0.6 constant_dynamic-update-slice_fusion.lookup_ref
  123.4 2.8 copy-done
  126.3 2.8 copy-done.5
  129.1 6.8 %shard_map.55 = bf16[6,2,128,128]{3,2,1,0:T(8,128)(2,1)S(1)} custom-call(s32[192]{0:T(256)S(1)} %reshape.38.i0_ref, s32[192]{0:T(256)S(1)} %reshape.39.i1_ref, s32[12]{0:T(128)S(1)} %reshape.40.own_ref, bf16[32,6,128,128]{3,2,1,0:T(8,128)(2,1)S(1)} %bitcast.61, bf16[6,128,128]{2,1,0:T(8,128)(2,1)S(1)} %get-tuple-element.5.self_ref, ...), custom_call_target="tpu_custom_call" | custom-call | tf_op jit(solution)/shard_map/pallas_call | solution.py:32
  135.8 53.0 %all-gather.13.cloned.1.call-done = bf16[192,1,128,128]{3,2,1,0:T(8,128)(2,1)} async-done(((bf16[6,1,128,128]{3,2,1,0:T(8,128)(2,1)}), bf16[192,1,128,128]{3,2,1,0:T(8,128)(2,1)}) %all-gather.13.cloned.1.call-update) | async-done | bytes 6291472 | tf_op jit(solution)/shard_map/all_gather | solution.py:83
  188.8 2.8 copy-done.1
  191.6 2.8 copy-done.6
  194.4 6.8 %shard_map.56 = bf16[6,2,128,128]{3,2,1,0:T(8,128)(2,1)S(1)} custom-call(s32[192]{0:T(256)S(1)} %reshape.41.i0_ref, s32[192]{0:T(256)S(1)} %reshape.42.i1_ref, s32[12]{0:T(128)S(1)} %reshape.43.own_ref, bf16[32,6,128,128]{3,2,1,0:T(8,128)(2,1)S(1)} %bitcast.62, bf16[6,128,128]{2,1,0:T(8,128)(2,1)S(1)} %get-tuple-element.6.self_ref, ...), custom_call_target="tpu_custom_call" | custom-call | tf_op jit(solution)/shard_map/pallas_call | solution.py:32
  201.2 75.4 %all-gather.15.cloned.1.call-done = bf16[192,1,128,128]{3,2,1,0:T(8,128)(2,1)} async-done(((bf16[6,1,128,128]{3,2,1,0:T(8,128)(2,1)}), bf16[192,1,128,128]{3,2,1,0:T(8,128)(2,1)}) %all-gather.15.cloned.1.call-update) | async-done | bytes 6291472 | tf_op jit(solution)/shard_map/all_gather | solution.py:83
  276.6 2.8 copy-done.2
  279.4 2.8 copy-done.7
  282.2 6.8 %shard_map.57 = bf16[6,2,128,128]{3,2,1,0:T(8,128)(2,1)S(1)} custom-call(s32[192]{0:T(256)S(1)} %reshape.44.i0_ref, s32[192]{0:T(256)S(1)} %reshape.45.i1_ref, s32[12]{0:T(128)S(1)} %reshape.46.own_ref, bf16[32,6,128,128]{3,2,1,0:T(8,128)(2,1)S(1)} %bitcast.63, bf16[6,128,128]{2,1,0:T(8,128)(2,1)S(1)} %get-tuple-element.7.self_ref, ...), custom_call_target="tpu_custom_call" | custom-call | tf_op jit(solution)/shard_map/pallas_call | solution.py:32
  289.0 75.3 %all-gather.17.cloned.1.call-done = bf16[192,1,128,128]{3,2,1,0:T(8,128)(2,1)} async-done(((bf16[6,1,128,128]{3,2,1,0:T(8,128)(2,1)}), bf16[192,1,128,128]{3,2,1,0:T(8,128)(2,1)}) %all-gather.17.cloned.1.call-update) | async-done | bytes 6291472 | tf_op jit(solution)/shard_map/all_gather | solution.py:83
  364.2 2.8 copy-done.3
  367.0 2.8 copy-done.4
  369.8 6.8 %shard_map.58 = bf16[6,2,128,128]{3,2,1,0:T(8,128)(2,1)S(1)} custom-call(s32[192]{0:T(256)S(1)} %reshape.47.i0_ref, s32[192]{0:T(256)S(1)} %reshape.48.i1_ref, s32[12]{0:T(128)S(1)} %reshape.49.own_ref, bf16[32,6,128,128]{3,2,1,0:T(8,128)(2,1)S(1)} %bitcast.60, bf16[6,128,128]{2,1,0:T(8,128)(2,1)S(1)} %get-tuple-element.8.self_ref, ...), custom_call_target="tpu_custom_call" | custom-call | tf_op jit(solution)/shard_map/pallas_call | solution.py:32
  376.6 1.3 maximum_bitcast_fusion
  (44 shorter events, 1.2 us)
Async XLA Ops:
  6.5 116.9 %all-gather.11.cloned.1.call-start = ((), (), s32[]{:S(2)}) async-start(), calls=%async_computation | async-start | bytes 6488064 | tf_op jit(solution)/shard_map/all_gather | solution.py:83
  8.9 179.9 %all-gather.13.cloned.1.call-start = ((), (), s32[]{:S(2)}) async-start(), calls=%async_computation.1 | async-start | bytes 6488064 | tf_op jit(solution)/shard_map/all_gather | solution.py:83
  9.7 266.9 %all-gather.15.cloned.1.call-start = ((), (), s32[]{:S(2)}) async-start(), calls=%async_computation.2 | async-start | bytes 6488064 | tf_op jit(solution)/shard_map/all_gather | solution.py:83
  10.4 353.8 %all-gather.17.cloned.1.call-start = ((), (), s32[]{:S(2)}) async-start(), calls=%async_computation.3 | async-start | bytes 6488064 | tf_op jit(solution)/shard_map/all_gather | solution.py:83
  11.0 82.0 %collective-permute-start = (bf16[24,128,128]{2,1,0:T(8,128)(2,1)}, bf16[24,128,128]{2,1,0:T(8,128)(2,1)}, u32[]{:S(2)}, u32[]{:S(2)}) collective-permute-start(bf16[24,128,128]{2,1,0:T(8,128)(2,1)} %bitcast.64), channel_id=1, source_target_pairs={{0,32},{32,64},{64,96},{96,128},{128,160},{160,192},{192,224},{224... | collective-permute-start | bytes 2359304 | tf_op jit(solution)/shard_map/ppermute | solution.py:65
  13.7 83.5 %collective-permute-start.1 = (bf16[24,128,128]{2,1,0:T(8,128)(2,1)}, bf16[24,128,128]{2,1,0:T(8,128)(2,1)}, u32[]{:S(2)}, u32[]{:S(2)}) collective-permute-start(bf16[24,128,128]{2,1,0:T(8,128)(2,1)} %bitcast.65), channel_id=1, source_target_pairs={{0,64},{32,96},{64,128},{96,160},{128,192},{160,224},{192,0},{224,... | collective-permute-start | bytes 2359304 | tf_op jit(solution)/shard_map/ppermute | solution.py:65
  15.0 88.7 %collective-permute-start.2 = (bf16[24,128,128]{2,1,0:T(8,128)(2,1)}, bf16[24,128,128]{2,1,0:T(8,128)(2,1)}, u32[]{:S(2)}, u32[]{:S(2)}) collective-permute-start(bf16[24,128,128]{2,1,0:T(8,128)(2,1)} %bitcast.66), channel_id=1, source_target_pairs={{0,96},{32,128},{64,160},{96,192},{128,224},{160,0},{192,32},{224,... | collective-permute-start | bytes 2359304 | tf_op jit(solution)/shard_map/ppermute | solution.py:65
  16.7 89.1 %collective-permute-start.3 = (bf16[24,128,128]{2,1,0:T(8,128)(2,1)}, bf16[24,128,128]{2,1,0:T(8,128)(2,1)}, u32[]{:S(2)}, u32[]{:S(2)}) collective-permute-start(bf16[24,128,128]{2,1,0:T(8,128)(2,1)} %bitcast.67), channel_id=1, source_target_pairs={{0,128},{32,160},{64,192},{96,224},{128,0},{160,32},{192,64},{224,... | collective-permute-start | bytes 2359304 | tf_op jit(solution)/shard_map/ppermute | solution.py:65
  18.0 90.0 %collective-permute-start.4 = (bf16[24,128,128]{2,1,0:T(8,128)(2,1)}, bf16[24,128,128]{2,1,0:T(8,128)(2,1)S(1)}, u32[]{:S(2)}, u32[]{:S(2)}) collective-permute-start(bf16[24,128,128]{2,1,0:T(8,128)(2,1)} %bitcast.68), channel_id=1, source_target_pairs={{0,160},{32,192},{64,224},{96,0},{128,32},{160,64},{192,96},{224,1... | collective-permute-start | bytes 2359304 | tf_op jit(solution)/shard_map/ppermute | solution.py:65
  87.4 5.3 %copy-start.9 = (s32[24,1,2]{0,2,1:T(2,128)S(1)}, s32[24,1,2]{0,2,1:T(2,128)}, u32[]{:S(2)}) copy-start(s32[24,1,2]{0,2,1:T(2,128)} %param.9) | copy-start | bytes 580
  87.4 5.3 %copy-start.10 = (s32[24,1]{0,1:T(1,128)S(1)}, s32[24,1]{0,1:T(1,128)}, u32[]{:S(2)}) copy-start(s32[24,1]{0,1:T(1,128)} %param.6) | copy-start | bytes 292
  87.4 5.6 %copy-start.8 = (bf16[24,1,128,128]{3,2,1,0:T(8,128)(2,1)S(1)}, bf16[24,1,128,128]{3,2,1,0:T(8,128)(2,1)}, u32[]{:S(2)}) copy-start(bf16[24,1,128,128]{3,2,1,0:T(8,128)(2,1)} %param.7) | copy-start | bytes 2359300
  93.0 19.1 %collective-permute-start.5 = (bf16[24,128,128]{2,1,0:T(8,128)(2,1)S(1)}, bf16[24,128,128]{2,1,0:T(8,128)(2,1)}, u32[]{:S(2)}, u32[]{:S(2)}) collective-permute-start(bf16[24,128,128]{2,1,0:T(8,128)(2,1)S(1)} %bitcast.69), channel_id=1, source_target_pairs={{0,192},{32,224},{64,0},{96,32},{128,64},{160,96},{192,128},{224,1... | collective-permute-start | bytes 2359304 | tf_op jit(solution)/shard_map/ppermute | solution.py:65
  97.2 24.6 %collective-permute-start.6 = (bf16[24,128,128]{2,1,0:T(8,128)(2,1)S(1)}, bf16[24,128,128]{2,1,0:T(8,128)(2,1)S(1)}, u32[]{:S(2)}, u32[]{:S(2)}) collective-permute-start(bf16[24,128,128]{2,1,0:T(8,128)(2,1)S(1)} %bitcast.70), channel_id=1, source_target_pairs={{0,224},{32,0},{64,32},{96,64},{128,96},{160,128},{192,160},{224,1... | collective-permute-start | bytes 2359304 | tf_op jit(solution)/shard_map/ppermute | solution.py:65
  123.4 2.8 copy-start
  126.3 2.8 copy-start.5
  188.8 2.8 copy-start.1
  191.6 2.8 copy-start.6
  276.6 2.8 copy-start.2
  279.4 2.8 copy-start.7
  364.2 2.8 copy-start.3
  367.0 2.8 copy-start.4
Sparse Core Ops, SparseCore 0:
  9.9 91.1 all-gather.10
  103.7 85.1 all-gather.12
  191.4 85.1 all-gather.14
  279.0 85.1 all-gather.16

commit v5 on v4

--- a/solution.py
+++ b/solution.py
@@ -6,7 +6,7 @@
 from jax.sharding import PartitionSpec as P
 
 
-CHUNKS = 4
+CHUNKS = 1
 
 
 def _row_kernel(i0_ref, i1_ref, own_ref, y_ref, self_ref, lookup_ref, out_ref, lhs_ref, stk_ref):

time: 385 us -> 237 us (0.62)
  waiting for transfers between devices: 216 us -> 92.2 us
  local copies, waits for them, and re-layouts: 52.4 us -> 26.6 us
    all_gather x4 -> x1, waiting for transfers between devices: 204 us -> 76.2 us  [shards(): lax.all_gather(y_blocks[rows, 0], ('cols', 'layers'), axis=0, tiled=False)]
    unnamed x36 -> x25, local copies, waits for them, and re-layouts: 41.2 us -> 19.3 us
    ppermute x7, waiting for transfers between devices: 10.9 us -> 15.2 us  [shards(): lax.ppermute(prod_blocks[:, 0], 'rows', [(r, (r + s) % groups) for r in r...]
    pallas_call x4 -> x1, Pallas kernels: 27.1 us -> 29.3 us  [_rows_product(): pl.pallas_call(_row_kernel, out_shape=jax.ShapeDtypeStruct((block_rows, o...]
  transfers between devices with their start and end apart: 11 -> 8, of which waited for: 5 -> 3; matrix products, arithmetic and copies ran while one was open for 7% -> 10% of each run, Pallas kernels for 5% -> 0%
where the time goes in v5:
time: 237 us; the launch traced here: 236 us
  waiting for transfers between devices  92.2 us (39%)
  blocking collectives  58.3 us (25%)
  Pallas kernels  29.3 us (12%)
  local copies, waits for them, and re-layouts  26.6 us (11%)
  between operations  14.8 us (6%)
  starting transfers between devices  14.3 us (6%)
    all_gather x1, waiting for transfers between devices, shards(): lax.all_gather(y_blocks[rows, 0], ('cols', 'layers'), axis=0, tiled=False)  76.2 us
    all_gather x1, blocking collectives, shards(): lookup_cols = lax.all_gather(prod_cols[:, 0], 'rows', axis=0, tiled=True)  39.7 us
    pallas_call x1, Pallas kernels, _rows_product(): pl.pallas_call(_row_kernel, out_shape=jax.ShapeDtypeStruct((block_rows, o...  29.3 us
    unnamed x25, local copies, waits for them, and re-layouts  19.3 us
    unnamed x1, blocking collectives  18.6 us
    ppermute x7, waiting for transfers between devices, shards(): lax.ppermute(prod_blocks[:, 0], 'rows', [(r, (r + s) % groups) for r in r...  15.2 us
    ppermute x7, starting transfers between devices, shards(): lax.ppermute(prod_blocks[:, 0], 'rows', [(r, (r + s) % groups) for r in r...  14.3 us
    gather x3, local copies, waits for them, and re-layouts, shards(): right_cols = lookup_cols[left_cols]  5.13 us
  transfers between devices with their start and end apart: 8, of which 3 were waited for; matrix products, arithmetic and copies ran while one was open for 10% of the time, Pallas kernels for 0%

profile of v5, /device:TPU:1, one launch (start us, length us, event | category | flops | bytes accessed | tf_op | source)
XLA Modules:
  0.0 235.5 jit_solution(4692058285793274169)
XLA Ops:
  6.5 0.0 all-gather.5.cloned.1.call-start
  6.5 0.7 all-gather.5.cloned.1.call-update
  7.3 2.7 %collective-permute-start = (bf16[24,128,128]{2,1,0:T(8,128)(2,1)}, bf16[24,128,128]{2,1,0:T(8,128)(2,1)}, u32[]{:S(2)}, u32[]{:S(2)}) collective-permute-start(bf16[24,128,128]{2,1,0:T(8,128)(2,1)} %bitcast.42), channel_id=1, source_target_pairs={{0,32},{32,64},{64,96},{96,128},{128,160},{160,192},{192,224},{224... | collective-permute-start | bytes 2359304 | tf_op jit(solution)/shard_map/ppermute | solution.py:65
  9.9 1.3 collective-permute-start.1
  11.2 1.7 collective-permute-start.2
  12.9 1.3 collective-permute-start.3
  14.2 2.6 %collective-permute-start.4 = (bf16[24,128,128]{2,1,0:T(8,128)(2,1)}, bf16[24,128,128]{2,1,0:T(8,128)(2,1)S(1)}, u32[]{:S(2)}, u32[]{:S(2)}) collective-permute-start(bf16[24,128,128]{2,1,0:T(8,128)(2,1)} %bitcast.46), channel_id=1, source_target_pairs={{0,160},{32,192},{64,224},{96,0},{128,32},{160,64},{192,96},{224,1... | collective-permute-start | bytes 2359304 | tf_op jit(solution)/shard_map/ppermute | solution.py:65
  16.8 1.3 dynamic-slice.1
  18.8 0.8 bitcast_dynamic-update-slice_fusion.1
  19.5 18.6 %all-reduce.1 = s32[768]{0:T(1024)S(1)} all-reduce(s32[768]{0:T(1024)S(1)} %bitcast_dynamic-update-slice_fusion.1), channel_id=3, replica_groups=mesh['rows'=8,'cols'=8,'layers'=4] {'cols','layers'}, use_global_device_ids=true, to_apply=%add.1 | all-reduce | flops 768 | bytes 6144
  38.2 0.1 reshape.22
  38.3 0.1 copy.15
  38.3 0.1 reshape.15
  38.4 1.3 dynamic-slice
  40.3 0.8 bitcast_dynamic-update-slice_fusion
  41.1 39.7 %all-reduce = s32[192]{0:T(256)S(1)} all-reduce(s32[192]{0:T(256)S(1)} %bitcast_dynamic-update-slice_fusion), channel_id=2, replica_groups=mesh['rows'=8,'cols'=8,'layers'=4] {'rows'}, use_global_device_ids=true, to_apply=%add | all-reduce | flops 192 | bytes 1536 | tf_op jit(solution)/shard_map/all_gather | solution.py:69
  80.8 2.2 constant_dynamic-update-slice_fusion.8
  82.9 0.8 slice_bitcast_fusion
  83.7 0.0 copy-start.3
  83.7 0.0 copy-start.4
  83.7 0.0 copy-start.2
  83.7 5.0 %gather_fusion = s32[768]{0:T(1024)S(1)} fusion(s32[192]{0:T(256)S(1)} %all-reduce, s32[1024]{0:T(1024)S(1)} %pad_clamp_fusion), kind=kCustom, calls=%fused_computation | custom fusion | bytes 9216 | tf_op jit(solution)/shard_map/gather | solution.py:72
  88.7 0.0 copy-start.1
  88.7 0.1 reshape.14
  88.8 0.1 copy.16
  88.9 0.0 copy-done.3
  88.9 0.1 copy.20
  89.0 0.1 copy.17
  89.1 0.1 reshape.11.i0_ref
  89.2 0.1 copy.19
  89.2 0.1 reshape.12.i1_ref
  89.3 0.0 copy-done.4
  89.3 0.1 eq.43
  89.4 0.1 eq.44
  89.5 0.1 squeeze.9
  89.6 0.0 collective-permute-done
  89.6 0.0 copy-done.2
  89.6 2.5 %collective-permute-start.5 = (bf16[24,128,128]{2,1,0:T(8,128)(2,1)S(1)}, bf16[24,128,128]{2,1,0:T(8,128)(2,1)S(1)}, u32[]{:S(2)}, u32[]{:S(2)}) collective-permute-start(bf16[24,128,128]{2,1,0:T(8,128)(2,1)S(1)} %bitcast.47), channel_id=1, source_target_pairs={{0,192},{32,224},{64,0},{96,32},{128,64},{160,96},{192,128},{224,1... | collective-permute-start | bytes 2359304 | tf_op jit(solution)/shard_map/ppermute | solution.py:65
  92.1 0.0 collective-permute-done.1
  92.1 2.2 collective-permute-start.6
  94.3 2.1 constant_dynamic-update-slice_fusion.7
  96.4 2.1 constant_dynamic-update-slice_fusion.6
  98.5 0.0 collective-permute-done.2
  98.5 2.1 constant_dynamic-update-slice_fusion.5
  100.6 0.0 collective-permute-done.3
  100.6 1.0 constant_dynamic-update-slice_fusion.4
  101.6 0.0 collective-permute-done.4
  101.6 1.0 constant_dynamic-update-slice_fusion.3
  102.6 6.1 %collective-permute-done.5 = bf16[24,128,128]{2,1,0:T(8,128)(2,1)S(1)} collective-permute-done((bf16[24,128,128]{2,1,0:T(8,128)(2,1)S(1)}, bf16[24,128,128]{2,1,0:T(8,128)(2,1)S(1)}, u32[]{:S(2)}, u32[]{:S(2)}) %collective-permute-start.5) | collective-permute-done | bytes 786464 | tf_op jit(solution)/shard_map/ppermute | solution.py:65
  108.7 1.0 constant_dynamic-update-slice_fusion.2
  109.7 9.1 %collective-permute-done.6 = bf16[24,128,128]{2,1,0:T(8,128)(2,1)S(1)} collective-permute-done((bf16[24,128,128]{2,1,0:T(8,128)(2,1)S(1)}, bf16[24,128,128]{2,1,0:T(8,128)(2,1)S(1)}, u32[]{:S(2)}, u32[]{:S(2)}) %collective-permute-start.6) | collective-permute-done | bytes 786464 | tf_op jit(solution)/shard_map/ppermute | solution.py:65
  118.8 0.9 constant_dynamic-update-slice_fusion.1
  119.8 0.6 constant_dynamic-update-slice_fusion.lookup_ref
  120.4 76.2 %all-gather.5.cloned.1.call-done = bf16[768,1,128,128]{3,2,1,0:T(8,128)(2,1)} async-done(((bf16[24,1,128,128]{3,2,1,0:T(8,128)(2,1)}), bf16[768,1,128,128]{3,2,1,0:T(8,128)(2,1)}) %all-gather.5.cloned.1.call-update) | async-done | bytes 25165840 | tf_op jit(solution)/shard_map/all_gather | solution.py:83
  196.6 0.0 copy-done.1
  196.6 0.0 copy-start
  196.6 2.8 %copy-done = bf16[193,128,128]{2,1,0:T(8,128)(2,1)S(1)} copy-done((bf16[193,128,128]{2,1,0:T(8,128)(2,1)S(1)}, bf16[193,128,128]{2,1,0:T(8,128)(2,1)}, u32[]{:S(2)}) %copy-start) | copy-done | bytes 6324248
  199.4 29.3 %shard_map.55 = bf16[24,2,128,128]{3,2,1,0:T(8,128)(2,1)} custom-call(s32[768]{0:T(1024)S(1)} %reshape.11.i0_ref, s32[768]{0:T(1024)S(1)} %reshape.12.i1_ref, s32[48]{0:T(128)S(1)} %compare_convert_fusion.own_ref, bf16[32,24,128,128]{3,2,1,0:T(8,128)(2,1)} %bitcast.41, bf16[24,128,128]{2,1,0:T(8,128)(2,1)S(1)} %bitcast.40, bf16[193,128,128]{2,1,0:T(8,128)(2,1)S(1)} %copy-done), custom_call_target="tpu_custom_call" | custom-call | tf_op jit(solution)/shard_map/pallas_call | solution.py:32
  (6 shorter events, 0.1 us)
Async XLA Ops:
  6.5 190.1 %all-gather.5.cloned.1.call-start = ((), (), s32[]{:S(2)}) async-start(), calls=%async_computation | async-start | bytes 25952256 | tf_op jit(solution)/shard_map/all_gather | solution.py:83
  7.3 82.3 %collective-permute-start = (bf16[24,128,128]{2,1,0:T(8,128)(2,1)}, bf16[24,128,128]{2,1,0:T(8,128)(2,1)}, u32[]{:S(2)}, u32[]{:S(2)}) collective-permute-start(bf16[24,128,128]{2,1,0:T(8,128)(2,1)} %bitcast.42), channel_id=1, source_target_pairs={{0,32},{32,64},{64,96},{96,128},{128,160},{160,192},{192,224},{224... | collective-permute-start | bytes 2359304 | tf_op jit(solution)/shard_map/ppermute | solution.py:65
  9.9 82.2 %collective-permute-start.1 = (bf16[24,128,128]{2,1,0:T(8,128)(2,1)}, bf16[24,128,128]{2,1,0:T(8,128)(2,1)}, u32[]{:S(2)}, u32[]{:S(2)}) collective-permute-start(bf16[24,128,128]{2,1,0:T(8,128)(2,1)} %bitcast.43), channel_id=1, source_target_pairs={{0,64},{32,96},{64,128},{96,160},{128,192},{160,224},{192,0},{224,... | collective-permute-start | bytes 2359304 | tf_op jit(solution)/shard_map/ppermute | solution.py:65
  11.2 87.3 %collective-permute-start.2 = (bf16[24,128,128]{2,1,0:T(8,128)(2,1)}, bf16[24,128,128]{2,1,0:T(8,128)(2,1)}, u32[]{:S(2)}, u32[]{:S(2)}) collective-permute-start(bf16[24,128,128]{2,1,0:T(8,128)(2,1)} %bitcast.44), channel_id=1, source_target_pairs={{0,96},{32,128},{64,160},{96,192},{128,224},{160,0},{192,32},{224,... | collective-permute-start | bytes 2359304 | tf_op jit(solution)/shard_map/ppermute | solution.py:65
  12.9 87.7 %collective-permute-start.3 = (bf16[24,128,128]{2,1,0:T(8,128)(2,1)}, bf16[24,128,128]{2,1,0:T(8,128)(2,1)S(1)}, u32[]{:S(2)}, u32[]{:S(2)}) collective-permute-start(bf16[24,128,128]{2,1,0:T(8,128)(2,1)} %bitcast.45), channel_id=1, source_target_pairs={{0,128},{32,160},{64,192},{96,224},{128,0},{160,32},{192,64},{224,... | collective-permute-start | bytes 2359304 | tf_op jit(solution)/shard_map/ppermute | solution.py:65
  14.2 87.4 %collective-permute-start.4 = (bf16[24,128,128]{2,1,0:T(8,128)(2,1)}, bf16[24,128,128]{2,1,0:T(8,128)(2,1)S(1)}, u32[]{:S(2)}, u32[]{:S(2)}) collective-permute-start(bf16[24,128,128]{2,1,0:T(8,128)(2,1)} %bitcast.46), channel_id=1, source_target_pairs={{0,160},{32,192},{64,224},{96,0},{128,32},{160,64},{192,96},{224,1... | collective-permute-start | bytes 2359304 | tf_op jit(solution)/shard_map/ppermute | solution.py:65
  83.7 5.2 %copy-start.3 = (s32[24,1,2]{0,2,1:T(2,128)S(1)}, s32[24,1,2]{0,2,1:T(2,128)}, u32[]{:S(2)}) copy-start(s32[24,1,2]{0,2,1:T(2,128)} %param.9) | copy-start | bytes 580
  83.7 5.6 %copy-start.4 = (s32[24,1]{0,1:T(1,128)S(1)}, s32[24,1]{0,1:T(1,128)}, u32[]{:S(2)}) copy-start(s32[24,1]{0,1:T(1,128)} %param.6) | copy-start | bytes 292
  83.7 5.9 %copy-start.2 = (bf16[24,1,128,128]{3,2,1,0:T(8,128)(2,1)S(1)}, bf16[24,1,128,128]{3,2,1,0:T(8,128)(2,1)}, u32[]{:S(2)}) copy-start(bf16[24,1,128,128]{3,2,1,0:T(8,128)(2,1)} %param.7) | copy-start | bytes 2359300
  88.7 107.9 %copy-start.1 = (bf16[24,1,128,128]{3,2,1,0:T(8,128)(2,1)S(1)}, bf16[24,1,128,128]{3,2,1,0:T(8,128)(2,1)}, u32[]{:S(2)}) copy-start(bf16[24,1,128,128]{3,2,1,0:T(8,128)(2,1)} %param.5) | copy-start | bytes 2359300
  89.6 19.1 %collective-permute-start.5 = (bf16[24,128,128]{2,1,0:T(8,128)(2,1)S(1)}, bf16[24,128,128]{2,1,0:T(8,128)(2,1)S(1)}, u32[]{:S(2)}, u32[]{:S(2)}) collective-permute-start(bf16[24,128,128]{2,1,0:T(8,128)(2,1)S(1)} %bitcast.47), channel_id=1, source_target_pairs={{0,192},{32,224},{64,0},{96,32},{128,64},{160,96},{192,128},{224,1... | collective-permute-start | bytes 2359304 | tf_op jit(solution)/shard_map/ppermute | solution.py:65
  92.1 26.7 %collective-permute-start.6 = (bf16[24,128,128]{2,1,0:T(8,128)(2,1)S(1)}, bf16[24,128,128]{2,1,0:T(8,128)(2,1)S(1)}, u32[]{:S(2)}, u32[]{:S(2)}) collective-permute-start(bf16[24,128,128]{2,1,0:T(8,128)(2,1)S(1)} %bitcast.48), channel_id=1, source_target_pairs={{0,224},{32,0},{64,32},{96,64},{128,96},{160,128},{192,160},{224,1... | collective-permute-start | bytes 2359304 | tf_op jit(solution)/shard_map/ppermute | solution.py:65
  196.6 2.8 %copy-start = (bf16[193,128,128]{2,1,0:T(8,128)(2,1)S(1)}, bf16[193,128,128]{2,1,0:T(8,128)(2,1)}, u32[]{:S(2)}) copy-start(bf16[193,128,128]{2,1,0:T(8,128)(2,1)} %constant_dynamic-update-slice_fusion.lookup_ref) | copy-start | bytes 18972676
Sparse Core Ops, SparseCore 0:
  9.9 186.6 all-gather.4

commit v6 on v5

v6 whole, which is shorter than its diff:
```python
import jax
import jax.numpy as jnp
from jax import lax
from jax.experimental import pallas as pl
from jax.experimental.pallas import tpu as pltpu
from jax.sharding import PartitionSpec as P


def _stack_kernel(krow_ref, lookup_ref, out_ref):
    i = pl.program_id(0)
    tiles = out_ref.shape[1] // out_ref.shape[2]
    bs = out_ref.shape[2]
    for tp in range(tiles):
        out_ref[0, tp * bs:(tp + 1) * bs, :] = lookup_ref[krow_ref[i * tiles + tp]]


def _stack_rows(krow, lookup, block_rows, tiles):
    nb, bs, _ = lookup.shape
    return pl.pallas_call(
        _stack_kernel,
        out_shape=jax.ShapeDtypeStruct((block_rows, tiles * bs, bs), lookup.dtype),
        grid_spec=pltpu.PrefetchScalarGridSpec(
            num_scalar_prefetch=1,
            grid=(block_rows,),
            in_specs=[pl.BlockSpec((nb, bs, bs), lambda i, *_: (0, 0, 0))],
            out_specs=pl.BlockSpec((1, tiles * bs, bs), lambda i, *_: (i, 0, 0)),
        ),
        compiler_params=pltpu.CompilerParams(
            dimension_semantics=("arbitrary",),
            vmem_limit_bytes=40 * 1024 * 1024,
        ),
    )(krow, lookup)


def _row_kernel(m0_ref, m1_ref, own_ref, y_ref, self_ref, stk_ref, out_ref, lhs_ref):
    i = pl.program_id(0)
    tiles = y_ref.shape[0]
    bs = y_ref.shape[-1]
    for tp in range(tiles):
        at = i * tiles + tp
        cols = slice(tp * bs, (tp + 1) * bs)
        y = y_ref[tp, 0]
        zero = jnp.zeros_like(y)
        lhs_ref[0:bs, cols] = jnp.where(m0_ref[at] != 0, y, zero)
        lhs_ref[bs:2 * bs, cols] = jnp.where(m1_ref[at] != 0, y, zero)
    res = jnp.dot(lhs_ref[...], stk_ref[0], preferred_element_type=jnp.float32)
    own = self_ref[0].astype(jnp.float32)
    for w in range(2):
        own_w = jnp.where(own_ref[2 * i + w] != 0, own, 0.0)
        out_ref[0, w] = (1.5 * own_w - 0.5 * res[w * bs:(w + 1) * bs]).astype(out_ref.dtype)


def _rows_product(m0, m1, own, left, own_blocks, stacked, out_width):
    tiles, block_rows, block_size, _ = left.shape
    return pl.pallas_call(
        _row_kernel,
        out_shape=jax.ShapeDtypeStruct((block_rows, out_width, block_size, block_size), jnp.bfloat16),
        grid_spec=pltpu.PrefetchScalarGridSpec(
            num_scalar_prefetch=3,
            grid=(block_rows,),
            in_specs=[
                pl.BlockSpec((tiles, 1, block_size, block_size), lambda i, *_: (0, i, 0, 0)),
                pl.BlockSpec((1, block_size, block_size), lambda i, *_: (i, 0, 0)),
                pl.BlockSpec((1, tiles * block_size, block_size), lambda i, *_: (i, 0, 0)),
            ],
            out_specs=pl.BlockSpec((1, out_width, block_size, block_size), lambda i, *_: (i, 0, 0, 0)),
            scratch_shapes=[
                pltpu.VMEM((out_width * block_size, tiles * block_size), jnp.bfloat16),
            ],
        ),
        compiler_params=pltpu.CompilerParams(
            dimension_semantics=("arbitrary",),
            vmem_limit_bytes=40 * 1024 * 1024,
        ),
    )(m0, m1, own, left, own_blocks, stacked)


def shards(y_blocks, y_cols, prod_blocks, prod_cols, out_cols):
    block_rows = y_blocks.shape[0]
    block_size = y_blocks.shape[2]
    out_width = out_cols.shape[2]

    groups = lax.axis_size("rows")
    me = lax.axis_index("rows")
    pieces = [prod_blocks[:, 0]]
    for s in range(1, groups):
        pieces.append(lax.ppermute(prod_blocks[:, 0], "rows", [(r, (r + s) % groups) for r in range(groups)]))
    lookup = jnp.concatenate(pieces, axis=0)
    lookup_cols = lax.all_gather(prod_cols[:, 0], "rows", axis=0, tiled=True)
    left_cols = lax.all_gather(y_cols[:, 0], ("cols", "layers"), axis=0, tiled=False).T

    right_cols = lookup_cols[left_cols]
    owner = left_cols // block_rows
    krow = ((me - owner) % groups) * block_rows + left_cols % block_rows
    m0 = (right_cols == out_cols[:, 0, 0][:, None]).astype(jnp.int32)
    m1 = (right_cols == out_cols[:, 0, 1][:, None]).astype(jnp.int32)
    own = (out_cols[:, 0, :] == y_cols[:, 0][:, None]).astype(jnp.int32)

    tiles = left_cols.shape[1]
    stacked = _stack_rows(krow.reshape(-1).astype(jnp.int32), lookup, block_rows, tiles)

    left = lax.all_gather(y_blocks[:, 0], ("cols", "layers"), axis=0, tiled=False)
    out = _rows_product(m0.reshape(-1), m1.reshape(-1), own.reshape(-1), left, y_blocks[:, 0], stacked, out_width)
    return out[:, None]


def solution(mesh):
    placed = (
        P("rows", ("cols", "layers"), None, None),
        P("rows", ("cols", "layers")),
        P("rows", ("cols", "layers"), None, None),
        P("rows", ("cols", "layers")),
        P("rows", ("cols", "layers"), None),
    )
    return jax.shard_map(
        shards,
        mesh=mesh,
        in_specs=placed,
        out_specs=P("rows", ("cols", "layers"), None, None, None),
        check_vma=False,
    )
```

time: 237 us -> 236 us (level)
  Pallas kernels: 29.3 us -> 45.5 us
  waiting for transfers between devices: 92.2 us -> 78 us
    all_gather x1, waiting for transfers between devices: 76.2 us -> 62.1 us  [shards(): lax.all_gather(y_blocks[:, 0], ('cols', 'layers'), axis=0, tiled=False)]
    pallas_call x0 -> x1, Pallas kernels: none -> 13.9 us  [_stack_rows(): pl.pallas_call(_stack_kernel, out_shape=jax.ShapeDtypeStruct((block_rows,...]
    pallas_call x1, Pallas kernels: 29.3 us -> 31.7 us  [_rows_product(): pl.pallas_call(_row_kernel, out_shape=jax.ShapeDtypeStruct((block_rows, o...]
    unnamed x25 -> x24, local copies, waits for them, and re-layouts: 19.3 us -> 18.5 us
    gather x3 -> x2, local copies, waits for them, and re-layouts: 5.13 us -> 5.05 us  [shards(): right_cols = lookup_cols[left_cols]]
  transfers between devices with their start and end apart: 8 -> 8, of which waited for: 3 -> 3; matrix products, arithmetic and copies ran while one was open for 10% -> 10% of each run, Pallas kernels for 0% -> 6%
where the time goes in v6:
time: 236 us; the launch traced here: 235 us
  waiting for transfers between devices  78 us (33%)
  blocking collectives  56.3 us (24%)
  Pallas kernels  45.5 us (19%)
  local copies, waits for them, and re-layouts  26.1 us (11%)
  between operations  14.8 us (6%)
  starting transfers between devices  14.3 us (6%)
    all_gather x1, waiting for transfers between devices, shards(): lax.all_gather(y_blocks[:, 0], ('cols', 'layers'), axis=0, tiled=False)  62.1 us
    all_gather x1, blocking collectives, shards(): lookup_cols = lax.all_gather(prod_cols[:, 0], 'rows', axis=0, tiled=True)  37.6 us
    pallas_call x1, Pallas kernels, _rows_product(): pl.pallas_call(_row_kernel, out_shape=jax.ShapeDtypeStruct((block_rows, o...  31.7 us
    unnamed x1, blocking collectives  18.6 us
    unnamed x24, local copies, waits for them, and re-layouts  18.5 us
    ppermute x7, waiting for transfers between devices, shards(): lax.ppermute(prod_blocks[:, 0], 'rows', [(r, (r + s) % groups) for r in r...  15.2 us
    ppermute x7, starting transfers between devices, shards(): lax.ppermute(prod_blocks[:, 0], 'rows', [(r, (r + s) % groups) for r in r...  14.3 us
    pallas_call x1, Pallas kernels, _stack_rows(): pl.pallas_call(_stack_kernel, out_shape=jax.ShapeDtypeStruct((block_rows,...  13.9 us
  transfers between devices with their start and end apart: 8, of which 3 were waited for; matrix products, arithmetic and copies ran while one was open for 10% of the time, Pallas kernels for 6%

profile of v6, /device:TPU:1, one launch (start us, length us, event | category | flops | bytes accessed | tf_op | source)
XLA Modules:
  0.0 235.1 jit_solution(10304632911789345478)
XLA Ops:
  6.5 0.0 all-gather.5.cloned.1.call-start
  6.5 0.7 all-gather.5.cloned.1.call-update
  7.3 2.7 %collective-permute-start = (bf16[24,128,128]{2,1,0:T(8,128)(2,1)}, bf16[24,128,128]{2,1,0:T(8,128)(2,1)}, u32[]{:S(2)}, u32[]{:S(2)}) collective-permute-start(bf16[24,128,128]{2,1,0:T(8,128)(2,1)} %bitcast.38), channel_id=1, source_target_pairs={{0,32},{32,64},{64,96},{96,128},{128,160},{160,192},{192,224},{224... | collective-permute-start | bytes 2359304 | tf_op jit(solution)/shard_map/ppermute | solution.py:87
  9.9 1.3 collective-permute-start.1
  11.2 1.7 collective-permute-start.2
  12.9 1.3 collective-permute-start.3
  14.2 2.6 %collective-permute-start.4 = (bf16[24,128,128]{2,1,0:T(8,128)(2,1)}, bf16[24,128,128]{2,1,0:T(8,128)(2,1)S(1)}, u32[]{:S(2)}, u32[]{:S(2)}) collective-permute-start(bf16[24,128,128]{2,1,0:T(8,128)(2,1)} %bitcast.42), channel_id=1, source_target_pairs={{0,160},{32,192},{64,224},{96,0},{128,32},{160,64},{192,96},{224,1... | collective-permute-start | bytes 2359304 | tf_op jit(solution)/shard_map/ppermute | solution.py:87
  16.8 1.3 dynamic-slice.1
  18.8 0.8 bitcast_dynamic-update-slice_fusion.1
  19.5 18.6 %all-reduce.1 = s32[768]{0:T(1024)S(1)} all-reduce(s32[768]{0:T(1024)S(1)} %bitcast_dynamic-update-slice_fusion.1), channel_id=3, replica_groups=mesh['rows'=8,'cols'=8,'layers'=4] {'cols','layers'}, use_global_device_ids=true, to_apply=%add.1 | all-reduce | flops 768 | bytes 6144
  38.2 0.1 reshape.32
  38.3 1.3 dynamic-slice
  40.2 2.2 constant_dynamic-update-slice_fusion.7
  42.4 0.7 bitcast_dynamic-update-slice_fusion
  43.1 37.6 %all-reduce = s32[192]{0:T(256)S(1)} all-reduce(s32[192]{0:T(256)S(1)} %bitcast_dynamic-update-slice_fusion), channel_id=2, replica_groups=mesh['rows'=8,'cols'=8,'layers'=4] {'rows'}, use_global_device_ids=true, to_apply=%add | all-reduce | flops 192 | bytes 1536 | tf_op jit(solution)/shard_map/all_gather | solution.py:89
  80.8 0.1 copy.12
  80.8 0.1 reshape.25
  80.9 0.8 slice_bitcast_fusion
  81.7 0.0 copy-start.3
  81.7 0.0 copy-start.4
  81.7 0.0 copy-start.2
  81.7 5.0 %gather_fusion = s32[768]{0:T(1024)S(1)} fusion(s32[192]{0:T(256)S(1)} %all-reduce, s32[1024]{0:T(1024)S(1)} %pad_clamp_fusion), kind=kCustom, calls=%fused_computation | custom fusion | bytes 9216 | tf_op jit(solution)/shard_map/gather | solution.py:92
  86.7 0.1 reshape.24
  86.8 0.1 compare_convert_fusion
  86.8 0.0 copy-done.3
  86.8 0.1 copy.13
  86.9 0.1 copy.14
  87.0 0.1 reshape.20.krow_ref
  87.1 0.1 reshape.21.m0_ref
  87.1 0.1 reshape.22.m1_ref
  87.2 0.0 copy-done.4
  87.2 0.1 eq.47
  87.3 0.1 eq.48
  87.4 0.1 squeeze.9
  87.5 0.0 collective-permute-done
  87.5 0.0 copy-done.2
  87.5 2.5 %collective-permute-start.5 = (bf16[24,128,128]{2,1,0:T(8,128)(2,1)S(1)}, bf16[24,128,128]{2,1,0:T(8,128)(2,1)S(1)}, u32[]{:S(2)}, u32[]{:S(2)}) collective-permute-start(bf16[24,128,128]{2,1,0:T(8,128)(2,1)S(1)} %bitcast.43), channel_id=1, source_target_pairs={{0,192},{32,224},{64,0},{96,32},{128,64},{160,96},{192,128},{224,1... | collective-permute-start | bytes 2359304 | tf_op jit(solution)/shard_map/ppermute | solution.py:87
  90.0 0.0 collective-permute-done.1
  90.0 2.2 collective-permute-start.6
  92.2 2.1 constant_dynamic-update-slice_fusion.6
  94.4 2.1 constant_dynamic-update-slice_fusion.5
  96.5 0.0 collective-permute-done.2
  96.5 2.1 constant_dynamic-update-slice_fusion.4
  98.6 0.0 collective-permute-done.3
  98.6 1.0 constant_dynamic-update-slice_fusion.3
  99.6 0.0 collective-permute-done.4
  99.6 1.0 constant_dynamic-update-slice_fusion.2
  100.6 6.1 %collective-permute-done.5 = bf16[24,128,128]{2,1,0:T(8,128)(2,1)S(1)} collective-permute-done((bf16[24,128,128]{2,1,0:T(8,128)(2,1)S(1)}, bf16[24,128,128]{2,1,0:T(8,128)(2,1)S(1)}, u32[]{:S(2)}, u32[]{:S(2)}) %collective-permute-start.5) | collective-permute-done | bytes 786464 | tf_op jit(solution)/shard_map/ppermute | solution.py:87
  106.7 1.0 constant_dynamic-update-slice_fusion.1
  107.6 9.1 %collective-permute-done.6 = bf16[24,128,128]{2,1,0:T(8,128)(2,1)S(1)} collective-permute-done((bf16[24,128,128]{2,1,0:T(8,128)(2,1)S(1)}, bf16[24,128,128]{2,1,0:T(8,128)(2,1)S(1)}, u32[]{:S(2)}, u32[]{:S(2)}) %collective-permute-start.6) | collective-permute-done | bytes 786464 | tf_op jit(solution)/shard_map/ppermute | solution.py:87
  116.7 0.9 constant_dynamic-update-slice_fusion.lookup_ref
  117.7 0.0 copy-start
  117.7 2.9 %copy-done = bf16[192,128,128]{2,1,0:T(8,128)(2,1)S(1)} copy-done((bf16[192,128,128]{2,1,0:T(8,128)(2,1)S(1)}, bf16[192,128,128]{2,1,0:T(8,128)(2,1)}, u32[]{:S(2)}) %copy-start) | copy-done | bytes 6291480
  120.6 0.0 copy-start.1
  120.6 13.9 %shard_map.55.stk_ref = bf16[24,4096,128]{2,1,0:T(8,128)(2,1)} custom-call(s32[768]{0:T(1024)S(1)} %reshape.20.krow_ref, bf16[192,128,128]{2,1,0:T(8,128)(2,1)S(1)} %copy-done), custom_call_target="tpu_custom_call" | custom-call | tf_op jit(solution)/shard_map/pallas_call | solution.py:19
  134.5 62.1 %all-gather.5.cloned.1.call-done = bf16[768,1,128,128]{3,2,1,0:T(8,128)(2,1)} async-done(((bf16[24,1,128,128]{3,2,1,0:T(8,128)(2,1)}), bf16[768,1,128,128]{3,2,1,0:T(8,128)(2,1)}) %all-gather.5.cloned.1.call-update) | async-done | bytes 25165840 | tf_op jit(solution)/shard_map/all_gather | solution.py:102
  196.6 0.0 copy-done.1
  196.6 31.7 %shard_map.56 = bf16[24,2,128,128]{3,2,1,0:T(8,128)(2,1)} custom-call(s32[768]{0:T(1024)S(1)} %reshape.21.m0_ref, s32[768]{0:T(1024)S(1)} %reshape.22.m1_ref, s32[48]{0:T(128)S(1)} %compare_convert_fusion.2.own_ref, bf16[32,24,128,128]{3,2,1,0:T(8,128)(2,1)} %bitcast.37, bf16[24,128,128]{2,1,0:T(8,128)(2,1)S(1)} %bitcast.36, ...), custom_call_target="tpu_custom_call" | custom-call | tf_op jit(solution)/shard_map/pallas_call | solution.py:55
  (5 shorter events, 0.0 us)
Async XLA Ops:
  6.5 190.1 %all-gather.5.cloned.1.call-start = ((), (), s32[]{:S(2)}) async-start(), calls=%async_computation | async-start | bytes 25952256 | tf_op jit(solution)/shard_map/all_gather | solution.py:102
  7.3 80.2 %collective-permute-start = (bf16[24,128,128]{2,1,0:T(8,128)(2,1)}, bf16[24,128,128]{2,1,0:T(8,128)(2,1)}, u32[]{:S(2)}, u32[]{:S(2)}) collective-permute-start(bf16[24,128,128]{2,1,0:T(8,128)(2,1)} %bitcast.38), channel_id=1, source_target_pairs={{0,32},{32,64},{64,96},{96,128},{128,160},{160,192},{192,224},{224... | collective-permute-start | bytes 2359304 | tf_op jit(solution)/shard_map/ppermute | solution.py:87
  9.9 80.1 %collective-permute-start.1 = (bf16[24,128,128]{2,1,0:T(8,128)(2,1)}, bf16[24,128,128]{2,1,0:T(8,128)(2,1)}, u32[]{:S(2)}, u32[]{:S(2)}) collective-permute-start(bf16[24,128,128]{2,1,0:T(8,128)(2,1)} %bitcast.39), channel_id=1, source_target_pairs={{0,64},{32,96},{64,128},{96,160},{128,192},{160,224},{192,0},{224,... | collective-permute-start | bytes 2359304 | tf_op jit(solution)/shard_map/ppermute | solution.py:87
  11.2 85.3 %collective-permute-start.2 = (bf16[24,128,128]{2,1,0:T(8,128)(2,1)}, bf16[24,128,128]{2,1,0:T(8,128)(2,1)}, u32[]{:S(2)}, u32[]{:S(2)}) collective-permute-start(bf16[24,128,128]{2,1,0:T(8,128)(2,1)} %bitcast.40), channel_id=1, source_target_pairs={{0,96},{32,128},{64,160},{96,192},{128,224},{160,0},{192,32},{224,... | collective-permute-start | bytes 2359304 | tf_op jit(solution)/shard_map/ppermute | solution.py:87
  12.9 85.7 %collective-permute-start.3 = (bf16[24,128,128]{2,1,0:T(8,128)(2,1)}, bf16[24,128,128]{2,1,0:T(8,128)(2,1)S(1)}, u32[]{:S(2)}, u32[]{:S(2)}) collective-permute-start(bf16[24,128,128]{2,1,0:T(8,128)(2,1)} %bitcast.41), channel_id=1, source_target_pairs={{0,128},{32,160},{64,192},{96,224},{128,0},{160,32},{192,64},{224,... | collective-permute-start | bytes 2359304 | tf_op jit(solution)/shard_map/ppermute | solution.py:87
  14.2 85.4 %collective-permute-start.4 = (bf16[24,128,128]{2,1,0:T(8,128)(2,1)}, bf16[24,128,128]{2,1,0:T(8,128)(2,1)S(1)}, u32[]{:S(2)}, u32[]{:S(2)}) collective-permute-start(bf16[24,128,128]{2,1,0:T(8,128)(2,1)} %bitcast.42), channel_id=1, source_target_pairs={{0,160},{32,192},{64,224},{96,0},{128,32},{160,64},{192,96},{224,1... | collective-permute-start | bytes 2359304 | tf_op jit(solution)/shard_map/ppermute | solution.py:87
  81.7 5.2 %copy-start.3 = (s32[24,1,2]{0,2,1:T(2,128)S(1)}, s32[24,1,2]{0,2,1:T(2,128)}, u32[]{:S(2)}) copy-start(s32[24,1,2]{0,2,1:T(2,128)} %param.9) | copy-start | bytes 580
  81.7 5.5 %copy-start.4 = (s32[24,1]{0,1:T(1,128)S(1)}, s32[24,1]{0,1:T(1,128)}, u32[]{:S(2)}) copy-start(s32[24,1]{0,1:T(1,128)} %param.6) | copy-start | bytes 292
  81.7 5.8 %copy-start.2 = (bf16[24,1,128,128]{3,2,1,0:T(8,128)(2,1)S(1)}, bf16[24,1,128,128]{3,2,1,0:T(8,128)(2,1)}, u32[]{:S(2)}) copy-start(bf16[24,1,128,128]{3,2,1,0:T(8,128)(2,1)} %param.7) | copy-start | bytes 2359300
  87.5 19.1 %collective-permute-start.5 = (bf16[24,128,128]{2,1,0:T(8,128)(2,1)S(1)}, bf16[24,128,128]{2,1,0:T(8,128)(2,1)S(1)}, u32[]{:S(2)}, u32[]{:S(2)}) collective-permute-start(bf16[24,128,128]{2,1,0:T(8,128)(2,1)S(1)} %bitcast.43), channel_id=1, source_target_pairs={{0,192},{32,224},{64,0},{96,32},{128,64},{160,96},{192,128},{224,1... | collective-permute-start | bytes 2359304 | tf_op jit(solution)/shard_map/ppermute | solution.py:87
  90.0 26.7 %collective-permute-start.6 = (bf16[24,128,128]{2,1,0:T(8,128)(2,1)S(1)}, bf16[24,128,128]{2,1,0:T(8,128)(2,1)S(1)}, u32[]{:S(2)}, u32[]{:S(2)}) collective-permute-start(bf16[24,128,128]{2,1,0:T(8,128)(2,1)S(1)} %bitcast.44), channel_id=1, source_target_pairs={{0,224},{32,0},{64,32},{96,64},{128,96},{160,128},{192,160},{224,1... | collective-permute-start | bytes 2359304 | tf_op jit(solution)/shard_map/ppermute | solution.py:87
  117.7 2.9 %copy-start = (bf16[192,128,128]{2,1,0:T(8,128)(2,1)S(1)}, bf16[192,128,128]{2,1,0:T(8,128)(2,1)}, u32[]{:S(2)}) copy-start(bf16[192,128,128]{2,1,0:T(8,128)(2,1)} %constant_dynamic-update-slice_fusion.lookup_ref) | copy-start | bytes 18874372
  120.6 76.0 %copy-start.1 = (bf16[24,1,128,128]{3,2,1,0:T(8,128)(2,1)S(1)}, bf16[24,1,128,128]{3,2,1,0:T(8,128)(2,1)}, u32[]{:S(2)}) copy-start(bf16[24,1,128,128]{3,2,1,0:T(8,128)(2,1)} %param.5) | copy-start | bytes 2359300
Sparse Core Ops, SparseCore 0:
  9.9 186.6 all-gather.4

commit v7 on v5

v7 whole, which is shorter than its diff:
```python
import jax
import jax.numpy as jnp
from jax import lax
from jax.experimental import pallas as pl
from jax.experimental.pallas import tpu as pltpu
from jax.sharding import PartitionSpec as P


ROWS_PER_STEP = 4
SIDE_ROWS = 4


def _row_kernel(i0_ref, i1_ref, own_ref, y_ref, self_ref, lookup_ref, out_ref, lhs_ref, stk_ref):
    g = pl.program_id(0)
    tiles = y_ref.shape[0]
    rb = y_ref.shape[1]
    bs = y_ref.shape[-1]
    for r in range(rb):
        i = g * rb + r
        for tp in range(tiles):
            at = i * tiles + tp
            cols = slice(tp * bs, (tp + 1) * bs)
            lhs_ref[:, cols] = y_ref[tp, r]
            stk_ref[cols, 0:bs] = lookup_ref[i0_ref[at]]
            stk_ref[cols, bs:2 * bs] = lookup_ref[i1_ref[at]]
        res = jnp.dot(lhs_ref[...], stk_ref[...], preferred_element_type=jnp.float32)
        own = self_ref[r].astype(jnp.float32)
        for w in range(2):
            own_w = jnp.where(own_ref[2 * i + w] != 0, own, 0.0)
            out_ref[r, w] = (1.5 * own_w - 0.5 * res[:, w * bs:(w + 1) * bs]).astype(out_ref.dtype)


def _rows_product(i0, i1, own, left, own_blocks, lookup, out_width):
    tiles, block_rows, block_size, _ = left.shape
    nb = lookup.shape[0]
    rb = ROWS_PER_STEP if block_rows % ROWS_PER_STEP == 0 else 1
    return pl.pallas_call(
        _row_kernel,
        out_shape=jax.ShapeDtypeStruct((block_rows, out_width, block_size, block_size), jnp.bfloat16),
        grid_spec=pltpu.PrefetchScalarGridSpec(
            num_scalar_prefetch=3,
            grid=(block_rows // rb,),
            in_specs=[
                pl.BlockSpec((tiles, rb, block_size, block_size), lambda g, *_: (0, g, 0, 0)),
                pl.BlockSpec((rb, block_size, block_size), lambda g, *_: (g, 0, 0)),
                pl.BlockSpec((nb, block_size, block_size), lambda g, *_: (0, 0, 0)),
            ],
            out_specs=pl.BlockSpec((rb, out_width, block_size, block_size), lambda g, *_: (g, 0, 0, 0)),
            scratch_shapes=[
                pltpu.VMEM((block_size, tiles * block_size), jnp.bfloat16),
                pltpu.VMEM((tiles * block_size, out_width * block_size), jnp.bfloat16),
            ],
        ),
        compiler_params=pltpu.CompilerParams(
            dimension_semantics=("arbitrary",),
            vmem_limit_bytes=48 * 1024 * 1024,
        ),
    )(i0, i1, own, left, own_blocks, lookup)


def shards(y_blocks, y_cols, prod_blocks, prod_cols, out_cols):
    block_rows = y_blocks.shape[0]
    block_size = y_blocks.shape[2]
    out_width = out_cols.shape[2]

    groups = lax.axis_size("rows")
    me = lax.axis_index("rows")
    pieces = [prod_blocks[:, 0]]
    for s in range(1, groups):
        pieces.append(lax.ppermute(prod_blocks[:, 0], "rows", [(r, (r + s) % groups) for r in range(groups)]))
    pieces.append(jnp.zeros((1, block_size, block_size), prod_blocks.dtype))
    lookup = jnp.concatenate(pieces, axis=0)
    nb = groups * block_rows
    lookup_cols = lax.all_gather(prod_cols[:, 0], "rows", axis=0, tiled=True)
    left_cols = lax.all_gather(y_cols[:, 0], ("cols", "layers"), axis=0, tiled=False).T

    right_cols = lookup_cols[left_cols]
    owner = left_cols // block_rows
    krow = ((me - owner) % groups) * block_rows + left_cols % block_rows
    i0 = jnp.where(right_cols == out_cols[:, 0, 0][:, None], krow, nb).astype(jnp.int32)
    i1 = jnp.where(right_cols == out_cols[:, 0, 1][:, None], krow, nb).astype(jnp.int32)
    own = (out_cols[:, 0, :] == y_cols[:, 0][:, None]).astype(jnp.int32)

    tiles = left_cols.shape[1]
    main = block_rows - SIDE_ROWS
    side_rows = slice(main, block_rows)
    side = lax.all_to_all(
        jnp.tile(y_blocks[side_rows, 0], (tiles, 1, 1)), ("cols", "layers"), 0, 0, tiled=True)
    side = side.reshape(tiles, SIDE_ROWS, block_size, block_size)
    out_side = _rows_product(
        i0[side_rows].reshape(-1), i1[side_rows].reshape(-1), own[side_rows].reshape(-1),
        side, y_blocks[side_rows, 0], lookup, out_width)
    rows = slice(0, main)
    left = lax.all_gather(y_blocks[rows, 0], ("cols", "layers"), axis=0, tiled=False)
    out_main = _rows_product(
        i0[rows].reshape(-1), i1[rows].reshape(-1), own[rows].reshape(-1),
        left, y_blocks[rows, 0], lookup, out_width)
    return jnp.concatenate([out_main, out_side], axis=0)[:, None]


def solution(mesh):
    placed = (
        P("rows", ("cols", "layers"), None, None),
        P("rows", ("cols", "layers")),
        P("rows", ("cols", "layers"), None, None),
        P("rows", ("cols", "layers")),
        P("rows", ("cols", "layers"), None),
    )
    return jax.shard_map(
        shards,
        mesh=mesh,
        in_specs=placed,
        out_specs=P("rows", ("cols", "layers"), None, None, None),
        check_vma=False,
    )
```

time: 237 us -> 271 us (1.14)
  blocking collectives: 58.3 us -> 129 us
  waiting for transfers between devices: 92.2 us -> 47.8 us
  starting transfers between devices: 14.3 us -> 21.8 us
    unnamed x1, blocking collectives: 18.6 us -> 114 us
    all_gather x1, waiting for transfers between devices: 76.2 us -> 33.1 us  [shards(): lax.all_gather(y_blocks[rows, 0], ('cols', 'layers'), axis=0, tiled=False)]
    all_gather x1, blocking collectives: 39.7 us -> 15 us  [shards(): lookup_cols = lax.all_gather(prod_cols[:, 0], 'rows', axis=0, tiled=True)]
    all_to_all x0 -> x1, starting transfers between devices: none -> 12 us  [shards(): lax.all_to_all(jnp.tile(y_blocks[side_rows, 0], (tiles, 1, 1)), ('cols',...]
    unnamed x25 -> x26, local copies, waits for them, and re-layouts: 19.3 us -> 13.9 us
    ppermute x7, starting transfers between devices: 14.3 us -> 9.85 us  [shards(): lax.ppermute(prod_blocks[:, 0], 'rows', [(r, (r + s) % groups) for r in r...]
    another operation x0 -> x2, local copies, waits for them, and re-layouts: none -> 3.9 us  [shards(): jnp.tile(y_blocks[side_rows, 0], (tiles, 1, 1))]
    pallas_call x1 -> x2, Pallas kernels: 29.3 us -> 28.7 us  [_rows_product(): pl.pallas_call(_row_kernel, out_shape=jax.ShapeDtypeStruct((block_rows, o...]
  transfers between devices with their start and end apart: 8 -> 9, of which waited for: 3 -> 3; matrix products, arithmetic and copies ran while one was open for 10% -> 9% of each run, Pallas kernels for 0% -> 3%
where the time goes in v7:
time: 271 us
  blocking collectives  129 us (48%)
  waiting for transfers between devices  47.8 us (18%)
  Pallas kernels  28.7 us (11%)
  local copies, waits for them, and re-layouts  27.3 us (10%)
  starting transfers between devices  21.8 us (8%)
  between operations  15 us (6%)
    unnamed x1, blocking collectives  114 us
    all_gather x1, waiting for transfers between devices, shards(): lax.all_gather(y_blocks[rows, 0], ('cols', 'layers'), axis=0, tiled=False)  33.1 us
    pallas_call x2, Pallas kernels, _rows_product(): pl.pallas_call(_row_kernel, out_shape=jax.ShapeDtypeStruct((block_rows, o...  28.7 us
    all_gather x1, blocking collectives, shards(): lookup_cols = lax.all_gather(prod_cols[:, 0], 'rows', axis=0, tiled=True)  15 us
    ppermute x7, waiting for transfers between devices, shards(): lax.ppermute(prod_blocks[:, 0], 'rows', [(r, (r + s) % groups) for r in r...  14.6 us
    unnamed x26, local copies, waits for them, and re-layouts  13.9 us
    all_to_all x1, starting transfers between devices, shards(): lax.all_to_all(jnp.tile(y_blocks[side_rows, 0], (tiles, 1, 1)), ('cols',...  12 us
    ppermute x7, starting transfers between devices, shards(): lax.ppermute(prod_blocks[:, 0], 'rows', [(r, (r + s) % groups) for r in r...  9.85 us
  transfers between devices with their start and end apart: 9, of which 3 were waited for; matrix products, arithmetic and copies ran while one was open for 9% of the time, Pallas kernels for 3%

profile of v7, /device:TPU:1, one launch (start us, length us, event | category | flops | bytes accessed | tf_op | source)
XLA Modules:
  0.0 271.1 jit_solution(6291057103174678284)
XLA Ops:
  6.5 2.3 slice_bitcast_fusion
  8.9 0.0 all-gather.5.cloned.1.call-update
  8.9 0.9 slice_bitcast_fusion.2.self_ref
  9.8 0.0 copy-start
  9.8 0.0 copy-start.5
  9.8 0.0 copy-start.2
  9.9 0.0 copy-start.4
  9.9 0.0 copy-start.3
  9.9 0.0 copy-start.1
  9.9 3.0 %tile.11 = bf16[32,4,128,128]{3,2,1,0:T(8,128)(2,1)} broadcast(bf16[4,128,128]{2,1,0:T(8,128)(2,1)S(1)} %slice_bitcast_fusion.2.self_ref), dimensions={1,2,3} | broadcast | bytes 4325376 | tf_op jit(solution)/shard_map/tile | solution.py:88
  12.9 12.0 %all-to-all-start = ((bf16[128,128,128]{2,1,0:T(8,128)(2,1)}), bf16[128,128,128]{2,1,0:T(8,128)(2,1)}, u32[]{:S(2)}, u32[]{:S(2)}) async-start(bf16[128,128,128]{2,1,0:T(8,128)(2,1)} %bitcast.53), calls=%async_computation | async-start | bytes 8388608 | tf_op jit(solution)/shard_map/all_to_all | solution.py:87
  24.9 2.1 collective-permute-start
  27.0 1.3 collective-permute-start.1
  28.3 1.7 collective-permute-start.2
  30.0 0.3 collective-permute-start.3
  30.4 1.9 collective-permute-start.4
  32.3 0.6 dynamic-slice.1
  33.6 0.1 bitcast_dynamic-update-slice_fusion.1
  33.8 114.2 %all-reduce.1 = s32[768]{0:T(1024)S(1)} all-reduce(s32[768]{0:T(1024)S(1)} %bitcast_dynamic-update-slice_fusion.1), channel_id=3, replica_groups=mesh['rows'=8,'cols'=8,'layers'=4] {'cols','layers'}, use_global_device_ids=true, to_apply=%add.1 | all-reduce | flops 768 | bytes 6144
  147.9 0.1 reshape.43
  148.0 0.1 copy.30
  148.1 0.1 reshape.36
  148.2 0.7 dynamic-slice
  149.6 0.1 bitcast_dynamic-update-slice_fusion
  149.7 15.0 %all-reduce = s32[192]{0:T(256)S(1)} all-reduce(s32[192]{0:T(256)S(1)} %bitcast_dynamic-update-slice_fusion), channel_id=2, replica_groups=mesh['rows'=8,'cols'=8,'layers'=4] {'rows'}, use_global_device_ids=true, to_apply=%add | all-reduce | flops 192 | bytes 1536 | tf_op jit(solution)/shard_map/all_gather | solution.py:74
  164.7 1.0 constant_dynamic-update-slice_fusion.8
  165.7 5.0 %gather_fusion = s32[768]{0:T(1024)S(1)} fusion(s32[192]{0:T(256)S(1)} %all-reduce, s32[1024]{0:T(1024)S(1)} %pad_clamp_fusion), kind=kCustom, calls=%fused_computation | custom fusion | bytes 9216 | tf_op jit(solution)/shard_map/gather | solution.py:77
  170.7 0.1 reshape.35
  170.7 0.1 copy.31
  170.8 0.1 slice.47
  170.9 0.1 copy.38
  171.0 0.1 reshape.30.i0_ref
  171.1 0.1 slice.48
  171.2 0.1 copy.39
  171.2 0.1 reshape.31.i1_ref
  171.3 0.2 collective-permute-start.5
  171.6 0.1 slice.40
  171.6 0.1 copy.40
  171.7 0.1 reshape.32.own_ref
  171.8 0.1 copy.32
  171.9 0.1 reshape.27.i0_ref
  172.0 0.1 copy.34
  172.0 0.1 reshape.28.i1_ref
  172.1 0.1 copy.35
  172.2 0.1 reshape.29.own_ref
  172.3 0.0 collective-permute-done.1
  172.3 2.2 collective-permute-start.6
  174.6 2.1 constant_dynamic-update-slice_fusion.7
  176.7 2.1 constant_dynamic-update-slice_fusion.6
  178.8 0.0 collective-permute-done.2
  178.8 2.1 constant_dynamic-update-slice_fusion.5
  180.9 0.0 collective-permute-done.3
  180.9 0.9 constant_dynamic-update-slice_fusion.4
  181.9 0.0 collective-permute-done.4
  181.9 1.0 constant_dynamic-update-slice_fusion.3
  182.9 6.1 %collective-permute-done.5 = bf16[24,128,128]{2,1,0:T(8,128)(2,1)} collective-permute-done((bf16[24,128,128]{2,1,0:T(8,128)(2,1)S(1)}, bf16[24,128,128]{2,1,0:T(8,128)(2,1)}, u32[]{:S(2)}, u32[]{:S(2)}) %collective-permute-start.5) | collective-permute-done | bytes 786464 | tf_op jit(solution)/shard_map/ppermute | solution.py:70
  189.0 2.1 constant_dynamic-update-slice_fusion.2
  191.1 8.5 %collective-permute-done.6 = bf16[24,128,128]{2,1,0:T(8,128)(2,1)S(1)} collective-permute-done((bf16[24,128,128]{2,1,0:T(8,128)(2,1)S(1)}, bf16[24,128,128]{2,1,0:T(8,128)(2,1)S(1)}, u32[]{:S(2)}, u32[]{:S(2)}) %collective-permute-start.6) | collective-permute-done | bytes 786464 | tf_op jit(solution)/shard_map/ppermute | solution.py:70
  199.6 1.0 constant_dynamic-update-slice_fusion.1
  200.6 0.6 constant_dynamic-update-slice_fusion.lookup_ref
  201.2 7.9 %shard_map.56 = bf16[4,2,128,128]{3,2,1,0:T(8,128)(2,1)S(1)} custom-call(s32[128]{0:T(128)S(1)} %reshape.30.i0_ref, s32[128]{0:T(128)S(1)} %reshape.31.i1_ref, s32[8]{0:T(128)S(1)} %reshape.32.own_ref, bf16[32,4,128,128]{3,2,1,0:T(8,128)(2,1)} %bitcast.15.y_ref, bf16[4,128,128]{2,1,0:T(8,128)(2,1)S(1)} %slice_bitcast_fusion.2.self_ref, ...), custom_call_target="tpu_custom_call" | custom-call | tf_op jit(solution)/shard_map/pallas_call | solution.py:37
  209.1 33.1 %all-gather.5.cloned.1.call-done = bf16[640,1,128,128]{3,2,1,0:T(8,128)(2,1)} async-done(((bf16[20,1,128,128]{3,2,1,0:T(8,128)(2,1)}), bf16[640,1,128,128]{3,2,1,0:T(8,128)(2,1)}) %all-gather.5.cloned.1.call-update) | async-done | bytes 20971536 | tf_op jit(solution)/shard_map/all_gather | solution.py:94
  242.2 20.8 %shard_map.55 = bf16[20,2,128,128]{3,2,1,0:T(8,128)(2,1)S(1)} custom-call(s32[640]{0:T(1024)S(1)} %reshape.27.i0_ref, s32[640]{0:T(1024)S(1)} %reshape.28.i1_ref, s32[40]{0:T(128)S(1)} %reshape.29.own_ref, bf16[32,20,128,128]{3,2,1,0:T(8,128)(2,1)} %bitcast.52, bf16[20,128,128]{2,1,0:T(8,128)(2,1)S(1)} %get-tuple-element.5.self_ref, ...), custom_call_target="tpu_custom_call" | custom-call | tf_op jit(solution)/shard_map/pallas_call | solution.py:37
  263.0 1.3 maximum_bitcast_fusion
  (16 shorter events, 0.1 us)
Async XLA Ops:
  6.5 235.7 %all-gather.5.cloned.1.call-start = ((), (), s32[]{:S(2)}) async-start(), calls=%async_computation.1 | async-start | bytes 21626880 | tf_op jit(solution)/shard_map/all_gather | solution.py:94
  9.8 15.1 %copy-start = (bf16[24,1,128,128]{3,2,1,0:T(8,128)(2,1)S(1)}, bf16[24,1,128,128]{3,2,1,0:T(8,128)(2,1)}, u32[]{:S(2)}) copy-start(bf16[24,1,128,128]{3,2,1,0:T(8,128)(2,1)} %param.7) | copy-start | bytes 2359300
  9.8 22.5 %copy-start.5 = (u32[256]{0:T(256)S(1)}, u32[256]{0:T(256)}, u32[]{:S(2)}) copy-start(u32[256]{0:T(256)} %constant.56) | copy-start | bytes 3076
  9.8 23.8 %copy-start.2 = (s32[24,1]{0,1:T(1,128)S(1)}, s32[24,1]{0,1:T(1,128)}, u32[]{:S(2)}) copy-start(s32[24,1]{0,1:T(1,128)} %param.6) | copy-start | bytes 292
  9.9 138.3 %copy-start.4 = (u32[256]{0:T(256)S(1)}, u32[256]{0:T(256)}, u32[]{:S(2)}) copy-start(u32[256]{0:T(256)} %constant.51) | copy-start | bytes 3076
  9.9 139.7 %copy-start.3 = (s32[24,1]{0,1:T(1,128)S(1)}, s32[24,1]{0,1:T(1,128)}, u32[]{:S(2)}) copy-start(s32[24,1]{0,1:T(1,128)} %param.8) | copy-start | bytes 292
  9.9 155.8 %copy-start.1 = (s32[24,1,2]{0,2,1:T(2,128)S(1)}, s32[24,1,2]{0,2,1:T(2,128)}, u32[]{:S(2)}) copy-start(s32[24,1,2]{0,2,1:T(2,128)} %param.9) | copy-start | bytes 580
  12.9 188.3 %all-to-all-start = ((bf16[128,128,128]{2,1,0:T(8,128)(2,1)}), bf16[128,128,128]{2,1,0:T(8,128)(2,1)}, u32[]{:S(2)}, u32[]{:S(2)}) async-start(bf16[128,128,128]{2,1,0:T(8,128)(2,1)} %bitcast.53), calls=%async_computation | async-start | bytes 8388608 | tf_op jit(solution)/shard_map/all_to_all | solution.py:87
  24.9 146.4 %collective-permute-start = (bf16[24,128,128]{2,1,0:T(8,128)(2,1)S(1)}, bf16[24,128,128]{2,1,0:T(8,128)(2,1)}, u32[]{:S(2)}, u32[]{:S(2)}) collective-permute-start(bf16[24,128,128]{2,1,0:T(8,128)(2,1)S(1)} %bitcast.54), channel_id=1, source_target_pairs={{0,32},{32,64},{64,96},{96,128},{128,160},{160,192},{192,224},{224... | collective-permute-start | bytes 2359304 | tf_op jit(solution)/shard_map/ppermute | solution.py:70
  27.0 145.3 %collective-permute-start.1 = (bf16[24,128,128]{2,1,0:T(8,128)(2,1)S(1)}, bf16[24,128,128]{2,1,0:T(8,128)(2,1)}, u32[]{:S(2)}, u32[]{:S(2)}) collective-permute-start(bf16[24,128,128]{2,1,0:T(8,128)(2,1)S(1)} %bitcast.55), channel_id=1, source_target_pairs={{0,64},{32,96},{64,128},{96,160},{128,192},{160,224},{192,0},{224,... | collective-permute-start | bytes 2359304 | tf_op jit(solution)/shard_map/ppermute | solution.py:70
  28.3 150.5 %collective-permute-start.2 = (bf16[24,128,128]{2,1,0:T(8,128)(2,1)S(1)}, bf16[24,128,128]{2,1,0:T(8,128)(2,1)}, u32[]{:S(2)}, u32[]{:S(2)}) collective-permute-start(bf16[24,128,128]{2,1,0:T(8,128)(2,1)S(1)} %bitcast.56), channel_id=1, source_target_pairs={{0,96},{32,128},{64,160},{96,192},{128,224},{160,0},{192,32},{224,... | collective-permute-start | bytes 2359304 | tf_op jit(solution)/shard_map/ppermute | solution.py:70
  30.0 150.9 %collective-permute-start.3 = (bf16[24,128,128]{2,1,0:T(8,128)(2,1)S(1)}, bf16[24,128,128]{2,1,0:T(8,128)(2,1)S(1)}, u32[]{:S(2)}, u32[]{:S(2)}) collective-permute-start(bf16[24,128,128]{2,1,0:T(8,128)(2,1)S(1)} %bitcast.57), channel_id=1, source_target_pairs={{0,128},{32,160},{64,192},{96,224},{128,0},{160,32},{192,64},{224,... | collective-permute-start | bytes 2359304 | tf_op jit(solution)/shard_map/ppermute | solution.py:70
  30.4 151.5 %collective-permute-start.4 = (bf16[24,128,128]{2,1,0:T(8,128)(2,1)S(1)}, bf16[24,128,128]{2,1,0:T(8,128)(2,1)S(1)}, u32[]{:S(2)}, u32[]{:S(2)}) collective-permute-start(bf16[24,128,128]{2,1,0:T(8,128)(2,1)S(1)} %bitcast.58), channel_id=1, source_target_pairs={{0,160},{32,192},{64,224},{96,0},{128,32},{160,64},{192,96},{224,1... | collective-permute-start | bytes 2359304 | tf_op jit(solution)/shard_map/ppermute | solution.py:70
  171.3 17.6 %collective-permute-start.5 = (bf16[24,128,128]{2,1,0:T(8,128)(2,1)S(1)}, bf16[24,128,128]{2,1,0:T(8,128)(2,1)}, u32[]{:S(2)}, u32[]{:S(2)}) collective-permute-start(bf16[24,128,128]{2,1,0:T(8,128)(2,1)S(1)} %bitcast.59), channel_id=1, source_target_pairs={{0,192},{32,224},{64,0},{96,32},{128,64},{160,96},{192,128},{224,1... | collective-permute-start | bytes 2359304 | tf_op jit(solution)/shard_map/ppermute | solution.py:70
  172.3 27.3 %collective-permute-start.6 = (bf16[24,128,128]{2,1,0:T(8,128)(2,1)S(1)}, bf16[24,128,128]{2,1,0:T(8,128)(2,1)S(1)}, u32[]{:S(2)}, u32[]{:S(2)}) collective-permute-start(bf16[24,128,128]{2,1,0:T(8,128)(2,1)S(1)} %bitcast.60), channel_id=1, source_target_pairs={{0,224},{32,0},{64,32},{96,64},{128,96},{160,128},{192,160},{224,1... | collective-permute-start | bytes 2359304 | tf_op jit(solution)/shard_map/ppermute | solution.py:70
Sparse Core Ops, SparseCore 0:
  9.9 232.2 all-gather.4

commit v8 on v7

--- a/solution.py
+++ b/solution.py
@@ -7,7 +7,6 @@
 
 
 ROWS_PER_STEP = 4
-SIDE_ROWS = 4
 
 
 def _row_kernel(i0_ref, i1_ref, own_ref, y_ref, self_ref, lookup_ref, out_ref, lhs_ref, stk_ref):
@@ -81,21 +80,10 @@
     i1 = jnp.where(right_cols == out_cols[:, 0, 1][:, None], krow, nb).astype(jnp.int32)
     own = (out_cols[:, 0, :] == y_cols[:, 0][:, None]).astype(jnp.int32)
 
-    tiles = left_cols.shape[1]
-    main = block_rows - SIDE_ROWS
-    side_rows = slice(main, block_rows)
-    side = lax.all_to_all(
-        jnp.tile(y_blocks[side_rows, 0], (tiles, 1, 1)), ("cols", "layers"), 0, 0, tiled=True)
-    side = side.reshape(tiles, SIDE_ROWS, block_size, block_size)
-    out_side = _rows_product(
-        i0[side_rows].reshape(-1), i1[side_rows].reshape(-1), own[side_rows].reshape(-1),
-        side, y_blocks[side_rows, 0], lookup, out_width)
-    rows = slice(0, main)
-    left = lax.all_gather(y_blocks[rows, 0], ("cols", "layers"), axis=0, tiled=False)
-    out_main = _rows_product(
-        i0[rows].reshape(-1), i1[rows].reshape(-1), own[rows].reshape(-1),
-        left, y_blocks[rows, 0], lookup, out_width)
-    return jnp.concatenate([out_main, out_side], axis=0)[:, None]
+    left = lax.all_gather(y_blocks[:, 0], ("cols", "layers"), axis=0, tiled=False)
+    out = _rows_product(
+        i0.reshape(-1), i1.reshape(-1), own.reshape(-1), left, y_blocks[:, 0], lookup, out_width)
+    return out[:, None]
 
 
 def solution(mesh):

time: 271 us -> 228 us (0.84)
  blocking collectives: 129 us -> 58.3 us
  waiting for transfers between devices: 47.8 us -> 92.2 us
  starting transfers between devices: 21.8 us -> 14.3 us
  Pallas kernels: 28.7 us -> 24.6 us
  local copies, waits for them, and re-layouts: 27.3 us -> 23.8 us
    unnamed x1, blocking collectives: 114 us -> 18.6 us
    all_gather x1, waiting for transfers between devices: 33.1 us -> 76.2 us  [shards(): lax.all_gather(y_blocks[:, 0], ('cols', 'layers'), axis=0, tiled=False)]
    all_gather x1, blocking collectives: 15 us -> 39.7 us  [shards(): lookup_cols = lax.all_gather(prod_cols[:, 0], 'rows', axis=0, tiled=True)]
    all_to_all x1 -> x0, starting transfers between devices: 12 us -> none  [shards(): lax.all_to_all(jnp.tile(y_blocks[side_rows, 0], (tiles, 1, 1)), ('cols',...]
    ppermute x7, starting transfers between devices: 9.85 us -> 14.3 us  [shards(): lax.ppermute(prod_blocks[:, 0], 'rows', [(r, (r + s) % groups) for r in r...]
    pallas_call x2 -> x1, Pallas kernels: 28.7 us -> 24.6 us  [_rows_product(): pl.pallas_call(_row_kernel, out_shape=jax.ShapeDtypeStruct((block_rows, o...]
    another operation x2 -> x0, local copies, waits for them, and re-layouts: 3.9 us -> none  [shards(): jnp.tile(y_blocks[side_rows, 0], (tiles, 1, 1))]
    unnamed x26 -> x23, local copies, waits for them, and re-layouts: 13.9 us -> 16.6 us
  transfers between devices with their start and end apart: 9 -> 8, of which waited for: 3 -> 3; matrix products, arithmetic and copies ran while one was open for 9% -> 10% of each run, Pallas kernels for 3% -> 0%
where the time goes in v8:
time: 228 us
  waiting for transfers between devices  92.2 us (40%)
  blocking collectives  58.3 us (26%)
  Pallas kernels  24.6 us (11%)
  local copies, waits for them, and re-layouts  23.8 us (10%)
  between operations  14.8 us (6%)
  starting transfers between devices  14.3 us (6%)
    all_gather x1, waiting for transfers between devices, shards(): lax.all_gather(y_blocks[:, 0], ('cols', 'layers'), axis=0, tiled=False)  76.2 us
    all_gather x1, blocking collectives, shards(): lookup_cols = lax.all_gather(prod_cols[:, 0], 'rows', axis=0, tiled=True)  39.7 us
    pallas_call x1, Pallas kernels, _rows_product(): pl.pallas_call(_row_kernel, out_shape=jax.ShapeDtypeStruct((block_rows, o...  24.6 us
    unnamed x1, blocking collectives  18.6 us
    unnamed x23, local copies, waits for them, and re-layouts  16.6 us
    ppermute x7, waiting for transfers between devices, shards(): lax.ppermute(prod_blocks[:, 0], 'rows', [(r, (r + s) % groups) for r in r...  15.2 us
    ppermute x7, starting transfers between devices, shards(): lax.ppermute(prod_blocks[:, 0], 'rows', [(r, (r + s) % groups) for r in r...  14.3 us
    gather x3, local copies, waits for them, and re-layouts, shards(): right_cols = lookup_cols[left_cols]  5.13 us
  transfers between devices with their start and end apart: 8, of which 3 were waited for; matrix products, arithmetic and copies ran while one was open for 10% of the time, Pallas kernels for 0%

profile of v8, /device:TPU:1, one launch (start us, length us, event | category | flops | bytes accessed | tf_op | source)
XLA Modules:
  0.0 228.1 jit_solution(13980114992441049842)
XLA Ops:
  6.5 0.0 all-gather.5.cloned.1.call-start
  6.5 0.7 all-gather.5.cloned.1.call-update
  7.3 2.7 %collective-permute-start = (bf16[24,128,128]{2,1,0:T(8,128)(2,1)}, bf16[24,128,128]{2,1,0:T(8,128)(2,1)}, u32[]{:S(2)}, u32[]{:S(2)}) collective-permute-start(bf16[24,128,128]{2,1,0:T(8,128)(2,1)} %bitcast.42), channel_id=1, source_target_pairs={{0,32},{32,64},{64,96},{96,128},{128,160},{160,192},{192,224},{224... | collective-permute-start | bytes 2359304 | tf_op jit(solution)/shard_map/ppermute | solution.py:69
  9.9 1.3 collective-permute-start.1
  11.2 1.7 collective-permute-start.2
  12.9 1.3 collective-permute-start.3
  14.2 2.6 %collective-permute-start.4 = (bf16[24,128,128]{2,1,0:T(8,128)(2,1)}, bf16[24,128,128]{2,1,0:T(8,128)(2,1)S(1)}, u32[]{:S(2)}, u32[]{:S(2)}) collective-permute-start(bf16[24,128,128]{2,1,0:T(8,128)(2,1)} %bitcast.46), channel_id=1, source_target_pairs={{0,160},{32,192},{64,224},{96,0},{128,32},{160,64},{192,96},{224,1... | collective-permute-start | bytes 2359304 | tf_op jit(solution)/shard_map/ppermute | solution.py:69
  16.8 1.3 dynamic-slice.1
  18.8 0.8 bitcast_dynamic-update-slice_fusion.1
  19.5 18.6 %all-reduce.1 = s32[768]{0:T(1024)S(1)} all-reduce(s32[768]{0:T(1024)S(1)} %bitcast_dynamic-update-slice_fusion.1), channel_id=3, replica_groups=mesh['rows'=8,'cols'=8,'layers'=4] {'cols','layers'}, use_global_device_ids=true, to_apply=%add.1 | all-reduce | flops 768 | bytes 6144
  38.2 0.1 reshape.22
  38.3 0.1 copy.15
  38.3 0.1 reshape.15
  38.4 1.3 dynamic-slice
  40.3 0.8 bitcast_dynamic-update-slice_fusion
  41.1 39.7 %all-reduce = s32[192]{0:T(256)S(1)} all-reduce(s32[192]{0:T(256)S(1)} %bitcast_dynamic-update-slice_fusion), channel_id=2, replica_groups=mesh['rows'=8,'cols'=8,'layers'=4] {'rows'}, use_global_device_ids=true, to_apply=%add | all-reduce | flops 192 | bytes 1536 | tf_op jit(solution)/shard_map/all_gather | solution.py:73
  80.8 2.2 constant_dynamic-update-slice_fusion.8
  82.9 0.8 slice_bitcast_fusion
  83.7 0.0 copy-start.2
  83.7 0.0 copy-start.3
  83.7 0.0 copy-start.1
  83.7 5.0 %gather_fusion = s32[768]{0:T(1024)S(1)} fusion(s32[192]{0:T(256)S(1)} %all-reduce, s32[1024]{0:T(1024)S(1)} %pad_clamp_fusion), kind=kCustom, calls=%fused_computation | custom fusion | bytes 9216 | tf_op jit(solution)/shard_map/gather | solution.py:76
  88.7 0.0 copy-start
  88.7 0.1 reshape.14
  88.8 0.1 copy.16
  88.9 0.0 copy-done.2
  88.9 0.1 copy.20
  89.0 0.1 copy.17
  89.1 0.1 reshape.11.i0_ref
  89.1 0.1 copy.19
  89.2 0.1 reshape.12.i1_ref
  89.3 0.0 copy-done.3
  89.3 0.1 eq.43
  89.4 0.1 eq.44
  89.5 0.1 squeeze.9
  89.6 0.0 collective-permute-done
  89.6 0.0 copy-done.1
  89.6 2.5 %collective-permute-start.5 = (bf16[24,128,128]{2,1,0:T(8,128)(2,1)S(1)}, bf16[24,128,128]{2,1,0:T(8,128)(2,1)S(1)}, u32[]{:S(2)}, u32[]{:S(2)}) collective-permute-start(bf16[24,128,128]{2,1,0:T(8,128)(2,1)S(1)} %bitcast.47), channel_id=1, source_target_pairs={{0,192},{32,224},{64,0},{96,32},{128,64},{160,96},{192,128},{224,1... | collective-permute-start | bytes 2359304 | tf_op jit(solution)/shard_map/ppermute | solution.py:69
  92.1 0.0 collective-permute-done.1
  92.1 2.2 collective-permute-start.6
  94.3 2.1 constant_dynamic-update-slice_fusion.7
  96.4 2.1 constant_dynamic-update-slice_fusion.6
  98.5 0.0 collective-permute-done.2
  98.5 2.1 constant_dynamic-update-slice_fusion.5
  100.6 0.0 collective-permute-done.3
  100.6 1.0 constant_dynamic-update-slice_fusion.4
  101.6 0.0 collective-permute-done.4
  101.6 1.0 constant_dynamic-update-slice_fusion.3
  102.6 6.1 %collective-permute-done.5 = bf16[24,128,128]{2,1,0:T(8,128)(2,1)S(1)} collective-permute-done((bf16[24,128,128]{2,1,0:T(8,128)(2,1)S(1)}, bf16[24,128,128]{2,1,0:T(8,128)(2,1)S(1)}, u32[]{:S(2)}, u32[]{:S(2)}) %collective-permute-start.5) | collective-permute-done | bytes 786464 | tf_op jit(solution)/shard_map/ppermute | solution.py:69
  108.7 1.0 constant_dynamic-update-slice_fusion.2
  109.7 9.1 %collective-permute-done.6 = bf16[24,128,128]{2,1,0:T(8,128)(2,1)S(1)} collective-permute-done((bf16[24,128,128]{2,1,0:T(8,128)(2,1)S(1)}, bf16[24,128,128]{2,1,0:T(8,128)(2,1)S(1)}, u32[]{:S(2)}, u32[]{:S(2)}) %collective-permute-start.6) | collective-permute-done | bytes 786464 | tf_op jit(solution)/shard_map/ppermute | solution.py:69
  118.8 1.0 constant_dynamic-update-slice_fusion.1
  119.8 0.6 constant_dynamic-update-slice_fusion.lookup_ref
  120.4 76.2 %all-gather.5.cloned.1.call-done = bf16[768,1,128,128]{3,2,1,0:T(8,128)(2,1)} async-done(((bf16[24,1,128,128]{3,2,1,0:T(8,128)(2,1)}), bf16[768,1,128,128]{3,2,1,0:T(8,128)(2,1)}) %all-gather.5.cloned.1.call-update) | async-done | bytes 25165840 | tf_op jit(solution)/shard_map/all_gather | solution.py:83
  196.6 0.0 copy-done
  196.6 24.6 %shard_map.55 = bf16[24,2,128,128]{3,2,1,0:T(8,128)(2,1)} custom-call(s32[768]{0:T(1024)S(1)} %reshape.11.i0_ref, s32[768]{0:T(1024)S(1)} %reshape.12.i1_ref, s32[48]{0:T(128)S(1)} %compare_convert_fusion.own_ref, bf16[32,24,128,128]{3,2,1,0:T(8,128)(2,1)} %bitcast.41, bf16[24,128,128]{2,1,0:T(8,128)(2,1)S(1)} %bitcast.40, ...), custom_call_target="tpu_custom_call" | custom-call | tf_op jit(solution)/shard_map/pallas_call | solution.py:36
  (6 shorter events, 0.1 us)
Async XLA Ops:
  6.5 190.1 %all-gather.5.cloned.1.call-start = ((), (), s32[]{:S(2)}) async-start(), calls=%async_computation | async-start | bytes 25952256 | tf_op jit(solution)/shard_map/all_gather | solution.py:83
  7.3 82.3 %collective-permute-start = (bf16[24,128,128]{2,1,0:T(8,128)(2,1)}, bf16[24,128,128]{2,1,0:T(8,128)(2,1)}, u32[]{:S(2)}, u32[]{:S(2)}) collective-permute-start(bf16[24,128,128]{2,1,0:T(8,128)(2,1)} %bitcast.42), channel_id=1, source_target_pairs={{0,32},{32,64},{64,96},{96,128},{128,160},{160,192},{192,224},{224... | collective-permute-start | bytes 2359304 | tf_op jit(solution)/shard_map/ppermute | solution.py:69
  9.9 82.1 %collective-permute-start.1 = (bf16[24,128,128]{2,1,0:T(8,128)(2,1)}, bf16[24,128,128]{2,1,0:T(8,128)(2,1)}, u32[]{:S(2)}, u32[]{:S(2)}) collective-permute-start(bf16[24,128,128]{2,1,0:T(8,128)(2,1)} %bitcast.43), channel_id=1, source_target_pairs={{0,64},{32,96},{64,128},{96,160},{128,192},{160,224},{192,0},{224,... | collective-permute-start | bytes 2359304 | tf_op jit(solution)/shard_map/ppermute | solution.py:69
  11.2 87.3 %collective-permute-start.2 = (bf16[24,128,128]{2,1,0:T(8,128)(2,1)}, bf16[24,128,128]{2,1,0:T(8,128)(2,1)}, u32[]{:S(2)}, u32[]{:S(2)}) collective-permute-start(bf16[24,128,128]{2,1,0:T(8,128)(2,1)} %bitcast.44), channel_id=1, source_target_pairs={{0,96},{32,128},{64,160},{96,192},{128,224},{160,0},{192,32},{224,... | collective-permute-start | bytes 2359304 | tf_op jit(solution)/shard_map/ppermute | solution.py:69
  12.9 87.7 %collective-permute-start.3 = (bf16[24,128,128]{2,1,0:T(8,128)(2,1)}, bf16[24,128,128]{2,1,0:T(8,128)(2,1)S(1)}, u32[]{:S(2)}, u32[]{:S(2)}) collective-permute-start(bf16[24,128,128]{2,1,0:T(8,128)(2,1)} %bitcast.45), channel_id=1, source_target_pairs={{0,128},{32,160},{64,192},{96,224},{128,0},{160,32},{192,64},{224,... | collective-permute-start | bytes 2359304 | tf_op jit(solution)/shard_map/ppermute | solution.py:69
  14.2 87.4 %collective-permute-start.4 = (bf16[24,128,128]{2,1,0:T(8,128)(2,1)}, bf16[24,128,128]{2,1,0:T(8,128)(2,1)S(1)}, u32[]{:S(2)}, u32[]{:S(2)}) collective-permute-start(bf16[24,128,128]{2,1,0:T(8,128)(2,1)} %bitcast.46), channel_id=1, source_target_pairs={{0,160},{32,192},{64,224},{96,0},{128,32},{160,64},{192,96},{224,1... | collective-permute-start | bytes 2359304 | tf_op jit(solution)/shard_map/ppermute | solution.py:69
  83.7 5.2 %copy-start.2 = (s32[24,1,2]{0,2,1:T(2,128)S(1)}, s32[24,1,2]{0,2,1:T(2,128)}, u32[]{:S(2)}) copy-start(s32[24,1,2]{0,2,1:T(2,128)} %param.9) | copy-start | bytes 580
  83.7 5.6 %copy-start.3 = (s32[24,1]{0,1:T(1,128)S(1)}, s32[24,1]{0,1:T(1,128)}, u32[]{:S(2)}) copy-start(s32[24,1]{0,1:T(1,128)} %param.6) | copy-start | bytes 292
  83.7 5.9 %copy-start.1 = (bf16[24,1,128,128]{3,2,1,0:T(8,128)(2,1)S(1)}, bf16[24,1,128,128]{3,2,1,0:T(8,128)(2,1)}, u32[]{:S(2)}) copy-start(bf16[24,1,128,128]{3,2,1,0:T(8,128)(2,1)} %param.7) | copy-start | bytes 2359300
  88.7 107.9 %copy-start = (bf16[24,1,128,128]{3,2,1,0:T(8,128)(2,1)S(1)}, bf16[24,1,128,128]{3,2,1,0:T(8,128)(2,1)}, u32[]{:S(2)}) copy-start(bf16[24,1,128,128]{3,2,1,0:T(8,128)(2,1)} %param.5) | copy-start | bytes 2359300
  89.6 19.1 %collective-permute-start.5 = (bf16[24,128,128]{2,1,0:T(8,128)(2,1)S(1)}, bf16[24,128,128]{2,1,0:T(8,128)(2,1)S(1)}, u32[]{:S(2)}, u32[]{:S(2)}) collective-permute-start(bf16[24,128,128]{2,1,0:T(8,128)(2,1)S(1)} %bitcast.47), channel_id=1, source_target_pairs={{0,192},{32,224},{64,0},{96,32},{128,64},{160,96},{192,128},{224,1... | collective-permute-start | bytes 2359304 | tf_op jit(solution)/shard_map/ppermute | solution.py:69
  92.1 26.7 %collective-permute-start.6 = (bf16[24,128,128]{2,1,0:T(8,128)(2,1)S(1)}, bf16[24,128,128]{2,1,0:T(8,128)(2,1)S(1)}, u32[]{:S(2)}, u32[]{:S(2)}) collective-permute-start(bf16[24,128,128]{2,1,0:T(8,128)(2,1)S(1)} %bitcast.48), channel_id=1, source_target_pairs={{0,224},{32,0},{64,32},{96,64},{128,96},{160,128},{192,160},{224,1... | collective-permute-start | bytes 2359304 | tf_op jit(solution)/shard_map/ppermute | solution.py:69
Sparse Core Ops, SparseCore 0:
  9.9 186.6 all-gather.4

commit v9 on v8

--- a/solution.py
+++ b/solution.py
@@ -9,20 +9,19 @@
 ROWS_PER_STEP = 4
 
 
-def _row_kernel(i0_ref, i1_ref, own_ref, y_ref, self_ref, lookup_ref, out_ref, lhs_ref, stk_ref):
+def _row_kernel(i0_ref, i1_ref, own_ref, y_ref, self_ref, lookup_ref, out_ref, stk_ref):
     g = pl.program_id(0)
-    tiles = y_ref.shape[0]
-    rb = y_ref.shape[1]
-    bs = y_ref.shape[-1]
+    rb = y_ref.shape[0]
+    bs = y_ref.shape[1]
+    tiles = y_ref.shape[2] // bs
     for r in range(rb):
         i = g * rb + r
         for tp in range(tiles):
             at = i * tiles + tp
             cols = slice(tp * bs, (tp + 1) * bs)
-            lhs_ref[:, cols] = y_ref[tp, r]
             stk_ref[cols, 0:bs] = lookup_ref[i0_ref[at]]
             stk_ref[cols, bs:2 * bs] = lookup_ref[i1_ref[at]]
-        res = jnp.dot(lhs_ref[...], stk_ref[...], preferred_element_type=jnp.float32)
+        res = jnp.dot(y_ref[r], stk_ref[...], preferred_element_type=jnp.float32)
         own = self_ref[r].astype(jnp.float32)
         for w in range(2):
             own_w = jnp.where(own_ref[2 * i + w] != 0, own, 0.0)
@@ -30,7 +29,8 @@
 
 
 def _rows_product(i0, i1, own, left, own_blocks, lookup, out_width):
-    tiles, block_rows, block_size, _ = left.shape
+    block_rows, block_size, width = left.shape
+    tiles = width // block_size
     nb = lookup.shape[0]
     rb = ROWS_PER_STEP if block_rows % ROWS_PER_STEP == 0 else 1
     return pl.pallas_call(
@@ -40,13 +40,12 @@
             num_scalar_prefetch=3,
             grid=(block_rows // rb,),
             in_specs=[
-                pl.BlockSpec((tiles, rb, block_size, block_size), lambda g, *_: (0, g, 0, 0)),
+                pl.BlockSpec((rb, block_size, width), lambda g, *_: (g, 0, 0)),
                 pl.BlockSpec((rb, block_size, block_size), lambda g, *_: (g, 0, 0)),
                 pl.BlockSpec((nb, block_size, block_size), lambda g, *_: (0, 0, 0)),
             ],
             out_specs=pl.BlockSpec((rb, out_width, block_size, block_size), lambda g, *_: (g, 0, 0, 0)),
             scratch_shapes=[
-                pltpu.VMEM((block_size, tiles * block_size), jnp.bfloat16),
                 pltpu.VMEM((tiles * block_size, out_width * block_size), jnp.bfloat16),
             ],
         ),
@@ -80,7 +79,7 @@
     i1 = jnp.where(right_cols == out_cols[:, 0, 1][:, None], krow, nb).astype(jnp.int32)
     own = (out_cols[:, 0, :] == y_cols[:, 0][:, None]).astype(jnp.int32)
 
-    left = lax.all_gather(y_blocks[:, 0], ("cols", "layers"), axis=0, tiled=False)
+    left = lax.all_gather(y_blocks[:, 0], ("cols", "layers"), axis=2, tiled=True)
     out = _rows_product(
         i0.reshape(-1), i1.reshape(-1), own.reshape(-1), left, y_blocks[:, 0], lookup, out_width)
     return out[:, None]

time: 228 us -> 237 us (1.039); the launches traced: 228 us -> 234 us
  waiting for transfers between devices: 92.2 us -> 102 us
  Pallas kernels: 24.6 us -> 20.5 us
    all_gather x1, waiting for transfers between devices: 76.2 us -> 87 us  [shards(): lax.all_gather(y_blocks[:, 0], ('cols', 'layers'), axis=2, tiled=True)]
    pallas_call x1, Pallas kernels: 24.6 us -> 20.5 us  [_rows_product(): pl.pallas_call(_row_kernel, out_shape=jax.ShapeDtypeStruct((block_rows, o...]
where the time goes in v9:
time: 237 us; the launch traced here: 234 us
  waiting for transfers between devices  102 us (43%)
  blocking collectives  58.2 us (25%)
  local copies, waits for them, and re-layouts  23.9 us (10%)
  Pallas kernels  20.5 us (9%)
  between operations  14.8 us (6%)
  starting transfers between devices  14.4 us (6%)
    all_gather x1, waiting for transfers between devices, shards(): lax.all_gather(y_blocks[:, 0], ('cols', 'layers'), axis=2, tiled=True)  87 us
    all_gather x1, blocking collectives, shards(): lookup_cols = lax.all_gather(prod_cols[:, 0], 'rows', axis=0, tiled=True)  39.8 us
    pallas_call x1, Pallas kernels, _rows_product(): pl.pallas_call(_row_kernel, out_shape=jax.ShapeDtypeStruct((block_rows, o...  20.5 us
    unnamed x1, blocking collectives  18.5 us
    unnamed x23, local copies, waits for them, and re-layouts  16.6 us
    ppermute x7, waiting for transfers between devices, shards(): lax.ppermute(prod_blocks[:, 0], 'rows', [(r, (r + s) % groups) for r in r...  14.4 us
    ppermute x7, starting transfers between devices, shards(): lax.ppermute(prod_blocks[:, 0], 'rows', [(r, (r + s) % groups) for r in r...  14.4 us
    gather x3, local copies, waits for them, and re-layouts, shards(): right_cols = lookup_cols[left_cols]  5.13 us
  transfers between devices with their start and end apart: 8, of which 3 were waited for; matrix products, arithmetic and copies ran while one was open for 10% of the time, Pallas kernels for 0%

profile of v9, /device:TPU:1, one launch (start us, length us, event | category | flops | bytes accessed | tf_op | source)
XLA Modules:
  0.0 234.0 jit_solution(11322418377164633356)
XLA Ops:
  6.5 0.0 all-gather.5.cloned.1.call-start
  6.5 0.7 all-gather.5.cloned.1.call-update
  7.3 2.7 %collective-permute-start = (bf16[24,128,128]{2,1,0:T(8,128)(2,1)}, bf16[24,128,128]{2,1,0:T(8,128)(2,1)}, u32[]{:S(2)}, u32[]{:S(2)}) collective-permute-start(bf16[24,128,128]{2,1,0:T(8,128)(2,1)} %bitcast.44), channel_id=1, source_target_pairs={{0,32},{32,64},{64,96},{96,128},{128,160},{160,192},{192,224},{224... | collective-permute-start | bytes 2359304 | tf_op jit(solution)/shard_map/ppermute | solution.py:68
  9.9 1.3 collective-permute-start.1
  11.2 1.7 collective-permute-start.2
  12.9 1.3 collective-permute-start.3
  14.2 2.6 %collective-permute-start.4 = (bf16[24,128,128]{2,1,0:T(8,128)(2,1)}, bf16[24,128,128]{2,1,0:T(8,128)(2,1)S(1)}, u32[]{:S(2)}, u32[]{:S(2)}) collective-permute-start(bf16[24,128,128]{2,1,0:T(8,128)(2,1)} %bitcast.48), channel_id=1, source_target_pairs={{0,160},{32,192},{64,224},{96,0},{128,32},{160,64},{192,96},{224,1... | collective-permute-start | bytes 2359304 | tf_op jit(solution)/shard_map/ppermute | solution.py:68
  16.8 1.3 dynamic-slice.1
  18.8 0.8 bitcast_dynamic-update-slice_fusion.1
  19.5 18.5 %all-reduce.1 = s32[768]{0:T(1024)S(1)} all-reduce(s32[768]{0:T(1024)S(1)} %bitcast_dynamic-update-slice_fusion.1), channel_id=3, replica_groups=mesh['rows'=8,'cols'=8,'layers'=4] {'cols','layers'}, use_global_device_ids=true, to_apply=%add.1 | all-reduce | flops 768 | bytes 6144
  38.0 0.1 reshape.22
  38.1 0.1 copy.9
  38.2 0.1 reshape.15
  38.3 1.3 dynamic-slice
  40.2 0.8 bitcast_dynamic-update-slice_fusion
  41.0 39.8 %all-reduce = s32[192]{0:T(256)S(1)} all-reduce(s32[192]{0:T(256)S(1)} %bitcast_dynamic-update-slice_fusion), channel_id=2, replica_groups=mesh['rows'=8,'cols'=8,'layers'=4] {'rows'}, use_global_device_ids=true, to_apply=%add | all-reduce | flops 192 | bytes 1536 | tf_op jit(solution)/shard_map/all_gather | solution.py:72
  80.7 2.2 constant_dynamic-update-slice_fusion.8
  82.9 0.8 slice_bitcast_fusion
  83.7 0.0 copy-start.2
  83.7 0.0 copy-start.3
  83.7 0.0 copy-start.1
  83.7 5.0 %gather_fusion = s32[768]{0:T(1024)S(1)} fusion(s32[192]{0:T(256)S(1)} %all-reduce, s32[1024]{0:T(1024)S(1)} %pad_clamp_fusion), kind=kCustom, calls=%fused_computation | custom fusion | bytes 9216 | tf_op jit(solution)/shard_map/gather | solution.py:75
  88.7 0.0 copy-start
  88.7 0.1 reshape.14
  88.8 0.1 copy.10
  88.9 0.0 copy-done.2
  88.9 0.1 copy.14
  89.0 0.1 copy.11
  89.0 0.1 reshape.11.i0_ref
  89.1 0.1 copy.13
  89.2 0.1 reshape.12.i1_ref
  89.3 0.0 copy-done.3
  89.3 0.1 eq.43
  89.3 0.1 eq.44
  89.4 0.1 squeeze.9
  89.5 0.0 collective-permute-done
  89.6 0.0 copy-done.1
  89.6 2.0 collective-permute-start.5
  91.6 0.0 collective-permute-done.1
  91.6 2.7 %collective-permute-start.6 = (bf16[24,128,128]{2,1,0:T(8,128)(2,1)S(1)}, bf16[24,128,128]{2,1,0:T(8,128)(2,1)S(1)}, u32[]{:S(2)}, u32[]{:S(2)}) collective-permute-start(bf16[24,128,128]{2,1,0:T(8,128)(2,1)S(1)} %bitcast.50), channel_id=1, source_target_pairs={{0,224},{32,0},{64,32},{96,64},{128,96},{160,128},{192,160},{224,1... | collective-permute-start | bytes 2359304 | tf_op jit(solution)/shard_map/ppermute | solution.py:68
  94.3 2.1 constant_dynamic-update-slice_fusion.7
  96.5 2.1 constant_dynamic-update-slice_fusion.6
  98.6 0.0 collective-permute-done.2
  98.6 2.1 constant_dynamic-update-slice_fusion.5
  100.7 0.0 collective-permute-done.3
  100.7 1.0 constant_dynamic-update-slice_fusion.4
  101.7 0.0 collective-permute-done.4
  101.7 1.0 constant_dynamic-update-slice_fusion.3
  102.6 4.5 %collective-permute-done.5 = bf16[24,128,128]{2,1,0:T(8,128)(2,1)S(1)} collective-permute-done((bf16[24,128,128]{2,1,0:T(8,128)(2,1)S(1)}, bf16[24,128,128]{2,1,0:T(8,128)(2,1)S(1)}, u32[]{:S(2)}, u32[]{:S(2)}) %collective-permute-start.5) | collective-permute-done | bytes 786464 | tf_op jit(solution)/shard_map/ppermute | solution.py:68
  107.2 1.0 constant_dynamic-update-slice_fusion.2
  108.1 9.9 %collective-permute-done.6 = bf16[24,128,128]{2,1,0:T(8,128)(2,1)S(1)} collective-permute-done((bf16[24,128,128]{2,1,0:T(8,128)(2,1)S(1)}, bf16[24,128,128]{2,1,0:T(8,128)(2,1)S(1)}, u32[]{:S(2)}, u32[]{:S(2)}) %collective-permute-start.6) | collective-permute-done | bytes 786464 | tf_op jit(solution)/shard_map/ppermute | solution.py:68
  118.0 1.0 constant_dynamic-update-slice_fusion.1
  119.0 0.6 constant_dynamic-update-slice_fusion.lookup_ref
  119.6 87.0 %all-gather.5.cloned.1.call-done = bf16[24,1,128,4096]{3,2,0,1:T(8,128)(2,1)} async-done(((bf16[24,1,128,128]{3,2,0,1:T(8,128)(2,1)}), bf16[24,1,128,4096]{3,2,0,1:T(8,128)(2,1)}) %all-gather.5.cloned.1.call-update) | async-done | bytes 25165840 | tf_op jit(solution)/shard_map/all_gather | solution.py:82
  206.7 0.0 copy-done
  206.7 20.5 %shard_map.55 = bf16[24,2,128,128]{3,2,1,0:T(8,128)(2,1)} custom-call(s32[768]{0:T(1024)S(1)} %reshape.11.i0_ref, s32[768]{0:T(1024)S(1)} %reshape.12.i1_ref, s32[48]{0:T(128)S(1)} %compare_convert_fusion.own_ref, bf16[24,128,4096]{2,1,0:T(8,128)(2,1)} %bitcast.43, bf16[24,128,128]{2,1,0:T(8,128)(2,1)S(1)} %bitcast.42, ...), custom_call_target="tpu_custom_call" | custom-call | tf_op jit(solution)/shard_map/pallas_call | solution.py:36
  (6 shorter events, 0.1 us)
Async XLA Ops:
  6.5 200.1 %all-gather.5.cloned.1.call-start = ((), (), s32[]{:S(2)}) async-start(), calls=%async_computation | async-start | bytes 25952256 | tf_op jit(solution)/shard_map/all_gather | solution.py:82
  7.3 82.3 %collective-permute-start = (bf16[24,128,128]{2,1,0:T(8,128)(2,1)}, bf16[24,128,128]{2,1,0:T(8,128)(2,1)}, u32[]{:S(2)}, u32[]{:S(2)}) collective-permute-start(bf16[24,128,128]{2,1,0:T(8,128)(2,1)} %bitcast.44), channel_id=1, source_target_pairs={{0,32},{32,64},{64,96},{96,128},{128,160},{160,192},{192,224},{224... | collective-permute-start | bytes 2359304 | tf_op jit(solution)/shard_map/ppermute | solution.py:68
  9.9 81.7 %collective-permute-start.1 = (bf16[24,128,128]{2,1,0:T(8,128)(2,1)}, bf16[24,128,128]{2,1,0:T(8,128)(2,1)}, u32[]{:S(2)}, u32[]{:S(2)}) collective-permute-start(bf16[24,128,128]{2,1,0:T(8,128)(2,1)} %bitcast.45), channel_id=1, source_target_pairs={{0,64},{32,96},{64,128},{96,160},{128,192},{160,224},{192,0},{224,... | collective-permute-start | bytes 2359304 | tf_op jit(solution)/shard_map/ppermute | solution.py:68
  11.2 87.4 %collective-permute-start.2 = (bf16[24,128,128]{2,1,0:T(8,128)(2,1)}, bf16[24,128,128]{2,1,0:T(8,128)(2,1)}, u32[]{:S(2)}, u32[]{:S(2)}) collective-permute-start(bf16[24,128,128]{2,1,0:T(8,128)(2,1)} %bitcast.46), channel_id=1, source_target_pairs={{0,96},{32,128},{64,160},{96,192},{128,224},{160,0},{192,32},{224,... | collective-permute-start | bytes 2359304 | tf_op jit(solution)/shard_map/ppermute | solution.py:68
  12.9 87.8 %collective-permute-start.3 = (bf16[24,128,128]{2,1,0:T(8,128)(2,1)}, bf16[24,128,128]{2,1,0:T(8,128)(2,1)S(1)}, u32[]{:S(2)}, u32[]{:S(2)}) collective-permute-start(bf16[24,128,128]{2,1,0:T(8,128)(2,1)} %bitcast.47), channel_id=1, source_target_pairs={{0,128},{32,160},{64,192},{96,224},{128,0},{160,32},{192,64},{224,... | collective-permute-start | bytes 2359304 | tf_op jit(solution)/shard_map/ppermute | solution.py:68
  14.2 87.4 %collective-permute-start.4 = (bf16[24,128,128]{2,1,0:T(8,128)(2,1)}, bf16[24,128,128]{2,1,0:T(8,128)(2,1)S(1)}, u32[]{:S(2)}, u32[]{:S(2)}) collective-permute-start(bf16[24,128,128]{2,1,0:T(8,128)(2,1)} %bitcast.48), channel_id=1, source_target_pairs={{0,160},{32,192},{64,224},{96,0},{128,32},{160,64},{192,96},{224,1... | collective-permute-start | bytes 2359304 | tf_op jit(solution)/shard_map/ppermute | solution.py:68
  83.7 5.2 %copy-start.2 = (s32[24,1,2]{0,2,1:T(2,128)S(1)}, s32[24,1,2]{0,2,1:T(2,128)}, u32[]{:S(2)}) copy-start(s32[24,1,2]{0,2,1:T(2,128)} %param.9) | copy-start | bytes 580
  83.7 5.6 %copy-start.3 = (s32[24,1]{0,1:T(1,128)S(1)}, s32[24,1]{0,1:T(1,128)}, u32[]{:S(2)}) copy-start(s32[24,1]{0,1:T(1,128)} %param.6) | copy-start | bytes 292
  83.7 5.9 %copy-start.1 = (bf16[24,1,128,128]{3,2,1,0:T(8,128)(2,1)S(1)}, bf16[24,1,128,128]{3,2,1,0:T(8,128)(2,1)}, u32[]{:S(2)}) copy-start(bf16[24,1,128,128]{3,2,1,0:T(8,128)(2,1)} %param.7) | copy-start | bytes 2359300
  88.7 118.0 %copy-start = (bf16[24,1,128,128]{3,2,1,0:T(8,128)(2,1)S(1)}, bf16[24,1,128,128]{3,2,1,0:T(8,128)(2,1)}, u32[]{:S(2)}) copy-start(bf16[24,1,128,128]{3,2,1,0:T(8,128)(2,1)} %param.5) | copy-start | bytes 2359300
  89.6 17.6 %collective-permute-start.5 = (bf16[24,128,128]{2,1,0:T(8,128)(2,1)S(1)}, bf16[24,128,128]{2,1,0:T(8,128)(2,1)S(1)}, u32[]{:S(2)}, u32[]{:S(2)}) collective-permute-start(bf16[24,128,128]{2,1,0:T(8,128)(2,1)S(1)} %bitcast.49), channel_id=1, source_target_pairs={{0,192},{32,224},{64,0},{96,32},{128,64},{160,96},{192,128},{224,1... | collective-permute-start | bytes 2359304 | tf_op jit(solution)/shard_map/ppermute | solution.py:68
  91.6 26.4 %collective-permute-start.6 = (bf16[24,128,128]{2,1,0:T(8,128)(2,1)S(1)}, bf16[24,128,128]{2,1,0:T(8,128)(2,1)S(1)}, u32[]{:S(2)}, u32[]{:S(2)}) collective-permute-start(bf16[24,128,128]{2,1,0:T(8,128)(2,1)S(1)} %bitcast.50), channel_id=1, source_target_pairs={{0,224},{32,0},{64,32},{96,64},{128,96},{160,128},{192,160},{224,1... | collective-permute-start | bytes 2359304 | tf_op jit(solution)/shard_map/ppermute | solution.py:68
Sparse Core Ops, SparseCore 0:
  9.8 196.8 all-gather.4

commit v10 on v6

--- a/solution.py
+++ b/solution.py
@@ -32,45 +32,52 @@
     )(krow, lookup)
 
 
+ROWS_PER_STEP = 4
+
+
 def _row_kernel(m0_ref, m1_ref, own_ref, y_ref, self_ref, stk_ref, out_ref, lhs_ref):
-    i = pl.program_id(0)
+    g = pl.program_id(0)
     tiles = y_ref.shape[0]
+    rb = y_ref.shape[1]
     bs = y_ref.shape[-1]
-    for tp in range(tiles):
-        at = i * tiles + tp
-        cols = slice(tp * bs, (tp + 1) * bs)
-        y = y_ref[tp, 0]
-        zero = jnp.zeros_like(y)
-        lhs_ref[0:bs, cols] = jnp.where(m0_ref[at] != 0, y, zero)
-        lhs_ref[bs:2 * bs, cols] = jnp.where(m1_ref[at] != 0, y, zero)
-    res = jnp.dot(lhs_ref[...], stk_ref[0], preferred_element_type=jnp.float32)
-    own = self_ref[0].astype(jnp.float32)
-    for w in range(2):
-        own_w = jnp.where(own_ref[2 * i + w] != 0, own, 0.0)
-        out_ref[0, w] = (1.5 * own_w - 0.5 * res[w * bs:(w + 1) * bs]).astype(out_ref.dtype)
+    for r in range(rb):
+        i = g * rb + r
+        for tp in range(tiles):
+            at = i * tiles + tp
+            cols = slice(tp * bs, (tp + 1) * bs)
+            y = y_ref[tp, r]
+            zero = jnp.zeros_like(y)
+            lhs_ref[0:bs, cols] = jnp.where(m0_ref[at] != 0, y, zero)
+            lhs_ref[bs:2 * bs, cols] = jnp.where(m1_ref[at] != 0, y, zero)
+        res = jnp.dot(lhs_ref[...], stk_ref[r], preferred_element_type=jnp.float32)
+        own = self_ref[r].astype(jnp.float32)
+        for w in range(2):
+            own_w = jnp.where(own_ref[2 * i + w] != 0, own, 0.0)
+            out_ref[r, w] = (1.5 * own_w - 0.5 * res[w * bs:(w + 1) * bs]).astype(out_ref.dtype)
 
 
 def _rows_product(m0, m1, own, left, own_blocks, stacked, out_width):
     tiles, block_rows, block_size, _ = left.shape
+    rb = ROWS_PER_STEP if block_rows % ROWS_PER_STEP == 0 else 1
     return pl.pallas_call(
         _row_kernel,
         out_shape=jax.ShapeDtypeStruct((block_rows, out_width, block_size, block_size), jnp.bfloat16),
         grid_spec=pltpu.PrefetchScalarGridSpec(
             num_scalar_prefetch=3,
-            grid=(block_rows,),
+            grid=(block_rows // rb,),
             in_specs=[
-                pl.BlockSpec((tiles, 1, block_size, block_size), lambda i, *_: (0, i, 0, 0)),
-                pl.BlockSpec((1, block_size, block_size), lambda i, *_: (i, 0, 0)),
-                pl.BlockSpec((1, tiles * block_size, block_size), lambda i, *_: (i, 0, 0)),
+                pl.BlockSpec((tiles, rb, block_size, block_size), lambda g, *_: (0, g, 0, 0)),
+                pl.BlockSpec((rb, block_size, block_size), lambda g, *_: (g, 0, 0)),
+                pl.BlockSpec((rb, tiles * block_size, block_size), lambda g, *_: (g, 0, 0)),
             ],
-            out_specs=pl.BlockSpec((1, out_width, block_size, block_size), lambda i, *_: (i, 0, 0, 0)),
+            out_specs=pl.BlockSpec((rb, out_width, block_size, block_size), lambda g, *_: (g, 0, 0, 0)),
             scratch_shapes=[
                 pltpu.VMEM((out_width * block_size, tiles * block_size), jnp.bfloat16),
             ],
         ),
         compiler_params=pltpu.CompilerParams(
             dimension_semantics=("arbitrary",),
-            vmem_limit_bytes=40 * 1024 * 1024,
+            vmem_limit_bytes=48 * 1024 * 1024,
         ),
     )(m0, m1, own, left, own_blocks, stacked)
 

time: 236 us -> 229 us (0.970)
  Pallas kernels: 45.5 us -> 38.7 us
    pallas_call x1, Pallas kernels: 31.7 us -> 24.9 us  [_rows_product(): pl.pallas_call(_row_kernel, out_shape=jax.ShapeDtypeStruct((block_rows, o...]
where the time goes in v10:
time: 229 us; the launch traced here: 228 us
  waiting for transfers between devices  78 us (34%)
  blocking collectives  56.3 us (25%)
  Pallas kernels  38.7 us (17%)
  local copies, waits for them, and re-layouts  26.1 us (11%)
  between operations  14.8 us (6%)
  starting transfers between devices  14.3 us (6%)
    all_gather x1, waiting for transfers between devices, shards(): lax.all_gather(y_blocks[:, 0], ('cols', 'layers'), axis=0, tiled=False)  62.1 us
    all_gather x1, blocking collectives, shards(): lookup_cols = lax.all_gather(prod_cols[:, 0], 'rows', axis=0, tiled=True)  37.6 us
    pallas_call x1, Pallas kernels, _rows_product(): pl.pallas_call(_row_kernel, out_shape=jax.ShapeDtypeStruct((block_rows, o...  24.9 us
    unnamed x1, blocking collectives  18.6 us
    unnamed x24, local copies, waits for them, and re-layouts  18.5 us
    ppermute x7, waiting for transfers between devices, shards(): lax.ppermute(prod_blocks[:, 0], 'rows', [(r, (r + s) % groups) for r in r...  15.2 us
    ppermute x7, starting transfers between devices, shards(): lax.ppermute(prod_blocks[:, 0], 'rows', [(r, (r + s) % groups) for r in r...  14.3 us
    pallas_call x1, Pallas kernels, _stack_rows(): pl.pallas_call(_stack_kernel, out_shape=jax.ShapeDtypeStruct((block_rows,...  13.9 us
  transfers between devices with their start and end apart: 8, of which 3 were waited for; matrix products, arithmetic and copies ran while one was open for 10% of the time, Pallas kernels for 6%

profile of v10, /device:TPU:1, one launch (start us, length us, event | category | flops | bytes accessed | tf_op | source)
XLA Modules:
  0.0 228.3 jit_solution(10851648087965396092)
XLA Ops:
  6.5 0.0 all-gather.5.cloned.1.call-start
  6.5 0.7 all-gather.5.cloned.1.call-update
  7.3 2.7 %collective-permute-start = (bf16[24,128,128]{2,1,0:T(8,128)(2,1)}, bf16[24,128,128]{2,1,0:T(8,128)(2,1)}, u32[]{:S(2)}, u32[]{:S(2)}) collective-permute-start(bf16[24,128,128]{2,1,0:T(8,128)(2,1)} %bitcast.38), channel_id=1, source_target_pairs={{0,32},{32,64},{64,96},{96,128},{128,160},{160,192},{192,224},{224... | collective-permute-start | bytes 2359304 | tf_op jit(solution)/shard_map/ppermute | solution.py:94
  9.9 1.3 collective-permute-start.1
  11.2 1.7 collective-permute-start.2
  12.9 1.3 collective-permute-start.3
  14.2 2.6 %collective-permute-start.4 = (bf16[24,128,128]{2,1,0:T(8,128)(2,1)}, bf16[24,128,128]{2,1,0:T(8,128)(2,1)S(1)}, u32[]{:S(2)}, u32[]{:S(2)}) collective-permute-start(bf16[24,128,128]{2,1,0:T(8,128)(2,1)} %bitcast.42), channel_id=1, source_target_pairs={{0,160},{32,192},{64,224},{96,0},{128,32},{160,64},{192,96},{224,1... | collective-permute-start | bytes 2359304 | tf_op jit(solution)/shard_map/ppermute | solution.py:94
  16.8 1.3 dynamic-slice.1
  18.8 0.8 bitcast_dynamic-update-slice_fusion.1
  19.5 18.6 %all-reduce.1 = s32[768]{0:T(1024)S(1)} all-reduce(s32[768]{0:T(1024)S(1)} %bitcast_dynamic-update-slice_fusion.1), channel_id=3, replica_groups=mesh['rows'=8,'cols'=8,'layers'=4] {'cols','layers'}, use_global_device_ids=true, to_apply=%add.1 | all-reduce | flops 768 | bytes 6144
  38.2 0.1 reshape.32
  38.3 1.3 dynamic-slice
  40.2 2.2 constant_dynamic-update-slice_fusion.7
  42.4 0.7 bitcast_dynamic-update-slice_fusion
  43.1 37.6 %all-reduce = s32[192]{0:T(256)S(1)} all-reduce(s32[192]{0:T(256)S(1)} %bitcast_dynamic-update-slice_fusion), channel_id=2, replica_groups=mesh['rows'=8,'cols'=8,'layers'=4] {'rows'}, use_global_device_ids=true, to_apply=%add | all-reduce | flops 192 | bytes 1536 | tf_op jit(solution)/shard_map/all_gather | solution.py:96
  80.8 0.1 copy.12
  80.8 0.1 reshape.25
  80.9 0.8 slice_bitcast_fusion
  81.7 0.0 copy-start.3
  81.7 0.0 copy-start.4
  81.7 0.0 copy-start.2
  81.7 5.0 %gather_fusion = s32[768]{0:T(1024)S(1)} fusion(s32[192]{0:T(256)S(1)} %all-reduce, s32[1024]{0:T(1024)S(1)} %pad_clamp_fusion), kind=kCustom, calls=%fused_computation | custom fusion | bytes 9216 | tf_op jit(solution)/shard_map/gather | solution.py:99
  86.7 0.1 reshape.24
  86.8 0.1 compare_convert_fusion
  86.8 0.0 copy-done.3
  86.8 0.1 copy.13
  86.9 0.1 copy.14
  87.0 0.1 reshape.20.krow_ref
  87.1 0.1 reshape.21.m0_ref
  87.1 0.1 reshape.22.m1_ref
  87.2 0.0 copy-done.4
  87.2 0.1 eq.47
  87.3 0.1 eq.48
  87.4 0.1 squeeze.9
  87.5 0.0 collective-permute-done
  87.5 0.0 copy-done.2
  87.5 2.5 %collective-permute-start.5 = (bf16[24,128,128]{2,1,0:T(8,128)(2,1)S(1)}, bf16[24,128,128]{2,1,0:T(8,128)(2,1)S(1)}, u32[]{:S(2)}, u32[]{:S(2)}) collective-permute-start(bf16[24,128,128]{2,1,0:T(8,128)(2,1)S(1)} %bitcast.43), channel_id=1, source_target_pairs={{0,192},{32,224},{64,0},{96,32},{128,64},{160,96},{192,128},{224,1... | collective-permute-start | bytes 2359304 | tf_op jit(solution)/shard_map/ppermute | solution.py:94
  90.0 0.0 collective-permute-done.1
  90.0 2.2 collective-permute-start.6
  92.2 2.1 constant_dynamic-update-slice_fusion.6
  94.4 2.1 constant_dynamic-update-slice_fusion.5
  96.5 0.0 collective-permute-done.2
  96.5 2.1 constant_dynamic-update-slice_fusion.4
  98.6 0.0 collective-permute-done.3
  98.6 1.0 constant_dynamic-update-slice_fusion.3
  99.6 0.0 collective-permute-done.4
  99.6 1.0 constant_dynamic-update-slice_fusion.2
  100.6 6.1 %collective-permute-done.5 = bf16[24,128,128]{2,1,0:T(8,128)(2,1)S(1)} collective-permute-done((bf16[24,128,128]{2,1,0:T(8,128)(2,1)S(1)}, bf16[24,128,128]{2,1,0:T(8,128)(2,1)S(1)}, u32[]{:S(2)}, u32[]{:S(2)}) %collective-permute-start.5) | collective-permute-done | bytes 786464 | tf_op jit(solution)/shard_map/ppermute | solution.py:94
  106.7 1.0 constant_dynamic-update-slice_fusion.1
  107.6 9.1 %collective-permute-done.6 = bf16[24,128,128]{2,1,0:T(8,128)(2,1)S(1)} collective-permute-done((bf16[24,128,128]{2,1,0:T(8,128)(2,1)S(1)}, bf16[24,128,128]{2,1,0:T(8,128)(2,1)S(1)}, u32[]{:S(2)}, u32[]{:S(2)}) %collective-permute-start.6) | collective-permute-done | bytes 786464 | tf_op jit(solution)/shard_map/ppermute | solution.py:94
  116.7 0.9 constant_dynamic-update-slice_fusion.lookup_ref
  117.7 0.0 copy-start
  117.7 2.9 %copy-done = bf16[192,128,128]{2,1,0:T(8,128)(2,1)S(1)} copy-done((bf16[192,128,128]{2,1,0:T(8,128)(2,1)S(1)}, bf16[192,128,128]{2,1,0:T(8,128)(2,1)}, u32[]{:S(2)}) %copy-start) | copy-done | bytes 6291480
  120.6 0.0 copy-start.1
  120.6 13.9 %shard_map.55.stk_ref = bf16[24,4096,128]{2,1,0:T(8,128)(2,1)} custom-call(s32[768]{0:T(1024)S(1)} %reshape.20.krow_ref, bf16[192,128,128]{2,1,0:T(8,128)(2,1)S(1)} %copy-done), custom_call_target="tpu_custom_call" | custom-call | tf_op jit(solution)/shard_map/pallas_call | solution.py:19
  134.5 62.1 %all-gather.5.cloned.1.call-done = bf16[768,1,128,128]{3,2,1,0:T(8,128)(2,1)} async-done(((bf16[24,1,128,128]{3,2,1,0:T(8,128)(2,1)}), bf16[768,1,128,128]{3,2,1,0:T(8,128)(2,1)}) %all-gather.5.cloned.1.call-update) | async-done | bytes 25165840 | tf_op jit(solution)/shard_map/all_gather | solution.py:109
  196.6 0.0 copy-done.1
  196.6 24.9 %shard_map.56 = bf16[24,2,128,128]{3,2,1,0:T(8,128)(2,1)} custom-call(s32[768]{0:T(1024)S(1)} %reshape.21.m0_ref, s32[768]{0:T(1024)S(1)} %reshape.22.m1_ref, s32[48]{0:T(128)S(1)} %compare_convert_fusion.2.own_ref, bf16[32,24,128,128]{3,2,1,0:T(8,128)(2,1)} %bitcast.37, bf16[24,128,128]{2,1,0:T(8,128)(2,1)S(1)} %bitcast.36, ...), custom_call_target="tpu_custom_call" | custom-call | tf_op jit(solution)/shard_map/pallas_call | solution.py:62
  (5 shorter events, 0.0 us)
Async XLA Ops:
  6.5 190.1 %all-gather.5.cloned.1.call-start = ((), (), s32[]{:S(2)}) async-start(), calls=%async_computation | async-start | bytes 25952256 | tf_op jit(solution)/shard_map/all_gather | solution.py:109
  7.3 80.2 %collective-permute-start = (bf16[24,128,128]{2,1,0:T(8,128)(2,1)}, bf16[24,128,128]{2,1,0:T(8,128)(2,1)}, u32[]{:S(2)}, u32[]{:S(2)}) collective-permute-start(bf16[24,128,128]{2,1,0:T(8,128)(2,1)} %bitcast.38), channel_id=1, source_target_pairs={{0,32},{32,64},{64,96},{96,128},{128,160},{160,192},{192,224},{224... | collective-permute-start | bytes 2359304 | tf_op jit(solution)/shard_map/ppermute | solution.py:94
  9.9 80.1 %collective-permute-start.1 = (bf16[24,128,128]{2,1,0:T(8,128)(2,1)}, bf16[24,128,128]{2,1,0:T(8,128)(2,1)}, u32[]{:S(2)}, u32[]{:S(2)}) collective-permute-start(bf16[24,128,128]{2,1,0:T(8,128)(2,1)} %bitcast.39), channel_id=1, source_target_pairs={{0,64},{32,96},{64,128},{96,160},{128,192},{160,224},{192,0},{224,... | collective-permute-start | bytes 2359304 | tf_op jit(solution)/shard_map/ppermute | solution.py:94
  11.2 85.3 %collective-permute-start.2 = (bf16[24,128,128]{2,1,0:T(8,128)(2,1)}, bf16[24,128,128]{2,1,0:T(8,128)(2,1)}, u32[]{:S(2)}, u32[]{:S(2)}) collective-permute-start(bf16[24,128,128]{2,1,0:T(8,128)(2,1)} %bitcast.40), channel_id=1, source_target_pairs={{0,96},{32,128},{64,160},{96,192},{128,224},{160,0},{192,32},{224,... | collective-permute-start | bytes 2359304 | tf_op jit(solution)/shard_map/ppermute | solution.py:94
  12.9 85.7 %collective-permute-start.3 = (bf16[24,128,128]{2,1,0:T(8,128)(2,1)}, bf16[24,128,128]{2,1,0:T(8,128)(2,1)S(1)}, u32[]{:S(2)}, u32[]{:S(2)}) collective-permute-start(bf16[24,128,128]{2,1,0:T(8,128)(2,1)} %bitcast.41), channel_id=1, source_target_pairs={{0,128},{32,160},{64,192},{96,224},{128,0},{160,32},{192,64},{224,... | collective-permute-start | bytes 2359304 | tf_op jit(solution)/shard_map/ppermute | solution.py:94
  14.2 85.4 %collective-permute-start.4 = (bf16[24,128,128]{2,1,0:T(8,128)(2,1)}, bf16[24,128,128]{2,1,0:T(8,128)(2,1)S(1)}, u32[]{:S(2)}, u32[]{:S(2)}) collective-permute-start(bf16[24,128,128]{2,1,0:T(8,128)(2,1)} %bitcast.42), channel_id=1, source_target_pairs={{0,160},{32,192},{64,224},{96,0},{128,32},{160,64},{192,96},{224,1... | collective-permute-start | bytes 2359304 | tf_op jit(solution)/shard_map/ppermute | solution.py:94
  81.7 5.2 %copy-start.3 = (s32[24,1,2]{0,2,1:T(2,128)S(1)}, s32[24,1,2]{0,2,1:T(2,128)}, u32[]{:S(2)}) copy-start(s32[24,1,2]{0,2,1:T(2,128)} %param.9) | copy-start | bytes 580
  81.7 5.5 %copy-start.4 = (s32[24,1]{0,1:T(1,128)S(1)}, s32[24,1]{0,1:T(1,128)}, u32[]{:S(2)}) copy-start(s32[24,1]{0,1:T(1,128)} %param.6) | copy-start | bytes 292
  81.7 5.8 %copy-start.2 = (bf16[24,1,128,128]{3,2,1,0:T(8,128)(2,1)S(1)}, bf16[24,1,128,128]{3,2,1,0:T(8,128)(2,1)}, u32[]{:S(2)}) copy-start(bf16[24,1,128,128]{3,2,1,0:T(8,128)(2,1)} %param.7) | copy-start | bytes 2359300
  87.5 19.1 %collective-permute-start.5 = (bf16[24,128,128]{2,1,0:T(8,128)(2,1)S(1)}, bf16[24,128,128]{2,1,0:T(8,128)(2,1)S(1)}, u32[]{:S(2)}, u32[]{:S(2)}) collective-permute-start(bf16[24,128,128]{2,1,0:T(8,128)(2,1)S(1)} %bitcast.43), channel_id=1, source_target_pairs={{0,192},{32,224},{64,0},{96,32},{128,64},{160,96},{192,128},{224,1... | collective-permute-start | bytes 2359304 | tf_op jit(solution)/shard_map/ppermute | solution.py:94
  90.0 26.7 %collective-permute-start.6 = (bf16[24,128,128]{2,1,0:T(8,128)(2,1)S(1)}, bf16[24,128,128]{2,1,0:T(8,128)(2,1)S(1)}, u32[]{:S(2)}, u32[]{:S(2)}) collective-permute-start(bf16[24,128,128]{2,1,0:T(8,128)(2,1)S(1)} %bitcast.44), channel_id=1, source_target_pairs={{0,224},{32,0},{64,32},{96,64},{128,96},{160,128},{192,160},{224,1... | collective-permute-start | bytes 2359304 | tf_op jit(solution)/shard_map/ppermute | solution.py:94
  117.7 2.9 %copy-start = (bf16[192,128,128]{2,1,0:T(8,128)(2,1)S(1)}, bf16[192,128,128]{2,1,0:T(8,128)(2,1)}, u32[]{:S(2)}) copy-start(bf16[192,128,128]{2,1,0:T(8,128)(2,1)} %constant_dynamic-update-slice_fusion.lookup_ref) | copy-start | bytes 18874372
  120.6 76.0 %copy-start.1 = (bf16[24,1,128,128]{3,2,1,0:T(8,128)(2,1)S(1)}, bf16[24,1,128,128]{3,2,1,0:T(8,128)(2,1)}, u32[]{:S(2)}) copy-start(bf16[24,1,128,128]{3,2,1,0:T(8,128)(2,1)} %param.5) | copy-start | bytes 2359300
Sparse Core Ops, SparseCore 0:
  9.9 186.6 all-gather.4

commit v11 on v8

--- a/solution.py
+++ b/solution.py
@@ -6,7 +6,7 @@
 from jax.sharding import PartitionSpec as P
 
 
-ROWS_PER_STEP = 4
+ROWS_PER_STEP = 3
 
 
 def _row_kernel(i0_ref, i1_ref, own_ref, y_ref, self_ref, lookup_ref, out_ref, lhs_ref, stk_ref):

time: 228 us -> 230 us (level)
  no operation moved by 1% of the time
where the time goes in v11:
time: 230 us; the launch traced here: 229 us
  waiting for transfers between devices  92.2 us (40%)
  blocking collectives  58.3 us (25%)
  Pallas kernels  26.1 us (11%)
  local copies, waits for them, and re-layouts  23.8 us (10%)
  between operations  14.8 us (6%)
  starting transfers between devices  14.3 us (6%)
    all_gather x1, waiting for transfers between devices, shards(): lax.all_gather(y_blocks[:, 0], ('cols', 'layers'), axis=0, tiled=False)  76.2 us
    all_gather x1, blocking collectives, shards(): lookup_cols = lax.all_gather(prod_cols[:, 0], 'rows', axis=0, tiled=True)  39.7 us
    pallas_call x1, Pallas kernels, _rows_product(): pl.pallas_call(_row_kernel, out_shape=jax.ShapeDtypeStruct((block_rows, o...  26.1 us
    unnamed x1, blocking collectives  18.6 us
    unnamed x23, local copies, waits for them, and re-layouts  16.6 us
    ppermute x7, waiting for transfers between devices, shards(): lax.ppermute(prod_blocks[:, 0], 'rows', [(r, (r + s) % groups) for r in r...  15.2 us
    ppermute x7, starting transfers between devices, shards(): lax.ppermute(prod_blocks[:, 0], 'rows', [(r, (r + s) % groups) for r in r...  14.3 us
    gather x3, local copies, waits for them, and re-layouts, shards(): right_cols = lookup_cols[left_cols]  5.13 us
  transfers between devices with their start and end apart: 8, of which 3 were waited for; matrix products, arithmetic and copies ran while one was open for 10% of the time, Pallas kernels for 0%

profile of v11, /device:TPU:1, one launch (start us, length us, event | category | flops | bytes accessed | tf_op | source)
XLA Modules:
  0.0 229.5 jit_solution(3628711038184589989)
XLA Ops:
  6.5 0.0 all-gather.5.cloned.1.call-start
  6.5 0.7 all-gather.5.cloned.1.call-update
  7.3 2.7 %collective-permute-start = (bf16[24,128,128]{2,1,0:T(8,128)(2,1)}, bf16[24,128,128]{2,1,0:T(8,128)(2,1)}, u32[]{:S(2)}, u32[]{:S(2)}) collective-permute-start(bf16[24,128,128]{2,1,0:T(8,128)(2,1)} %bitcast.42), channel_id=1, source_target_pairs={{0,32},{32,64},{64,96},{96,128},{128,160},{160,192},{192,224},{224... | collective-permute-start | bytes 2359304 | tf_op jit(solution)/shard_map/ppermute | solution.py:69
  9.9 1.3 collective-permute-start.1
  11.2 1.7 collective-permute-start.2
  12.9 1.3 collective-permute-start.3
  14.2 2.6 %collective-permute-start.4 = (bf16[24,128,128]{2,1,0:T(8,128)(2,1)}, bf16[24,128,128]{2,1,0:T(8,128)(2,1)S(1)}, u32[]{:S(2)}, u32[]{:S(2)}) collective-permute-start(bf16[24,128,128]{2,1,0:T(8,128)(2,1)} %bitcast.46), channel_id=1, source_target_pairs={{0,160},{32,192},{64,224},{96,0},{128,32},{160,64},{192,96},{224,1... | collective-permute-start | bytes 2359304 | tf_op jit(solution)/shard_map/ppermute | solution.py:69
  16.8 1.3 dynamic-slice.1
  18.8 0.8 bitcast_dynamic-update-slice_fusion.1
  19.5 18.6 %all-reduce.1 = s32[768]{0:T(1024)S(1)} all-reduce(s32[768]{0:T(1024)S(1)} %bitcast_dynamic-update-slice_fusion.1), channel_id=3, replica_groups=mesh['rows'=8,'cols'=8,'layers'=4] {'cols','layers'}, use_global_device_ids=true, to_apply=%add.1 | all-reduce | flops 768 | bytes 6144
  38.2 0.1 reshape.22
  38.3 0.1 copy.15
  38.3 0.1 reshape.15
  38.4 1.3 dynamic-slice
  40.3 0.8 bitcast_dynamic-update-slice_fusion
  41.1 39.7 %all-reduce = s32[192]{0:T(256)S(1)} all-reduce(s32[192]{0:T(256)S(1)} %bitcast_dynamic-update-slice_fusion), channel_id=2, replica_groups=mesh['rows'=8,'cols'=8,'layers'=4] {'rows'}, use_global_device_ids=true, to_apply=%add | all-reduce | flops 192 | bytes 1536 | tf_op jit(solution)/shard_map/all_gather | solution.py:73
  80.8 2.2 constant_dynamic-update-slice_fusion.8
  82.9 0.8 slice_bitcast_fusion
  83.7 0.0 copy-start.2
  83.7 0.0 copy-start.3
  83.7 0.0 copy-start.1
  83.7 5.0 %gather_fusion = s32[768]{0:T(1024)S(1)} fusion(s32[192]{0:T(256)S(1)} %all-reduce, s32[1024]{0:T(1024)S(1)} %pad_clamp_fusion), kind=kCustom, calls=%fused_computation | custom fusion | bytes 9216 | tf_op jit(solution)/shard_map/gather | solution.py:76
  88.7 0.0 copy-start
  88.7 0.1 reshape.14
  88.8 0.1 copy.16
  88.9 0.0 copy-done.2
  88.9 0.1 copy.20
  89.0 0.1 copy.17
  89.1 0.1 reshape.11.i0_ref
  89.1 0.1 copy.19
  89.2 0.1 reshape.12.i1_ref
  89.3 0.0 copy-done.3
  89.3 0.1 eq.43
  89.4 0.1 eq.44
  89.5 0.1 squeeze.9
  89.6 0.0 collective-permute-done
  89.6 0.0 copy-done.1
  89.6 2.5 %collective-permute-start.5 = (bf16[24,128,128]{2,1,0:T(8,128)(2,1)S(1)}, bf16[24,128,128]{2,1,0:T(8,128)(2,1)S(1)}, u32[]{:S(2)}, u32[]{:S(2)}) collective-permute-start(bf16[24,128,128]{2,1,0:T(8,128)(2,1)S(1)} %bitcast.47), channel_id=1, source_target_pairs={{0,192},{32,224},{64,0},{96,32},{128,64},{160,96},{192,128},{224,1... | collective-permute-start | bytes 2359304 | tf_op jit(solution)/shard_map/ppermute | solution.py:69
  92.1 0.0 collective-permute-done.1
  92.1 2.2 collective-permute-start.6
  94.3 2.1 constant_dynamic-update-slice_fusion.7
  96.4 2.1 constant_dynamic-update-slice_fusion.6
  98.5 0.0 collective-permute-done.2
  98.5 2.1 constant_dynamic-update-slice_fusion.5
  100.6 0.0 collective-permute-done.3
  100.6 1.0 constant_dynamic-update-slice_fusion.4
  101.6 0.0 collective-permute-done.4
  101.6 1.0 constant_dynamic-update-slice_fusion.3
  102.6 6.1 %collective-permute-done.5 = bf16[24,128,128]{2,1,0:T(8,128)(2,1)S(1)} collective-permute-done((bf16[24,128,128]{2,1,0:T(8,128)(2,1)S(1)}, bf16[24,128,128]{2,1,0:T(8,128)(2,1)S(1)}, u32[]{:S(2)}, u32[]{:S(2)}) %collective-permute-start.5) | collective-permute-done | bytes 786464 | tf_op jit(solution)/shard_map/ppermute | solution.py:69
  108.7 1.0 constant_dynamic-update-slice_fusion.2
  109.7 9.1 %collective-permute-done.6 = bf16[24,128,128]{2,1,0:T(8,128)(2,1)S(1)} collective-permute-done((bf16[24,128,128]{2,1,0:T(8,128)(2,1)S(1)}, bf16[24,128,128]{2,1,0:T(8,128)(2,1)S(1)}, u32[]{:S(2)}, u32[]{:S(2)}) %collective-permute-start.6) | collective-permute-done | bytes 786464 | tf_op jit(solution)/shard_map/ppermute | solution.py:69
  118.8 1.0 constant_dynamic-update-slice_fusion.1
  119.8 0.6 constant_dynamic-update-slice_fusion.lookup_ref
  120.4 76.2 %all-gather.5.cloned.1.call-done = bf16[768,1,128,128]{3,2,1,0:T(8,128)(2,1)} async-done(((bf16[24,1,128,128]{3,2,1,0:T(8,128)(2,1)}), bf16[768,1,128,128]{3,2,1,0:T(8,128)(2,1)}) %all-gather.5.cloned.1.call-update) | async-done | bytes 25165840 | tf_op jit(solution)/shard_map/all_gather | solution.py:83
  196.6 0.0 copy-done
  196.6 26.1 %shard_map.55 = bf16[24,2,128,128]{3,2,1,0:T(8,128)(2,1)} custom-call(s32[768]{0:T(1024)S(1)} %reshape.11.i0_ref, s32[768]{0:T(1024)S(1)} %reshape.12.i1_ref, s32[48]{0:T(128)S(1)} %compare_convert_fusion.own_ref, bf16[32,24,128,128]{3,2,1,0:T(8,128)(2,1)} %bitcast.41, bf16[24,128,128]{2,1,0:T(8,128)(2,1)S(1)} %bitcast.40, ...), custom_call_target="tpu_custom_call" | custom-call | tf_op jit(solution)/shard_map/pallas_call | solution.py:36
  (6 shorter events, 0.1 us)
Async XLA Ops:
  6.5 190.1 %all-gather.5.cloned.1.call-start = ((), (), s32[]{:S(2)}) async-start(), calls=%async_computation | async-start | bytes 25952256 | tf_op jit(solution)/shard_map/all_gather | solution.py:83
  7.3 82.3 %collective-permute-start = (bf16[24,128,128]{2,1,0:T(8,128)(2,1)}, bf16[24,128,128]{2,1,0:T(8,128)(2,1)}, u32[]{:S(2)}, u32[]{:S(2)}) collective-permute-start(bf16[24,128,128]{2,1,0:T(8,128)(2,1)} %bitcast.42), channel_id=1, source_target_pairs={{0,32},{32,64},{64,96},{96,128},{128,160},{160,192},{192,224},{224... | collective-permute-start | bytes 2359304 | tf_op jit(solution)/shard_map/ppermute | solution.py:69
  9.9 82.1 %collective-permute-start.1 = (bf16[24,128,128]{2,1,0:T(8,128)(2,1)}, bf16[24,128,128]{2,1,0:T(8,128)(2,1)}, u32[]{:S(2)}, u32[]{:S(2)}) collective-permute-start(bf16[24,128,128]{2,1,0:T(8,128)(2,1)} %bitcast.43), channel_id=1, source_target_pairs={{0,64},{32,96},{64,128},{96,160},{128,192},{160,224},{192,0},{224,... | collective-permute-start | bytes 2359304 | tf_op jit(solution)/shard_map/ppermute | solution.py:69
  11.2 87.3 %collective-permute-start.2 = (bf16[24,128,128]{2,1,0:T(8,128)(2,1)}, bf16[24,128,128]{2,1,0:T(8,128)(2,1)}, u32[]{:S(2)}, u32[]{:S(2)}) collective-permute-start(bf16[24,128,128]{2,1,0:T(8,128)(2,1)} %bitcast.44), channel_id=1, source_target_pairs={{0,96},{32,128},{64,160},{96,192},{128,224},{160,0},{192,32},{224,... | collective-permute-start | bytes 2359304 | tf_op jit(solution)/shard_map/ppermute | solution.py:69
  12.9 87.7 %collective-permute-start.3 = (bf16[24,128,128]{2,1,0:T(8,128)(2,1)}, bf16[24,128,128]{2,1,0:T(8,128)(2,1)S(1)}, u32[]{:S(2)}, u32[]{:S(2)}) collective-permute-start(bf16[24,128,128]{2,1,0:T(8,128)(2,1)} %bitcast.45), channel_id=1, source_target_pairs={{0,128},{32,160},{64,192},{96,224},{128,0},{160,32},{192,64},{224,... | collective-permute-start | bytes 2359304 | tf_op jit(solution)/shard_map/ppermute | solution.py:69
  14.2 87.4 %collective-permute-start.4 = (bf16[24,128,128]{2,1,0:T(8,128)(2,1)}, bf16[24,128,128]{2,1,0:T(8,128)(2,1)S(1)}, u32[]{:S(2)}, u32[]{:S(2)}) collective-permute-start(bf16[24,128,128]{2,1,0:T(8,128)(2,1)} %bitcast.46), channel_id=1, source_target_pairs={{0,160},{32,192},{64,224},{96,0},{128,32},{160,64},{192,96},{224,1... | collective-permute-start | bytes 2359304 | tf_op jit(solution)/shard_map/ppermute | solution.py:69
  83.7 5.2 %copy-start.2 = (s32[24,1,2]{0,2,1:T(2,128)S(1)}, s32[24,1,2]{0,2,1:T(2,128)}, u32[]{:S(2)}) copy-start(s32[24,1,2]{0,2,1:T(2,128)} %param.9) | copy-start | bytes 580
  83.7 5.6 %copy-start.3 = (s32[24,1]{0,1:T(1,128)S(1)}, s32[24,1]{0,1:T(1,128)}, u32[]{:S(2)}) copy-start(s32[24,1]{0,1:T(1,128)} %param.6) | copy-start | bytes 292
  83.7 5.9 %copy-start.1 = (bf16[24,1,128,128]{3,2,1,0:T(8,128)(2,1)S(1)}, bf16[24,1,128,128]{3,2,1,0:T(8,128)(2,1)}, u32[]{:S(2)}) copy-start(bf16[24,1,128,128]{3,2,1,0:T(8,128)(2,1)} %param.7) | copy-start | bytes 2359300
  88.7 107.9 %copy-start = (bf16[24,1,128,128]{3,2,1,0:T(8,128)(2,1)S(1)}, bf16[24,1,128,128]{3,2,1,0:T(8,128)(2,1)}, u32[]{:S(2)}) copy-start(bf16[24,1,128,128]{3,2,1,0:T(8,128)(2,1)} %param.5) | copy-start | bytes 2359300
  89.6 19.1 %collective-permute-start.5 = (bf16[24,128,128]{2,1,0:T(8,128)(2,1)S(1)}, bf16[24,128,128]{2,1,0:T(8,128)(2,1)S(1)}, u32[]{:S(2)}, u32[]{:S(2)}) collective-permute-start(bf16[24,128,128]{2,1,0:T(8,128)(2,1)S(1)} %bitcast.47), channel_id=1, source_target_pairs={{0,192},{32,224},{64,0},{96,32},{128,64},{160,96},{192,128},{224,1... | collective-permute-start | bytes 2359304 | tf_op jit(solution)/shard_map/ppermute | solution.py:69
  92.1 26.7 %collective-permute-start.6 = (bf16[24,128,128]{2,1,0:T(8,128)(2,1)S(1)}, bf16[24,128,128]{2,1,0:T(8,128)(2,1)S(1)}, u32[]{:S(2)}, u32[]{:S(2)}) collective-permute-start(bf16[24,128,128]{2,1,0:T(8,128)(2,1)S(1)} %bitcast.48), channel_id=1, source_target_pairs={{0,224},{32,0},{64,32},{96,64},{128,96},{160,128},{192,160},{224,1... | collective-permute-start | bytes 2359304 | tf_op jit(solution)/shard_map/ppermute | solution.py:69
Sparse Core Ops, SparseCore 0:
  9.9 186.6 all-gather.4

commit v12 on v8

--- a/solution.py
+++ b/solution.py
@@ -9,19 +9,25 @@
 ROWS_PER_STEP = 4
 
 
-def _row_kernel(i0_ref, i1_ref, own_ref, y_ref, self_ref, lookup_ref, out_ref, lhs_ref, stk_ref):
+def _row_kernel(i0_ref, i1_ref, own_ref, y_ref, self_ref, lookup_ref, out_ref, lhs_ref, stk_ref, sems):
     g = pl.program_id(0)
     tiles = y_ref.shape[0]
     rb = y_ref.shape[1]
     bs = y_ref.shape[-1]
     for r in range(rb):
         i = g * rb + r
+        copies = []
+        for tp in range(tiles):
+            copy = pltpu.make_async_copy(y_ref.at[tp, r], lhs_ref.at[:, pl.ds(tp * bs, bs)], sems.at[tp])
+            copy.start()
+            copies.append(copy)
         for tp in range(tiles):
             at = i * tiles + tp
             cols = slice(tp * bs, (tp + 1) * bs)
-            lhs_ref[:, cols] = y_ref[tp, r]
             stk_ref[cols, 0:bs] = lookup_ref[i0_ref[at]]
             stk_ref[cols, bs:2 * bs] = lookup_ref[i1_ref[at]]
+        for copy in copies:
+            copy.wait()
         res = jnp.dot(lhs_ref[...], stk_ref[...], preferred_element_type=jnp.float32)
         own = self_ref[r].astype(jnp.float32)
         for w in range(2):
@@ -48,6 +54,7 @@
             scratch_shapes=[
                 pltpu.VMEM((block_size, tiles * block_size), jnp.bfloat16),
                 pltpu.VMEM((tiles * block_size, out_width * block_size), jnp.bfloat16),
+                pltpu.SemaphoreType.DMA((tiles,)),
             ],
         ),
         compiler_params=pltpu.CompilerParams(

time: 228 us -> 244 us (1.070)
  Pallas kernels: 24.6 us -> 39.8 us
    pallas_call x1, Pallas kernels: 24.6 us -> 39.8 us  [_rows_product(): pl.pallas_call(_row_kernel, out_shape=jax.ShapeDtypeStruct((block_rows, o...]
where the time goes in v12:
time: 244 us; the launch traced here: 243 us
  waiting for transfers between devices  92.2 us (38%)
  blocking collectives  58.3 us (24%)
  Pallas kernels  39.8 us (16%)
  local copies, waits for them, and re-layouts  23.8 us (10%)
  between operations  14.8 us (6%)
  starting transfers between devices  14.3 us (6%)
    all_gather x1, waiting for transfers between devices, shards(): lax.all_gather(y_blocks[:, 0], ('cols', 'layers'), axis=0, tiled=False)  76.2 us
    pallas_call x1, Pallas kernels, _rows_product(): pl.pallas_call(_row_kernel, out_shape=jax.ShapeDtypeStruct((block_rows, o...  39.8 us
    all_gather x1, blocking collectives, shards(): lookup_cols = lax.all_gather(prod_cols[:, 0], 'rows', axis=0, tiled=True)  39.7 us
    unnamed x1, blocking collectives  18.6 us
    unnamed x23, local copies, waits for them, and re-layouts  16.6 us
    ppermute x7, waiting for transfers between devices, shards(): lax.ppermute(prod_blocks[:, 0], 'rows', [(r, (r + s) % groups) for r in r...  15.2 us
    ppermute x7, starting transfers between devices, shards(): lax.ppermute(prod_blocks[:, 0], 'rows', [(r, (r + s) % groups) for r in r...  14.3 us
    gather x3, local copies, waits for them, and re-layouts, shards(): right_cols = lookup_cols[left_cols]  5.13 us
  transfers between devices with their start and end apart: 8, of which 3 were waited for; matrix products, arithmetic and copies ran while one was open for 10% of the time, Pallas kernels for 0%

profile of v12, /device:TPU:1, one launch (start us, length us, event | category | flops | bytes accessed | tf_op | source)
XLA Modules:
  0.0 243.3 jit_solution(17536464600214741927)
XLA Ops:
  6.5 0.0 all-gather.5.cloned.1.call-start
  6.5 0.7 all-gather.5.cloned.1.call-update
  7.3 2.7 %collective-permute-start = (bf16[24,128,128]{2,1,0:T(8,128)(2,1)}, bf16[24,128,128]{2,1,0:T(8,128)(2,1)}, u32[]{:S(2)}, u32[]{:S(2)}) collective-permute-start(bf16[24,128,128]{2,1,0:T(8,128)(2,1)} %bitcast.42), channel_id=1, source_target_pairs={{0,32},{32,64},{64,96},{96,128},{128,160},{160,192},{192,224},{224... | collective-permute-start | bytes 2359304 | tf_op jit(solution)/shard_map/ppermute | solution.py:76
  9.9 1.3 collective-permute-start.1
  11.2 1.7 collective-permute-start.2
  12.9 1.3 collective-permute-start.3
  14.2 2.6 %collective-permute-start.4 = (bf16[24,128,128]{2,1,0:T(8,128)(2,1)}, bf16[24,128,128]{2,1,0:T(8,128)(2,1)S(1)}, u32[]{:S(2)}, u32[]{:S(2)}) collective-permute-start(bf16[24,128,128]{2,1,0:T(8,128)(2,1)} %bitcast.46), channel_id=1, source_target_pairs={{0,160},{32,192},{64,224},{96,0},{128,32},{160,64},{192,96},{224,1... | collective-permute-start | bytes 2359304 | tf_op jit(solution)/shard_map/ppermute | solution.py:76
  16.8 1.3 dynamic-slice.1
  18.8 0.8 bitcast_dynamic-update-slice_fusion.1
  19.5 18.6 %all-reduce.1 = s32[768]{0:T(1024)S(1)} all-reduce(s32[768]{0:T(1024)S(1)} %bitcast_dynamic-update-slice_fusion.1), channel_id=3, replica_groups=mesh['rows'=8,'cols'=8,'layers'=4] {'cols','layers'}, use_global_device_ids=true, to_apply=%add.1 | all-reduce | flops 768 | bytes 6144
  38.2 0.1 reshape.22
  38.3 0.1 copy.15
  38.3 0.1 reshape.15
  38.4 1.3 dynamic-slice
  40.3 0.8 bitcast_dynamic-update-slice_fusion
  41.1 39.7 %all-reduce = s32[192]{0:T(256)S(1)} all-reduce(s32[192]{0:T(256)S(1)} %bitcast_dynamic-update-slice_fusion), channel_id=2, replica_groups=mesh['rows'=8,'cols'=8,'layers'=4] {'rows'}, use_global_device_ids=true, to_apply=%add | all-reduce | flops 192 | bytes 1536 | tf_op jit(solution)/shard_map/all_gather | solution.py:80
  80.8 2.2 constant_dynamic-update-slice_fusion.8
  82.9 0.8 slice_bitcast_fusion
  83.7 0.0 copy-start.2
  83.7 0.0 copy-start.3
  83.7 0.0 copy-start.1
  83.7 5.0 %gather_fusion = s32[768]{0:T(1024)S(1)} fusion(s32[192]{0:T(256)S(1)} %all-reduce, s32[1024]{0:T(1024)S(1)} %pad_clamp_fusion), kind=kCustom, calls=%fused_computation | custom fusion | bytes 9216 | tf_op jit(solution)/shard_map/gather | solution.py:83
  88.7 0.0 copy-start
  88.7 0.1 reshape.14
  88.8 0.1 copy.16
  88.9 0.0 copy-done.2
  88.9 0.1 copy.20
  89.0 0.1 copy.17
  89.1 0.1 reshape.11.i0_ref
  89.1 0.1 copy.19
  89.2 0.1 reshape.12.i1_ref
  89.3 0.0 copy-done.3
  89.3 0.1 eq.43
  89.4 0.1 eq.44
  89.5 0.1 squeeze.9
  89.6 0.0 collective-permute-done
  89.6 0.0 copy-done.1
  89.6 2.5 %collective-permute-start.5 = (bf16[24,128,128]{2,1,0:T(8,128)(2,1)S(1)}, bf16[24,128,128]{2,1,0:T(8,128)(2,1)S(1)}, u32[]{:S(2)}, u32[]{:S(2)}) collective-permute-start(bf16[24,128,128]{2,1,0:T(8,128)(2,1)S(1)} %bitcast.47), channel_id=1, source_target_pairs={{0,192},{32,224},{64,0},{96,32},{128,64},{160,96},{192,128},{224,1... | collective-permute-start | bytes 2359304 | tf_op jit(solution)/shard_map/ppermute | solution.py:76
  92.1 0.0 collective-permute-done.1
  92.1 2.2 collective-permute-start.6
  94.3 2.1 constant_dynamic-update-slice_fusion.7
  96.4 2.1 constant_dynamic-update-slice_fusion.6
  98.5 0.0 collective-permute-done.2
  98.5 2.1 constant_dynamic-update-slice_fusion.5
  100.6 0.0 collective-permute-done.3
  100.6 1.0 constant_dynamic-update-slice_fusion.4
  101.6 0.0 collective-permute-done.4
  101.6 1.0 constant_dynamic-update-slice_fusion.3
  102.6 6.1 %collective-permute-done.5 = bf16[24,128,128]{2,1,0:T(8,128)(2,1)S(1)} collective-permute-done((bf16[24,128,128]{2,1,0:T(8,128)(2,1)S(1)}, bf16[24,128,128]{2,1,0:T(8,128)(2,1)S(1)}, u32[]{:S(2)}, u32[]{:S(2)}) %collective-permute-start.5) | collective-permute-done | bytes 786464 | tf_op jit(solution)/shard_map/ppermute | solution.py:76
  108.7 1.0 constant_dynamic-update-slice_fusion.2
  109.7 9.1 %collective-permute-done.6 = bf16[24,128,128]{2,1,0:T(8,128)(2,1)S(1)} collective-permute-done((bf16[24,128,128]{2,1,0:T(8,128)(2,1)S(1)}, bf16[24,128,128]{2,1,0:T(8,128)(2,1)S(1)}, u32[]{:S(2)}, u32[]{:S(2)}) %collective-permute-start.6) | collective-permute-done | bytes 786464 | tf_op jit(solution)/shard_map/ppermute | solution.py:76
  118.8 1.0 constant_dynamic-update-slice_fusion.1
  119.8 0.6 constant_dynamic-update-slice_fusion.lookup_ref
  120.4 76.2 %all-gather.5.cloned.1.call-done = bf16[768,1,128,128]{3,2,1,0:T(8,128)(2,1)} async-done(((bf16[24,1,128,128]{3,2,1,0:T(8,128)(2,1)}), bf16[768,1,128,128]{3,2,1,0:T(8,128)(2,1)}) %all-gather.5.cloned.1.call-update) | async-done | bytes 25165840 | tf_op jit(solution)/shard_map/all_gather | solution.py:90
  196.6 0.0 copy-done
  196.6 39.8 %shard_map.55 = bf16[24,2,128,128]{3,2,1,0:T(8,128)(2,1)} custom-call(s32[768]{0:T(1024)S(1)} %reshape.11.i0_ref, s32[768]{0:T(1024)S(1)} %reshape.12.i1_ref, s32[48]{0:T(128)S(1)} %compare_convert_fusion.own_ref, bf16[32,24,128,128]{3,2,1,0:T(8,128)(2,1)} %bitcast.41, bf16[24,128,128]{2,1,0:T(8,128)(2,1)S(1)} %bitcast.40, ...), custom_call_target="tpu_custom_call" | custom-call | tf_op jit(solution)/shard_map/pallas_call | solution.py:42
  (6 shorter events, 0.1 us)
Async XLA Ops:
  6.5 190.1 %all-gather.5.cloned.1.call-start = ((), (), s32[]{:S(2)}) async-start(), calls=%async_computation | async-start | bytes 25952256 | tf_op jit(solution)/shard_map/all_gather | solution.py:90
  7.3 82.3 %collective-permute-start = (bf16[24,128,128]{2,1,0:T(8,128)(2,1)}, bf16[24,128,128]{2,1,0:T(8,128)(2,1)}, u32[]{:S(2)}, u32[]{:S(2)}) collective-permute-start(bf16[24,128,128]{2,1,0:T(8,128)(2,1)} %bitcast.42), channel_id=1, source_target_pairs={{0,32},{32,64},{64,96},{96,128},{128,160},{160,192},{192,224},{224... | collective-permute-start | bytes 2359304 | tf_op jit(solution)/shard_map/ppermute | solution.py:76
  9.9 82.1 %collective-permute-start.1 = (bf16[24,128,128]{2,1,0:T(8,128)(2,1)}, bf16[24,128,128]{2,1,0:T(8,128)(2,1)}, u32[]{:S(2)}, u32[]{:S(2)}) collective-permute-start(bf16[24,128,128]{2,1,0:T(8,128)(2,1)} %bitcast.43), channel_id=1, source_target_pairs={{0,64},{32,96},{64,128},{96,160},{128,192},{160,224},{192,0},{224,... | collective-permute-start | bytes 2359304 | tf_op jit(solution)/shard_map/ppermute | solution.py:76
  11.2 87.3 %collective-permute-start.2 = (bf16[24,128,128]{2,1,0:T(8,128)(2,1)}, bf16[24,128,128]{2,1,0:T(8,128)(2,1)}, u32[]{:S(2)}, u32[]{:S(2)}) collective-permute-start(bf16[24,128,128]{2,1,0:T(8,128)(2,1)} %bitcast.44), channel_id=1, source_target_pairs={{0,96},{32,128},{64,160},{96,192},{128,224},{160,0},{192,32},{224,... | collective-permute-start | bytes 2359304 | tf_op jit(solution)/shard_map/ppermute | solution.py:76
  12.9 87.7 %collective-permute-start.3 = (bf16[24,128,128]{2,1,0:T(8,128)(2,1)}, bf16[24,128,128]{2,1,0:T(8,128)(2,1)S(1)}, u32[]{:S(2)}, u32[]{:S(2)}) collective-permute-start(bf16[24,128,128]{2,1,0:T(8,128)(2,1)} %bitcast.45), channel_id=1, source_target_pairs={{0,128},{32,160},{64,192},{96,224},{128,0},{160,32},{192,64},{224,... | collective-permute-start | bytes 2359304 | tf_op jit(solution)/shard_map/ppermute | solution.py:76
  14.2 87.4 %collective-permute-start.4 = (bf16[24,128,128]{2,1,0:T(8,128)(2,1)}, bf16[24,128,128]{2,1,0:T(8,128)(2,1)S(1)}, u32[]{:S(2)}, u32[]{:S(2)}) collective-permute-start(bf16[24,128,128]{2,1,0:T(8,128)(2,1)} %bitcast.46), channel_id=1, source_target_pairs={{0,160},{32,192},{64,224},{96,0},{128,32},{160,64},{192,96},{224,1... | collective-permute-start | bytes 2359304 | tf_op jit(solution)/shard_map/ppermute | solution.py:76
  83.7 5.2 %copy-start.2 = (s32[24,1,2]{0,2,1:T(2,128)S(1)}, s32[24,1,2]{0,2,1:T(2,128)}, u32[]{:S(2)}) copy-start(s32[24,1,2]{0,2,1:T(2,128)} %param.9) | copy-start | bytes 580
  83.7 5.6 %copy-start.3 = (s32[24,1]{0,1:T(1,128)S(1)}, s32[24,1]{0,1:T(1,128)}, u32[]{:S(2)}) copy-start(s32[24,1]{0,1:T(1,128)} %param.6) | copy-start | bytes 292
  83.7 5.9 %copy-start.1 = (bf16[24,1,128,128]{3,2,1,0:T(8,128)(2,1)S(1)}, bf16[24,1,128,128]{3,2,1,0:T(8,128)(2,1)}, u32[]{:S(2)}) copy-start(bf16[24,1,128,128]{3,2,1,0:T(8,128)(2,1)} %param.7) | copy-start | bytes 2359300
  88.7 107.9 %copy-start = (bf16[24,1,128,128]{3,2,1,0:T(8,128)(2,1)S(1)}, bf16[24,1,128,128]{3,2,1,0:T(8,128)(2,1)}, u32[]{:S(2)}) copy-start(bf16[24,1,128,128]{3,2,1,0:T(8,128)(2,1)} %param.5) | copy-start | bytes 2359300
  89.6 19.1 %collective-permute-start.5 = (bf16[24,128,128]{2,1,0:T(8,128)(2,1)S(1)}, bf16[24,128,128]{2,1,0:T(8,128)(2,1)S(1)}, u32[]{:S(2)}, u32[]{:S(2)}) collective-permute-start(bf16[24,128,128]{2,1,0:T(8,128)(2,1)S(1)} %bitcast.47), channel_id=1, source_target_pairs={{0,192},{32,224},{64,0},{96,32},{128,64},{160,96},{192,128},{224,1... | collective-permute-start | bytes 2359304 | tf_op jit(solution)/shard_map/ppermute | solution.py:76
  92.1 26.7 %collective-permute-start.6 = (bf16[24,128,128]{2,1,0:T(8,128)(2,1)S(1)}, bf16[24,128,128]{2,1,0:T(8,128)(2,1)S(1)}, u32[]{:S(2)}, u32[]{:S(2)}) collective-permute-start(bf16[24,128,128]{2,1,0:T(8,128)(2,1)S(1)} %bitcast.48), channel_id=1, source_target_pairs={{0,224},{32,0},{64,32},{96,64},{128,96},{160,128},{192,160},{224,1... | collective-permute-start | bytes 2359304 | tf_op jit(solution)/shard_map/ppermute | solution.py:76
Sparse Core Ops, SparseCore 0:
  9.9 186.6 all-gather.4
